TPU v7x, 512 devices: a whole 4x8x8 slice. The times are simulated.
512 devices in a mesh: pipe: 32 (over y, z_lo), seq: 16 (over z_hi, x, core).
Axes of the slice: x: 4, y: 8, z: 8 (z_hi: 2, z_lo: 4; z = z_hi * 4 + z_lo), core: 2. Of those that a mesh axis runs over, the one named last changes fastest.
Arguments:
- x_first: bfloat16 [4096, 2560], P(('pipe', 'seq')), may hold values from -6 to 6
- x_second: bfloat16 [4096, 2560], P(('pipe', 'seq')), may hold values from -6 to 6
- stale_kv: bfloat16 [2, 4096, 2048], P(None, 'pipe', 'seq'), may hold values from -6 to 6
- w_qkv: bfloat16 [3, 2560, 2048], P(None, None, 'seq'), may hold values from -0.125 to 0.125
- w_out: bfloat16 [2048, 2560], P('seq'), may hold values from -0.125 to 0.125
- q_gain: float32 [2048], P('seq'), may hold values from 0.4 to 5
- k_gain: float32 [2048], P('seq'), may hold values from 0.4 to 5
- layout: int32 [32, 16], replicated, may hold values from 0 to 31, as said below
- counts: int32 [32], replicated, may hold values from 1 to 16, as said below
- slot_block: int32 [32], replicated, may hold values from 0 to 31, each once
Outputs:
- out_first: bfloat16 [4096, 2560], P(('pipe', 'seq'))
- out_second: bfloat16 [4096, 2560], P(('pipe', 'seq'))
Inputs may be any that keep to these rules, and one draw needn't show every extreme that they name: `layout`: entries of a row are distinct sequence blocks and the first entry of row b is b itself. `counts`: some block reads 16 entries. `slot_block`: each block once.
All inputs are finite; a program needn't handle non-finite values.
Results may differ from a plain program's by a relative error of at most 0.019.
Values may be sent and summed in bfloat16 or wider, within the bound.
No kernel may reach another device: no remote copies, remote signals or barrier semaphores. Data moves between devices by JAX's collectives and lax.ppermute only.
A program may use at most 64 MiB of HBM per device.

v0:
```python
import math

import jax
import jax.numpy as jnp
from jax import lax
from jax.sharding import PartitionSpec as P

HS = 64
BLOCK = 128
BPM = 1


HIGH = lax.Precision.HIGHEST
NEG = -1e30


def slot_mask(layout, counts, slot_block):
    total = layout.shape[0]
    width = layout.shape[1]
    blocks = jnp.arange(total, dtype=jnp.int32)
    valid = jnp.arange(width, dtype=jnp.int32)[None, :] < counts[:, None]
    member = jnp.sum(
        ((layout[:, :, None] == blocks[None, None, :]) & valid[:, :, None]).astype(jnp.float32),
        axis=1,
    )
    placed = (slot_block[:, None] == blocks[None, :]).astype(jnp.float32)
    linked = jnp.dot(jnp.dot(placed, member, precision=HIGH), placed.T, precision=HIGH)
    return linked > 0.5


def normalize(raw, gain, size):
    count = raw.shape[0]
    grid = raw.reshape(count, -1, size)
    factor = lax.rsqrt(jnp.mean(grid * grid, axis=2, keepdims=True) + 1e-06)
    return (grid * factor).reshape(count, -1) * gain[None, :]


def partial_attend(query, keys, values, allowed, scale):
    heads = query.shape[1]
    qrows = query.shape[0]
    krows = keys.shape[0]
    scores = jnp.einsum("qhd,khd->hqk", query, keys, preferred_element_type=jnp.float32) * scale
    grid = scores.reshape(heads, qrows // BLOCK, BLOCK, krows // BLOCK, BLOCK)
    keep = allowed[None, :, None, :, None]
    grid = jnp.where(keep, grid, NEG)
    top = jnp.max(grid, axis=(3, 4))
    weights = jnp.where(keep, jnp.exp(grid - top[:, :, :, None, None]), 0.0)
    total = jnp.sum(weights, axis=(3, 4))
    weights = weights.reshape(heads, qrows, krows)
    summed = jnp.einsum("hqk,khd->qhd", weights, values.astype(jnp.float32), precision=HIGH)
    return (top.reshape(heads, qrows), total.reshape(heads, qrows), summed)


def merge_parts(first, second):
    top_a, total_a, summed_a = first
    top_b, total_b, summed_b = second
    best = jnp.maximum(top_a, top_b)
    keep_a = jnp.exp(top_a - best)
    keep_b = jnp.exp(top_b - best)
    merged = summed_a * keep_a.T[:, :, None] + summed_b * keep_b.T[:, :, None]
    return (best, total_a * keep_a + total_b * keep_b, merged)


def on_device(
    x_first, x_second, stale_kv, w_qkv, w_out, q_gain, k_gain, layout, counts, slot_block
):
    me = lax.axis_index("pipe")
    tokens = BPM * BLOCK
    heads = w_qkv.shape[2] // HS
    width = heads * HS
    scale = 1.0 / math.sqrt(HS)
    linked = slot_mask(layout, counts, slot_block)
    total_blocks = linked.shape[0]
    block_ids = jnp.arange(total_blocks, dtype=jnp.int32)
    batch_of = block_ids // BPM
    mine = lax.dynamic_slice_in_dim(linked, me * BPM, BPM, 0)
    own = lax.dynamic_slice_in_dim(mine, me * BPM, BPM, 1)
    remote = mine & (batch_of != me)[None, :]

    def step(x_rows, prior_k, prior_v):
        raw = jnp.einsum(
            "rd,cdh->crh",
            lax.all_gather(x_rows, "seq", axis=0, tiled=True),
            w_qkv,
            preferred_element_type=jnp.float32,
        )
        query = normalize(raw[0], q_gain, HS).astype(jnp.bfloat16)
        keys = normalize(raw[1], k_gain, HS).astype(jnp.bfloat16)
        values = raw[2].astype(jnp.bfloat16)
        query_h = query.reshape(tokens, heads, HS)
        start_part = partial_attend(
            query_h, keys.reshape(tokens, heads, HS), values.reshape(tokens, heads, HS), own, scale
        )
        piece_k = lax.all_gather(prior_k, "pipe", axis=0, tiled=True)
        piece_v = lax.all_gather(prior_v, "pipe", axis=0, tiled=True)
        count = piece_k.shape[0]
        fresh = partial_attend(
            query_h,
            piece_k.reshape(count, heads, HS),
            piece_v.reshape(count, heads, HS),
            remote,
            scale,
        )
        best, denom_h, numer = merge_parts(start_part, fresh)
        denom = denom_h.T
        attn = (numer / denom[:, :, None]).reshape(tokens, width).astype(jnp.bfloat16)
        out = lax.psum_scatter(
            jnp.dot(attn, w_out, preferred_element_type=jnp.float32).astype(jnp.bfloat16),
            "seq",
            scatter_dimension=0,
            tiled=True,
        )
        return (out, keys, values)

    out_first, keys_first, values_first = step(x_first, stale_kv[0], stale_kv[1])
    out_second, unused_k, unused_v = step(x_second, keys_first, values_first)
    return (out_first, out_second)


def solution(mesh):
    placed = (
        P(("pipe", "seq"), None),
        P(("pipe", "seq"), None),
        P(None, "pipe", "seq"),
        P(None, None, "seq"),
        P("seq", None),
        P("seq"),
        P("seq"),
        P(),
        P(),
        P(),
    )
    return jax.shard_map(
        on_device,
        mesh=mesh,
        in_specs=placed,
        out_specs=(P(("pipe", "seq"), None), P(("pipe", "seq"), None)),
        check_vma=False,
    )
```

profile of v0, /device:TPU:1, one launch (start us, length us, event | category | flops | bytes accessed | tf_op | source)
XLA Modules:
  0.0 785.5 jit_solution(18196252297809986685)
XLA Ops:
  7.2 0.0 copy-start
  7.2 0.0 copy-start.7
  7.2 0.0 copy-start.5
  7.2 0.0 copy-start.6
  7.2 0.0 copy-start.8
  7.2 0.0 copy-start.9
  7.2 0.0 copy-start.10
  7.2 0.0 all-gather.8.cloned.1.call-start
  7.3 38.4 %all_gather.18 = bf16[128,2560]{1,0:T(8,128)(2,1)S(1)} all-gather(bf16[8,2560]{1,0:T(8,128)(2,1)} %param.10), channel_id=1, replica_groups=mesh['pipe'=32,'seq'=16] {'seq'}, dimensions={0}, use_global_device_ids=true | all-gather | bytes 696320 | tf_op jit(solution)/shard_map/all_gather | solution.py:83
  45.7 0.0 copy-done
  45.7 0.7 convolution_bitcast_fusion.1
  46.5 1.3 fusion.32
  47.8 0.0 all-gather.8.cloned.1.call-update
  47.9 0.0 all-gather.10.cloned.1.call-start
  47.9 1.4 fusion.62
  49.3 0.0 all-gather.10.cloned.1.call-update
  49.3 0.0 all-gather.14.cloned.1.call-start
  49.4 0.6 slice.43
  50.0 0.1 all-gather.14.cloned.1.call-update
  50.1 0.0 all-gather.12.cloned.1.call-start
  50.1 0.5 all-gather.12.cloned.1.call-update
  50.7 0.0 reduce-scatter.5.cloned.1.call-start
  50.7 0.0 copy-done.7
  50.7 0.1 mul.181
  50.8 0.0 copy-done.5
  50.8 27.6 %all_gather.21 = bf16[128,2560]{1,0:T(8,128)(2,1)S(1)} all-gather(bf16[8,2560]{1,0:T(8,128)(2,1)S(1)} %copy-done.5), channel_id=1, replica_groups=mesh['pipe'=32,'seq'=16] {'seq'}, dimensions={0}, use_global_device_ids=true | all-gather | bytes 696320 | tf_op jit(solution)/shard_map/all_gather | solution.py:83
  78.4 0.7 convolution_bitcast_fusion
  79.2 0.0 copy-done.6
  79.2 0.1 copy.20
  79.2 0.0 copy-done.8
  79.3 0.1 iota_compare_fusion.1
  79.3 0.2 convert_reduce_fusion
  79.6 0.0 copy-done.9
  79.6 0.2 fusion.43
  79.8 0.2 convolution_compare_fusion
  80.0 0.7 dynamic_slice.6
  80.7 0.1 mul.175
  80.9 0.1 broadcast_bitcast_fusion
  80.9 1.0 fusion.65
  81.9 1.0 fusion.66
  82.9 0.7 fusion.29
  83.6 66.0 %all-gather.8.cloned.1.call-done = bf16[4096,128]{0,1:T(8,128)(2,1)} async-done(((bf16[128,128]{0,1:T(8,128)(2,1)}), bf16[4096,128]{0,1:T(8,128)(2,1)}) %all-gather.8.cloned.1.call-update) | async-done | bytes 1048592 | tf_op jit(solution)/shard_map/all_gather | solution.py:94
  149.6 4.0 fusion.64
  153.6 146.0 %all-gather.10.cloned.1.call-done = bf16[1,4096,128]{2,1,0:T(8,128)(2,1)} async-done(((bf16[1,128,128]{2,1,0:T(8,128)(2,1)}), bf16[1,4096,128]{2,1,0:T(8,128)(2,1)}) %all-gather.10.cloned.1.call-update) | async-done | bytes 1048592 | tf_op jit(solution)/shard_map/all_gather | solution.py:94
  299.6 1.5 copy.22
  301.1 0.9 fusion.63
  302.0 1.9 copy-done.1
  304.0 1.6 fusion.4
  305.6 0.0 copy-start.3
  305.7 123.1 %all-gather.14.cloned.1.call-done = bf16[1,4096,128]{1,2,0:T(8,128)(2,1)} async-done(((bf16[1,128,128]{1,2,0:T(8,128)(2,1)}), bf16[1,4096,128]{1,2,0:T(8,128)(2,1)}) %all-gather.14.cloned.1.call-update) | async-done | bytes 1048592 | tf_op jit(solution)/shard_map/all_gather | solution.py:95
  428.8 5.6 fusion.23
  434.4 0.9 fusion.24
  435.3 1.2 convolution_convert_fusion
  436.5 0.0 reduce-scatter.5.cloned.1.call-update
  436.5 0.2 reduce-scatter.3.cloned.1.call-start
  436.7 142.6 %all-gather.12.cloned.1.call-done = bf16[1,4096,128]{2,1,0:T(8,128)(2,1)} async-done(((bf16[1,128,128]{2,1,0:T(8,128)(2,1)}), bf16[1,4096,128]{2,1,0:T(8,128)(2,1)}) %all-gather.12.cloned.1.call-update) | async-done | bytes 1048592 | tf_op jit(solution)/shard_map/all_gather | solution.py:95
  579.3 2.3 copy.23
  581.6 5.5 fusion.22
  587.1 0.0 copy-done.4
  587.1 0.9 fusion.25
  588.0 1.2 convolution_convert_fusion.1
  589.2 0.0 reduce-scatter.3.cloned.1.call-update
  589.2 102.0 %reduce-scatter.5.cloned.1.call-done = bf16[8,2560]{1,0:T(8,128)(2,1)} async-done(((bf16[128,2560]{1,0:T(8,128)(2,1)}), bf16[8,2560]{1,0:T(8,128)(2,1)}) %reduce-scatter.5.cloned.1.call-update) | async-done | bytes 40976 | tf_op jit(solution)/shard_map/reduce_scatter | solution.py:107
  691.2 87.4 %reduce-scatter.3.cloned.1.call-done = bf16[8,2560]{1,0:T(8,128)(2,1)} async-done(((bf16[128,2560]{1,0:T(8,128)(2,1)}), bf16[8,2560]{1,0:T(8,128)(2,1)}) %reduce-scatter.3.cloned.1.call-update) | async-done | bytes 40976 | tf_op jit(solution)/shard_map/reduce_scatter | solution.py:107
  (20 shorter events, 0.2 us)
Async XLA Ops:
  7.2 38.6 %copy-start = (bf16[3,2560,128]{2,1,0:T(8,128)(2,1)S(1)}, bf16[3,2560,128]{2,1,0:T(8,128)(2,1)}, u32[]{:S(2)}) copy-start(bf16[3,2560,128]{2,1,0:T(8,128)(2,1)} %param.13) | copy-start | bytes 5898244
  7.2 43.5 %copy-start.7 = (f32[128]{0:T(128)S(1)}, f32[128]{0:T(128)}, u32[]{:S(2)}) copy-start(f32[128]{0:T(128)} %param.16) | copy-start | bytes 1540
  7.2 43.6 %copy-start.5 = (bf16[8,2560]{1,0:T(8,128)(2,1)S(1)}, bf16[8,2560]{1,0:T(8,128)(2,1)}, u32[]{:S(2)}) copy-start(bf16[8,2560]{1,0:T(8,128)(2,1)} %param.11) | copy-start | bytes 122884
  7.2 72.0 %copy-start.6 = (s32[32,16]{0,1:T(8,128)S(1)}, s32[32,16]{0,1:T(8,128)}, u32[]{:S(2)}) copy-start(s32[32,16]{0,1:T(8,128)} %param.17) | copy-start | bytes 6148
  7.2 72.0 %copy-start.8 = (s32[32]{0:T(128)S(1)}, s32[32]{0:T(128)}, u32[]{:S(2)}) copy-start(s32[32]{0:T(128)} %param.18) | copy-start | bytes 388
  7.2 72.3 %copy-start.9 = (s32[32]{0:T(128)S(1)}, s32[32]{0:T(128)}, u32[]{:S(2)}) copy-start(s32[32]{0:T(128)} %param.19) | copy-start | bytes 388
  7.2 73.5 %copy-start.10 = (f32[128]{0:T(128)S(1)}, f32[128]{0:T(128)}, u32[]{:S(2)}) copy-start(f32[128]{0:T(128)} %param.15) | copy-start | bytes 1540
  7.2 142.3 %all-gather.8.cloned.1.call-start = ((), (), s32[]{:S(2)}) async-start(), calls=%async_computation.3 | async-start | bytes 1081344 | tf_op jit(solution)/shard_map/all_gather | solution.py:94
  47.9 251.7 %all-gather.10.cloned.1.call-start = ((), (), s32[]{:S(2)}) async-start(), calls=%async_computation.5 | async-start | bytes 1081344 | tf_op jit(solution)/shard_map/all_gather | solution.py:94
  49.3 379.4 %all-gather.14.cloned.1.call-start = ((), (), s32[]{:S(2)}) async-start(), calls=%async_computation.7 | async-start | bytes 1081344 | tf_op jit(solution)/shard_map/all_gather | solution.py:95
  50.1 529.2 %all-gather.12.cloned.1.call-start = ((), (), s32[]{:S(2)}) async-start(), calls=%async_computation.6 | async-start | bytes 1081344 | tf_op jit(solution)/shard_map/all_gather | solution.py:95
  50.7 640.6 %reduce-scatter.5.cloned.1.call-start = ((), (), s32[]{:S(2)}) async-start(), calls=%async_computation.4 | async-start | bytes 696320 | tf_op jit(solution)/shard_map/reduce_scatter | solution.py:107
  301.1 2.9 copy-start.1
  302.0 3.6 copy-start.2
  305.6 129.6 %copy-start.3 = (bf16[128,2560]{1,0:T(8,128)(2,1)S(1)}, bf16[128,2560]{1,0:T(8,128)(2,1)}, u32[]{:S(2)}) copy-start(bf16[128,2560]{1,0:T(8,128)(2,1)} %param.14) | copy-start | bytes 1966084
  436.5 150.7 %copy-start.4 = (bf16[1,128,128]{1,2,0:T(8,128)(2,1)S(1)}, bf16[1,128,128]{1,2,0:T(8,128)(2,1)}, u32[]{:S(2)}) copy-start(bf16[1,128,128]{1,2,0:T(8,128)(2,1)} %slice.43) | copy-start | bytes 98308
  436.5 342.2 %reduce-scatter.3.cloned.1.call-start = ((), (), s32[]{:S(2)}) async-start(), calls=%async_computation.2 | async-start | bytes 696320 | tf_op jit(solution)/shard_map/reduce_scatter | solution.py:107
Sparse Core Ops, SparseCore 0:
  48.0 101.5 all-gather.7
  152.2 147.3 all-gather.9
  301.6 127.1 all-gather.13
  431.3 148.0 all-gather.11
  584.4 106.8 reduce-scatter.4
  696.3 82.3 reduce-scatter.2
where the time goes:
time: 787 us; the launch traced here: 786 us
  waiting for transfers between devices  668 us (85%)
  blocking collectives  66 us (8%)
  matrix products  24 us (3%)
  between operations  14.4 us (2%)
  local copies, waits for them, and re-layouts  8.75 us (1%)
    all_gather x2, waiting for transfers between devices, step(): piece_v = lax.all_gather(prior_v, 'pipe', axis=0, tiled=True)  266 us
    all_gather x2, waiting for transfers between devices, step(): piece_k = lax.all_gather(prior_k, 'pipe', axis=0, tiled=True)  212 us
    reduce_scatter x2, waiting for transfers between devices, step(): lax.psum_scatter(jnp.dot(attn, w_out, preferred_element_type=jnp.float32)...  189 us
    all_gather x2, blocking collectives, step(): lax.all_gather(x_rows, 'seq', axis=0, tiled=True)  66 us
  transfers between devices with their start and end apart: 6, of which 6 were waited for; matrix products, arithmetic and copies ran while one was open for 4% of the time, Pallas kernels for 0%

commit v1 on v0

--- a/solution.py
+++ b/solution.py
@@ -2,7 +2,9 @@
 
 import jax
 import jax.numpy as jnp
+import numpy as np
 from jax import lax
+from jax.sharding import Mesh
 from jax.sharding import PartitionSpec as P
 
 HS = 64
@@ -12,6 +14,11 @@
 
 HIGH = lax.Precision.HIGHEST
 NEG = -1e30
+
+PIPE_PARTS = (("y", 8), ("zl", 4))
+SEQ_PARTS = (("zh", 2), ("x", 4), ("c", 2))
+PIPE = tuple(n for n, _ in PIPE_PARTS)
+SEQ = tuple(n for n, _ in SEQ_PARTS)
 
 
 def slot_mask(layout, counts, slot_block):
@@ -61,10 +68,17 @@
     return (best, total_a * keep_a + total_b * keep_b, merged)
 
 
+def gather_pipe(piece):
+    for name in reversed(PIPE):
+        piece = lax.all_gather(piece, name, axis=0, tiled=True)
+    return piece
+
+
 def on_device(
     x_first, x_second, stale_kv, w_qkv, w_out, q_gain, k_gain, layout, counts, slot_block
 ):
-    me = lax.axis_index("pipe")
+    me = lax.axis_index(PIPE)
+    n_seq = math.prod(s for _, s in SEQ_PARTS)
     tokens = BPM * BLOCK
     heads = w_qkv.shape[2] // HS
     width = heads * HS
@@ -77,23 +91,27 @@
     own = lax.dynamic_slice_in_dim(mine, me * BPM, BPM, 1)
     remote = mine & (batch_of != me)[None, :]
 
-    def step(x_rows, prior_k, prior_v):
-        raw = jnp.einsum(
-            "rd,cdh->crh",
-            lax.all_gather(x_rows, "seq", axis=0, tiled=True),
-            w_qkv,
-            preferred_element_type=jnp.float32,
-        )
+    xs = lax.all_gather(jnp.stack([x_first, x_second]), SEQ, axis=1, tiled=True)
+
+    def project(x):
+        raw = jnp.einsum("rd,cdh->crh", x, w_qkv, preferred_element_type=jnp.float32)
         query = normalize(raw[0], q_gain, HS).astype(jnp.bfloat16)
         keys = normalize(raw[1], k_gain, HS).astype(jnp.bfloat16)
         values = raw[2].astype(jnp.bfloat16)
+        return (query, keys, values)
+
+    q1, k1, v1 = project(xs[0])
+    q2, k2, v2 = project(xs[1])
+
+    kv = jnp.stack([stale_kv[0], stale_kv[1], k1, v1])[None]
+    gathered = gather_pipe(kv)
+    count = gathered.shape[0] * tokens
+
+    def attend(query, keys, values, piece_k, piece_v):
         query_h = query.reshape(tokens, heads, HS)
         start_part = partial_attend(
             query_h, keys.reshape(tokens, heads, HS), values.reshape(tokens, heads, HS), own, scale
         )
-        piece_k = lax.all_gather(prior_k, "pipe", axis=0, tiled=True)
-        piece_v = lax.all_gather(prior_v, "pipe", axis=0, tiled=True)
-        count = piece_k.shape[0]
         fresh = partial_attend(
             query_h,
             piece_k.reshape(count, heads, HS),
@@ -104,36 +122,40 @@
         best, denom_h, numer = merge_parts(start_part, fresh)
         denom = denom_h.T
         attn = (numer / denom[:, :, None]).reshape(tokens, width).astype(jnp.bfloat16)
-        out = lax.psum_scatter(
-            jnp.dot(attn, w_out, preferred_element_type=jnp.float32).astype(jnp.bfloat16),
-            "seq",
-            scatter_dimension=0,
-            tiled=True,
-        )
-        return (out, keys, values)
+        return jnp.dot(attn, w_out, preferred_element_type=jnp.float32).astype(jnp.bfloat16)
 
-    out_first, keys_first, values_first = step(x_first, stale_kv[0], stale_kv[1])
-    out_second, unused_k, unused_v = step(x_second, keys_first, values_first)
-    return (out_first, out_second)
+    part1 = attend(q1, k1, v1, gathered[:, 0], gathered[:, 1])
+    part2 = attend(q2, k2, v2, gathered[:, 2], gathered[:, 3])
+    parts = jnp.stack([part1, part2])
+    sent = lax.all_to_all(
+        parts.reshape(2, n_seq, tokens // n_seq, -1), SEQ, 1, 1, tiled=False
+    )
+    out = jnp.sum(sent.astype(jnp.float32), axis=1).astype(jnp.bfloat16)
+    return (out[0], out[1])
 
 
 def solution(mesh):
+    names = PIPE_PARTS + SEQ_PARTS
+    fine = Mesh(
+        np.asarray(mesh.devices).reshape([s for _, s in names]), tuple(n for n, _ in names)
+    )
+    rows = P(PIPE + SEQ, None)
     placed = (
-        P(("pipe", "seq"), None),
-        P(("pipe", "seq"), None),
-        P(None, "pipe", "seq"),
-        P(None, None, "seq"),
-        P("seq", None),
-        P("seq"),
-        P("seq"),
+        rows,
+        rows,
+        P(None, PIPE, SEQ),
+        P(None, None, SEQ),
+        P(SEQ, None),
+        P(SEQ),
+        P(SEQ),
         P(),
         P(),
         P(),
     )
     return jax.shard_map(
         on_device,
-        mesh=mesh,
+        mesh=fine,
         in_specs=placed,
-        out_specs=(P(("pipe", "seq"), None), P(("pipe", "seq"), None)),
+        out_specs=(rows, rows),
         check_vma=False,
     )

time: 787 us -> 233 us (0.30)
  the two profiles are of different devices: /device:TPU:1 before, /device:TPU:64 now
where the time goes in v1:
time: 233 us; the launch traced here: 232 us
  waiting for transfers between devices  114 us (49%)
  blocking collectives  61.4 us (26%)
  local copies, waits for them, and re-layouts  20.8 us (9%)
  matrix products  16.3 us (7%)
  between operations  14.4 us (6%)
  other arithmetic  5.38 us (2%)
    all_gather x1, waiting for transfers between devices, on_device(): xs = lax.all_gather(jnp.stack([x_first, x_second]), SEQ, axis=1, tiled=True)  65.3 us
    all_gather x1, waiting for transfers between devices, gather_pipe(): piece = lax.all_gather(piece, name, axis=0, tiled=True)  48.8 us
    all_to_all x1, blocking collectives, on_device(): lax.all_to_all(parts.reshape(2, n_seq, tokens // n_seq, -1), SEQ, 1, 1, t...  46 us
    all_gather x1, blocking collectives, gather_pipe(): piece = lax.all_gather(piece, name, axis=0, tiled=True)  15.3 us
    slice x3, local copies, waits for them, and re-layouts, on_device(): part1 = attend(q1, k1, v1, gathered[:, 0], gathered[:, 1])  8.57 us
    dot_general x4, matrix products, partial_attend(): jnp.einsum('hqk,khd->qhd', weights, values.astype(jnp.float32), precision...  7.93 us
  transfers between devices with their start and end apart: 2, of which 2 were waited for; matrix products, arithmetic and copies ran while one was open for 4% of the time, Pallas kernels for 0%

profile of v1, /device:TPU:64, one launch (start us, length us, event | category | flops | bytes accessed | tf_op | source)
XLA Modules:
  0.0 232.4 jit_solution(3354113923606738813)
XLA Ops:
  7.2 0.0 copy-start
  7.2 0.0 copy-start.5
  7.2 0.0 copy-start.3
  7.2 0.0 all-gather.4.cloned.1.call-start
  7.2 1.5 pad_maximum_fusion.2
  8.7 0.0 all-gather.4.cloned.1.call-update
  8.8 0.0 copy-start.7
  8.8 0.0 copy-start.4
  8.8 0.0 copy-start.6
  8.8 0.0 copy-start.8
  8.8 0.0 all-gather.6.cloned.1.call-start
  8.9 2.7 %copy.33 = bf16[3,2560,128]{1,2,0:T(8,128)(2,1)S(1)} copy(bf16[3,2560,128]{2,1,0:T(8,128)(2,1)} %param.13) | data formatting | bytes 3932160 | tf_op args[3]
  11.5 65.3 %all-gather.4.cloned.1.call-done = bf16[2,128,2560]{2,1,0:T(8,128)(2,1)} async-done(((bf16[2,8,2560]{2,1,0:T(8,128)(2,1)}), bf16[2,128,2560]{2,1,0:T(8,128)(2,1)}) %all-gather.4.cloned.1.call-update) | async-done | bytes 1310736 | tf_op jit(solution)/shard_map/all_gather | solution.py:94
  76.8 1.7 fusion.29
  78.6 0.1 copy.37
  78.8 0.0 copy-done.5
  78.8 0.1 fusion.64
  78.9 0.1 copy.36
  79.0 0.0 copy-done.3
  79.0 15.3 %all-gather = bf16[16,128,128]{2,1,0:T(8,128)(2,1)} all-gather(bf16[4,128,128]{2,1,0:T(8,128)(2,1)S(1)} %pad_maximum_fusion.1), channel_id=2, replica_groups=mesh['y'=8,'zl'=4,'zh'=2,'x'=4,'c'=2] {'zl'}, dimensions={0}, use_global_device_ids=true | all-gather | bytes 655360 | tf_op jit(solution)/shard_map/all_gather | solution.py:73
  94.4 0.0 all-gather.6.cloned.1.call-update
  94.4 0.1 mul.187
  94.5 0.0 copy-done.7
  94.5 0.1 mul.181
  94.6 0.0 copy-done.4
  94.6 0.1 copy.34
  94.7 0.0 copy-done.6
  94.7 0.1 iota_compare_fusion.1
  94.7 0.2 convert_reduce_fusion
  95.0 0.0 copy-done.8
  95.0 0.2 fusion.45
  95.2 0.2 convolution_compare_fusion
  95.4 0.6 dynamic_slice.6
  96.0 0.1 broadcast_bitcast_fusion
  96.1 1.7 fusion.28
  98.0 0.9 fusion.68
  98.9 0.7 fusion.31
  99.6 0.9 fusion.67
  100.6 0.7 fusion.32
  101.3 48.8 %all-gather.6.cloned.1.call-done = bf16[32,4,128,128]{3,2,1,0:T(8,128)(2,1)} async-done(((bf16[4,4,128,128]{3,2,1,0:T(8,128)(2,1)}), bf16[32,4,128,128]{3,2,1,0:T(8,128)(2,1)}) %all-gather.6.cloned.1.call-update) | async-done | bytes 4194320 | tf_op jit(solution)/shard_map/all_gather | solution.py:73
  150.1 4.0 %fusion.62 = (bf16[32,1,128,128]{3,2,1,0:T(8,128)(2,1)}, bf16[32,1,128,128]{3,2,1,0:T(8,128)(2,1)S(1)}, bf16[32,1,128,128]{3,2,1,0:T(8,128)(2,1)}, bf16[32,1,128,128]{3,2,1,0:T(8,128)(2,1)}) fusion(bf16[32,4,128,128]{3,2,1,0:T(8,128)(2,1)} %all-gather.6.cloned.1.call-done), kind=kLoop, calls=%fused_computation.107 | loop fusion | bytes 8388608 | tf_op jit(solution)/shard_map/slice | solution.py:127
  154.1 1.9 copy.39
  156.0 1.3 reshape_squeeze.27
  157.3 1.0 copy.43
  158.3 1.3 reshape_squeeze.31
  159.6 1.9 copy.42
  161.5 0.5 reshape_squeeze.30
  162.0 2.7 %copy.38 = bf16[32,1,128,128]{2,0,3,1:T(8,128)(2,1)} copy(bf16[32,1,128,128]{3,2,1,0:T(8,128)(2,1)} %get-tuple-element.13) | data formatting | bytes 2097152 | tf_op jit(solution)/shard_map/slice | solution.py:127
  164.7 1.7 reshape_squeeze.26
  166.4 0.9 fusion.66
  167.3 0.9 fusion.65
  168.3 1.6 fusion.4
  170.0 0.0 copy-done.2
  170.0 3.1 %fusion.24 = f32[128,2,64]{0,2,1:T(8,128)S(1)} fusion(bf16[4096,2,64]{0,2,1:T(8,128)(2,1)S(1)} %copy-done.2, f32[2,128,4096]{2,1,0:T(8,128)S(1)} %get-tuple-element.23, f32[2,128]{1,0:T(2,128)S(1)} %get-tuple-element.22, pred[4096]{0:T(1024)(128)(4,1)S(1)} %broadcast_bitcast_fusion, f32[128,2]{0,1:T(2,128)S(1)} %get-tuple-element.29), kind=kOutput, calls=%fused_computation.35 | convolution fusion | flops 807419904 | bytes 5314560 | tf_op jit(solution)/shard_map/hqk,khd->qhd/dot_general | solution.py:57
  173.1 0.0 copy-done.1
  173.1 3.1 %fusion.25 = f32[128,2,64]{0,2,1:T(8,128)S(1)} fusion(bf16[4096,2,64]{0,2,1:T(8,128)(2,1)S(1)} %copy-done.1, f32[2,128,4096]{2,1,0:T(8,128)S(1)} %get-tuple-element.21, f32[2,128]{1,0:T(2,128)S(1)} %get-tuple-element.20, pred[4096]{0:T(1024)(128)(4,1)S(1)} %broadcast_bitcast_fusion, f32[128,2]{0,1:T(2,128)S(1)} %get-tuple-element.9), kind=kOutput, calls=%fused_computation.36 | convolution fusion | flops 807419904 | bytes 5314560 | tf_op jit(solution)/shard_map/hqk,khd->qhd/dot_general | solution.py:57
  176.2 0.9 fusion.26
  177.1 0.4 fusion.3
  177.4 0.9 fusion.27
  178.3 0.3 fusion.2
  178.6 0.1 pad_maximum_fusion
  178.8 46.0 %all_to_all.5 = bf16[2,16,8,2560]{3,2,0,1:T(8,128)(2,1)S(1)} all-to-all(bf16[2,16,8,2560]{3,2,0,1:T(8,128)(2,1)S(1)} %pad_maximum_fusion), channel_id=1, replica_groups=mesh['y'=8,'zl'=4,'zh'=2,'x'=4,'c'=2] {'zh','x','c'}, dimensions={1} | all-to-all | bytes 2621440 | tf_op jit(solution)/shard_map/all_to_all | solution.py:130
  224.8 0.2 reduce_sum.114
  225.0 0.6 slice_bitcast_fusion.4
  (18 shorter events, 0.2 us)
Async XLA Ops:
  7.2 169.9 %copy-start = (bf16[128,2560]{1,0:T(8,128)(2,1)S(1)}, bf16[128,2560]{1,0:T(8,128)(2,1)}, u32[]{:S(2)}) copy-start(bf16[128,2560]{1,0:T(8,128)(2,1)} %param.14) | copy-start | bytes 1966084
  7.2 71.6 %copy-start.5 = (f32[128]{0:T(128)S(1)}, f32[128]{0:T(128)}, u32[]{:S(2)}) copy-start(f32[128]{0:T(128)} %param.16) | copy-start | bytes 1540
  7.2 71.8 %copy-start.3 = (bf16[2,128,128]{2,1,0:T(8,128)(2,1)S(1)}, bf16[2,128,128]{2,1,0:T(8,128)(2,1)}, u32[]{:S(2)}) copy-start(bf16[2,128,128]{2,1,0:T(8,128)(2,1)} %param.12) | copy-start | bytes 196612
  7.2 69.6 %all-gather.4.cloned.1.call-start = ((), (), s32[]{:S(2)}) async-start(), calls=%async_computation.1 | async-start | bytes 1392640 | tf_op jit(solution)/shard_map/all_gather | solution.py:94
  8.8 85.7 %copy-start.7 = (f32[128]{0:T(128)S(1)}, f32[128]{0:T(128)}, u32[]{:S(2)}) copy-start(f32[128]{0:T(128)} %param.15) | copy-start | bytes 1540
  8.8 85.8 %copy-start.4 = (s32[32,16]{0,1:T(8,128)S(1)}, s32[32,16]{0,1:T(8,128)}, u32[]{:S(2)}) copy-start(s32[32,16]{0,1:T(8,128)} %param.17) | copy-start | bytes 6148
  8.8 85.9 %copy-start.6 = (s32[32]{0:T(128)S(1)}, s32[32]{0:T(128)}, u32[]{:S(2)}) copy-start(s32[32]{0:T(128)} %param.18) | copy-start | bytes 388
  8.8 86.2 %copy-start.8 = (s32[32]{0:T(128)S(1)}, s32[32]{0:T(128)}, u32[]{:S(2)}) copy-start(s32[32]{0:T(128)} %param.19) | copy-start | bytes 388
  8.8 141.3 %all-gather.6.cloned.1.call-start = ((), (), s32[]{:S(2)}) async-start(), calls=%async_computation.2 | async-start | bytes 4718592 | tf_op jit(solution)/shard_map/all_gather | solution.py:73
  168.3 1.7 copy-start.2
  169.9 3.1 %copy-start.1 = (bf16[4096,2,64]{0,2,1:T(8,128)(2,1)S(1)}, bf16[4096,2,64]{0,2,1:T(8,128)(2,1)}, u32[]{:S(2)}) copy-start(bf16[4096,2,64]{0,2,1:T(8,128)(2,1)} %reshape_squeeze.31) | copy-start | bytes 3145732
Sparse Core Ops, SparseCore 0:
  11.4 65.4 all-gather.3
  94.5 55.5 all-gather.5

commit v2 on v1

--- a/solution.py
+++ b/solution.py
@@ -91,7 +91,11 @@
     own = lax.dynamic_slice_in_dim(mine, me * BPM, BPM, 1)
     remote = mine & (batch_of != me)[None, :]
 
-    xs = lax.all_gather(jnp.stack([x_first, x_second]), SEQ, axis=1, tiled=True)
+    stale = gather_pipe(stale_kv[None])
+
+    pair = jnp.stack([x_first, x_second])
+    spread = jnp.broadcast_to(pair[:, None], (2, n_seq) + x_first.shape)
+    xs = lax.all_to_all(spread, SEQ, 1, 1, tiled=False).reshape(2, tokens, -1)
 
     def project(x):
         raw = jnp.einsum("rd,cdh->crh", x, w_qkv, preferred_element_type=jnp.float32)
@@ -103,9 +107,8 @@
     q1, k1, v1 = project(xs[0])
     q2, k2, v2 = project(xs[1])
 
-    kv = jnp.stack([stale_kv[0], stale_kv[1], k1, v1])[None]
-    gathered = gather_pipe(kv)
-    count = gathered.shape[0] * tokens
+    fresh_kv = gather_pipe(jnp.stack([k1, v1])[None])
+    count = fresh_kv.shape[0] * tokens
 
     def attend(query, keys, values, piece_k, piece_v):
         query_h = query.reshape(tokens, heads, HS)
@@ -122,16 +125,14 @@
         best, denom_h, numer = merge_parts(start_part, fresh)
         denom = denom_h.T
         attn = (numer / denom[:, :, None]).reshape(tokens, width).astype(jnp.bfloat16)
-        return jnp.dot(attn, w_out, preferred_element_type=jnp.float32).astype(jnp.bfloat16)
+        part = jnp.dot(attn, w_out, preferred_element_type=jnp.float32).astype(jnp.bfloat16)
+        sent = lax.all_to_all(part.reshape(n_seq, tokens // n_seq, -1), SEQ, 0, 0, tiled=False)
+        return jnp.sum(sent.astype(jnp.float32), axis=0).astype(jnp.bfloat16)
 
-    part1 = attend(q1, k1, v1, gathered[:, 0], gathered[:, 1])
-    part2 = attend(q2, k2, v2, gathered[:, 2], gathered[:, 3])
-    parts = jnp.stack([part1, part2])
-    sent = lax.all_to_all(
-        parts.reshape(2, n_seq, tokens // n_seq, -1), SEQ, 1, 1, tiled=False
-    )
-    out = jnp.sum(sent.astype(jnp.float32), axis=1).astype(jnp.bfloat16)
-    return (out[0], out[1])
+    out_first = attend(q1, k1, v1, stale[:, 0], stale[:, 1])
+    out_first, fresh_kv = lax.optimization_barrier((out_first, fresh_kv))
+    out_second = attend(q2, k2, v2, fresh_kv[:, 0], fresh_kv[:, 1])
+    return (out_first, out_second)
 
 
 def solution(mesh):

time: 233 us -> 208 us (0.89)
  the two profiles are of different devices: /device:TPU:64 before, /device:TPU:1 now
where the time goes in v2:
time: 208 us; the launch traced here: 204 us
  blocking collectives  83 us (40%)
  waiting for transfers between devices  33.7 us (16%)
  starting transfers between devices  28.2 us (14%)
  matrix products  19 us (9%)
  local copies, waits for them, and re-layouts  18.2 us (9%)
  between operations  14.4 us (7%)
  other arithmetic  7.7 us (4%)
    all_gather x2, blocking collectives, gather_pipe(): piece = lax.all_gather(piece, name, axis=0, tiled=True)  52.6 us
    all_to_all x1, blocking collectives, attend(): lax.all_to_all(part.reshape(n_seq, tokens // n_seq, -1), SEQ, 0, 0, tiled...  30.3 us
    all_gather x2, waiting for transfers between devices, gather_pipe(): piece = lax.all_gather(piece, name, axis=0, tiled=True)  17.2 us
    all_to_all x1, waiting for transfers between devices, attend(): lax.all_to_all(part.reshape(n_seq, tokens // n_seq, -1), SEQ, 0, 0, tiled...  16.5 us
    all_to_all x1, starting transfers between devices, on_device(): xs = lax.all_to_all(spread, SEQ, 1, 1, tiled=False).reshape(2, tokens, -1)  14.2 us
    all_to_all x1, starting transfers between devices, attend(): lax.all_to_all(part.reshape(n_seq, tokens // n_seq, -1), SEQ, 0, 0, tiled...  13.9 us
    dot_general x4, matrix products, partial_attend(): jnp.einsum('hqk,khd->qhd', weights, values.astype(jnp.float32), precision...  7.91 us
    dot_general x4, matrix products, partial_attend(): jnp.einsum('qhd,khd->hqk', query, keys, preferred_element_type=jnp.float32)  5.62 us
  transfers between devices with their start and end apart: 4, of which 2 were waited for; matrix products, arithmetic and copies ran while one was open for 13% of the time, Pallas kernels for 0%

profile of v2, /device:TPU:1, one launch (start us, length us, event | category | flops | bytes accessed | tf_op | source)
XLA Modules:
  0.0 204.1 jit_solution(14378837768875720348)
XLA Ops:
  7.2 0.0 copy-start
  7.2 0.0 copy-start.4
  7.2 0.0 copy-start.5
  7.2 0.9 pad_maximum_fusion
  8.1 0.0 copy-start.8
  8.1 0.0 copy-start.6
  8.1 0.0 copy-start.7
  8.1 0.0 copy-start.9
  8.1 1.2 broadcast_in_dim.102
  9.3 14.2 %all-to-all-start = ((bf16[2,16,8,2560]{3,2,0,1:T(8,128)(2,1)}), bf16[2,16,8,2560]{3,2,0,1:T(8,128)(2,1)}, u32[]{:S(2)}, u32[]{:S(2)}) async-start(bf16[2,16,8,2560]{3,2,0,1:T(8,128)(2,1)} %broadcast_in_dim.102), calls=%async_computation | async-start | bytes 2621440 | tf_op jit(solution)/shard_map/all_to_all | solution.py:98
  23.6 0.0 all-gather.5.cloned.1.call-start
  23.6 0.0 copy-done.4
  23.6 40.8 %all-gather = bf16[8,128,128]{2,1,0:T(8,128)(2,1)} all-gather(bf16[2,128,128]{2,1,0:T(8,128)(2,1)S(1)} %copy-done.4), channel_id=2, replica_groups=mesh['y'=8,'zl'=4,'zh'=2,'x'=4,'c'=2] {'zl'}, dimensions={0}, use_global_device_ids=true | all-gather | bytes 327680 | tf_op jit(solution)/shard_map/all_gather | solution.py:73
  64.4 0.0 all-gather.5.cloned.1.call-update
  64.4 0.0 all-gather.7.cloned.1.call-start
  64.5 0.0 copy-done.5
  64.5 0.1 copy.31
  64.6 2.7 %copy.30 = bf16[3,2560,128]{1,2,0:T(8,128)(2,1)S(1)} copy(bf16[3,2560,128]{2,1,0:T(8,128)(2,1)} %param.13) | data formatting | bytes 3932160 | tf_op args[3]
  67.2 0.0 copy-done.8
  67.3 0.1 mul.181
  67.3 0.1 mul.187
  67.4 0.1 iota_compare_fusion.1
  67.5 0.2 convert_reduce_fusion
  67.7 0.2 fusion.45
  67.9 0.2 convolution_compare_fusion
  68.2 0.6 dynamic_slice.6
  68.8 0.1 broadcast_bitcast_fusion
  68.8 0.0 all-to-all-done
  68.8 1.7 fusion.29
  70.7 0.1 fusion.34
  70.8 0.1 copy.35
  70.9 11.8 %all-gather.1 = bf16[8,128,128]{2,1,0:T(8,128)(2,1)} all-gather(bf16[2,128,128]{2,1,0:T(8,128)(2,1)S(1)} %copy.35), channel_id=3, replica_groups=mesh['y'=8,'zl'=4,'zh'=2,'x'=4,'c'=2] {'zl'}, dimensions={0}, use_global_device_ids=true | all-gather | bytes 327680 | tf_op jit(solution)/shard_map/all_gather | solution.py:73
  82.8 1.7 fusion.28
  84.6 0.0 all-gather.7.cloned.1.call-update
  84.6 0.9 fusion.66
  85.6 1.0 fusion.68
  86.6 0.7 fusion.31
  87.3 17.2 %all-gather.5.cloned.1.call-done = bf16[32,2,128,128]{3,2,1,0:T(8,128)(2,1)} async-done(((bf16[4,2,128,128]{3,2,1,0:T(8,128)(2,1)}), bf16[32,2,128,128]{3,2,1,0:T(8,128)(2,1)}) %all-gather.5.cloned.1.call-update) | async-done | bytes 2097168 | tf_op jit(solution)/shard_map/all_gather | solution.py:73
  104.5 2.7 %fusion.63 = (bf16[32,1,128,128]{3,2,1,0:T(8,128)(2,1)S(1)}, bf16[32,1,128,128]{3,2,1,0:T(8,128)(2,1)}) fusion(bf16[32,2,128,128]{3,2,1,0:T(8,128)(2,1)} %all-gather.5.cloned.1.call-done), kind=kLoop, calls=%fused_computation.105 | loop fusion | bytes 4194304 | tf_op jit(solution)/shard_map/slice | solution.py:132
  107.2 1.0 copy.33
  108.2 0.5 reshape_squeeze.26
  108.7 1.9 copy.34
  110.6 1.3 reshape_squeeze.27
  111.9 0.9 fusion.65
  112.8 0.9 fusion.4
  113.8 3.1 %fusion.24 = f32[128,2,64]{0,2,1:T(8,128)S(1)} fusion(bf16[4096,2,64]{0,2,1:T(8,128)(2,1)S(1)} %copy-done.3, f32[2,128,4096]{2,1,0:T(8,128)S(1)} %get-tuple-element.21, f32[2,128]{1,0:T(2,128)S(1)} %get-tuple-element.20, pred[4096]{0:T(1024)(128)(4,1)S(1)} %broadcast_bitcast_fusion, f32[128,2]{0,1:T(2,128)S(1)} %get-tuple-element.11), kind=kOutput, calls=%fused_computation.34 | convolution fusion | flops 807419904 | bytes 5314560 | tf_op jit(solution)/shard_map/hqk,khd->qhd/dot_general | solution.py:57
  116.9 0.9 fusion.27
  117.7 1.2 fusion.2
  118.9 13.9 %all-to-all-start.1 = ((bf16[16,8,2560]{2,1,0:T(8,128)(2,1)}), bf16[16,8,2560]{2,1,0:T(8,128)(2,1)S(1)}, u32[]{:S(2)}, u32[]{:S(2)}) async-start(bf16[16,8,2560]{2,1,0:T(8,128)(2,1)} %fusion.2), calls=%async_computation.1 | async-start | bytes 1310720 | tf_op jit(solution)/shard_map/all_to_all | solution.py:129
  132.8 16.5 %all-to-all-done.1 = bf16[16,8,2560]{2,1,0:T(8,128)(2,1)S(1)} async-done(((bf16[16,8,2560]{2,1,0:T(8,128)(2,1)}), bf16[16,8,2560]{2,1,0:T(8,128)(2,1)S(1)}, u32[]{:S(2)}, u32[]{:S(2)}) %all-to-all-start.1) | async-done | bytes 655392 | tf_op jit(solution)/shard_map/all_to_all | solution.py:129
  149.3 0.7 reduce_sum.120
  150.0 2.7 %fusion.62 = (bf16[32,1,128,128]{3,2,1,0:T(8,128)(2,1)S(1)}, bf16[32,1,128,128]{3,2,1,0:T(8,128)(2,1)}) fusion(bf16[32,2,128,128]{3,2,1,0:T(8,128)(2,1)} %all-gather.7.cloned.1.call-done), kind=kLoop, calls=%fused_computation.104 | loop fusion | bytes 4194304 | tf_op jit(solution)/shard_map/slice | solution.py:134
  152.7 1.0 copy.38
  153.7 0.5 reshape_squeeze.30
  154.2 2.8 %fusion.67 = (f32[2,128]{1,0:T(2,128)S(1)}, f32[2,128,4096]{2,1,0:T(8,128)}) fusion(bf16[4096,2,64]{0,2,1:T(8,128)(2,1)S(1)} %reshape_squeeze.30, f32[128,2,64]{0,2,1:T(8,128)S(1)} %bitcast.145, f32[128,2]{0,1:T(2,128)S(1)} %add_rsqrt_fusion.1, f32[2,64]{1,0:T(2,128)S(1)} %mul.181, pred[4096]{0:T(1024)(128)(4,1)S(1)} %broadcast_bitcast_fusion), kind=kOutput, calls=%fused_computation.109 | convolution fusion | flops 137412352 | bytes 5315072 | tf_op jit(solution)/shard_map/qhd,khd->hqk/dot_general | solution.py:49
  157.0 1.0 copy.39
  158.0 0.5 reshape_squeeze.31
  158.5 3.2 %fusion.6 = f32[2,128]{1,0:T(2,128)S(1)} fusion(f32[2,128,4096]{2,1,0:T(8,128)} %get-tuple-element.25, f32[2,128]{1,0:T(2,128)S(1)} %get-tuple-element.24, pred[4096]{0:T(1024)(128)(4,1)S(1)} %broadcast_bitcast_fusion), kind=kLoop, calls=%fused_computation.12 | loop fusion | flops 3145472 | bytes 4200448 | tf_op jit(solution)/shard_map/reduce_sum | solution.py:55
  161.7 0.2 copy-done.1
  161.9 3.1 %fusion.25 = f32[128,2,64]{0,2,1:T(8,128)S(1)} fusion(bf16[4096,2,64]{0,2,1:T(8,128)(2,1)S(1)} %reshape_squeeze.31, f32[2,128,4096]{2,1,0:T(8,128)S(1)} %copy-done.1, f32[2,128]{1,0:T(2,128)S(1)} %get-tuple-element.24, pred[4096]{0:T(1024)(128)(4,1)S(1)} %broadcast_bitcast_fusion, f32[128,2]{0,1:T(2,128)S(1)} %get-tuple-element.8), kind=kOutput, calls=%fused_computation.35 | convolution fusion | flops 807419904 | bytes 5314560 | tf_op jit(solution)/shard_map/hqk,khd->qhd/dot_general | solution.py:57
  165.0 0.9 fusion.26
  165.9 0.4 fusion.3
  166.3 30.3 %all_to_all.15 = bf16[16,8,2560]{2,1,0:T(8,128)(2,1)S(1)} all-to-all(bf16[16,8,2560]{2,1,0:T(8,128)(2,1)S(1)} %fusion.3), channel_id=1, replica_groups=mesh['y'=8,'zl'=4,'zh'=2,'x'=4,'c'=2] {'zh','x','c'}, dimensions={0} | all-to-all | bytes 1310720 | tf_op jit(solution)/shard_map/all_to_all | solution.py:129
  196.6 0.7 reduce_sum.127
  (26 shorter events, 0.2 us)
Async XLA Ops:
  7.2 110.6 %copy-start = (bf16[128,2560]{1,0:T(8,128)(2,1)S(1)}, bf16[128,2560]{1,0:T(8,128)(2,1)}, u32[]{:S(2)}) copy-start(bf16[128,2560]{1,0:T(8,128)(2,1)} %param.14) | copy-start | bytes 1966084
  7.2 16.4 %copy-start.4 = (bf16[2,128,128]{2,1,0:T(8,128)(2,1)S(1)}, bf16[2,128,128]{2,1,0:T(8,128)(2,1)}, u32[]{:S(2)}) copy-start(bf16[2,128,128]{2,1,0:T(8,128)(2,1)} %param.12) | copy-start | bytes 196612
  7.2 57.3 %copy-start.5 = (s32[32,16]{0,1:T(8,128)S(1)}, s32[32,16]{0,1:T(8,128)}, u32[]{:S(2)}) copy-start(s32[32,16]{0,1:T(8,128)} %param.17) | copy-start | bytes 6148
  8.1 59.2 %copy-start.8 = (f32[128]{0:T(128)S(1)}, f32[128]{0:T(128)}, u32[]{:S(2)}) copy-start(f32[128]{0:T(128)} %param.15) | copy-start | bytes 1540
  8.1 59.3 %copy-start.6 = (f32[128]{0:T(128)S(1)}, f32[128]{0:T(128)}, u32[]{:S(2)}) copy-start(f32[128]{0:T(128)} %param.16) | copy-start | bytes 1540
  8.1 59.3 %copy-start.7 = (s32[32]{0:T(128)S(1)}, s32[32]{0:T(128)}, u32[]{:S(2)}) copy-start(s32[32]{0:T(128)} %param.18) | copy-start | bytes 388
  8.1 59.6 %copy-start.9 = (s32[32]{0:T(128)S(1)}, s32[32]{0:T(128)}, u32[]{:S(2)}) copy-start(s32[32]{0:T(128)} %param.19) | copy-start | bytes 388
  9.3 59.5 %all-to-all-start = ((bf16[2,16,8,2560]{3,2,0,1:T(8,128)(2,1)}), bf16[2,16,8,2560]{3,2,0,1:T(8,128)(2,1)}, u32[]{:S(2)}, u32[]{:S(2)}) async-start(bf16[2,16,8,2560]{3,2,0,1:T(8,128)(2,1)} %broadcast_in_dim.102), calls=%async_computation | async-start | bytes 2621440 | tf_op jit(solution)/shard_map/all_to_all | solution.py:98
  23.6 80.9 %all-gather.5.cloned.1.call-start = ((), (), s32[]{:S(2)}) async-start(), calls=%async_computation.3 | async-start | bytes 2359296 | tf_op jit(solution)/shard_map/all_gather | solution.py:73
  64.4 85.6 %all-gather.7.cloned.1.call-start = ((), (), s32[]{:S(2)}) async-start(), calls=%async_computation.4 | async-start | bytes 2359296 | tf_op jit(solution)/shard_map/all_gather | solution.py:73
  111.9 1.9 copy-start.3
  118.9 30.4 %all-to-all-start.1 = ((bf16[16,8,2560]{2,1,0:T(8,128)(2,1)}), bf16[16,8,2560]{2,1,0:T(8,128)(2,1)S(1)}, u32[]{:S(2)}, u32[]{:S(2)}) async-start(bf16[16,8,2560]{2,1,0:T(8,128)(2,1)} %fusion.2), calls=%async_computation.1 | async-start | bytes 1310720 | tf_op jit(solution)/shard_map/all_to_all | solution.py:129
  154.2 2.8 %copy-start.2 = (bf16[32,1,128,128]{3,2,1,0:T(8,128)(2,1)S(1)}, bf16[32,1,128,128]{3,2,1,0:T(8,128)(2,1)}, u32[]{:S(2)}) copy-start(bf16[32,1,128,128]{3,2,1,0:T(8,128)(2,1)} %get-tuple-element.13) | copy-start | bytes 3145732
  158.5 3.5 %copy-start.1 = (f32[2,128,4096]{2,1,0:T(8,128)S(1)}, f32[2,128,4096]{2,1,0:T(8,128)}, u32[]{:S(2)}) copy-start(f32[2,128,4096]{2,1,0:T(8,128)} %get-tuple-element.25) | copy-start | bytes 12582916
Sparse Core Ops, SparseCore 0:
  64.5 39.8 all-gather.4
  106.5 41.9 all-gather.6

commit v3 on v2

--- a/solution.py
+++ b/solution.py
@@ -68,8 +68,8 @@
     return (best, total_a * keep_a + total_b * keep_b, merged)
 
 
-def gather_pipe(piece):
-    for name in reversed(PIPE):
+def gather_pipe(piece, order):
+    for name in order:
         piece = lax.all_gather(piece, name, axis=0, tiled=True)
     return piece
 
@@ -91,7 +91,9 @@
     own = lax.dynamic_slice_in_dim(mine, me * BPM, BPM, 1)
     remote = mine & (batch_of != me)[None, :]
 
-    stale = gather_pipe(stale_kv[None])
+    stale = gather_pipe(stale_kv[None], PIPE)
+    sizes = [s for _, s in PIPE_PARTS]
+    remote_stale = remote.reshape(BPM, *sizes).transpose(0, 2, 1).reshape(BPM, -1)
 
     pair = jnp.stack([x_first, x_second])
     spread = jnp.broadcast_to(pair[:, None], (2, n_seq) + x_first.shape)
@@ -107,10 +109,10 @@
     q1, k1, v1 = project(xs[0])
     q2, k2, v2 = project(xs[1])
 
-    fresh_kv = gather_pipe(jnp.stack([k1, v1])[None])
+    fresh_kv = gather_pipe(jnp.stack([k1, v1])[None], tuple(reversed(PIPE)))
     count = fresh_kv.shape[0] * tokens
 
-    def attend(query, keys, values, piece_k, piece_v):
+    def attend(query, keys, values, piece_k, piece_v, remote):
         query_h = query.reshape(tokens, heads, HS)
         start_part = partial_attend(
             query_h, keys.reshape(tokens, heads, HS), values.reshape(tokens, heads, HS), own, scale
@@ -129,9 +131,9 @@
         sent = lax.all_to_all(part.reshape(n_seq, tokens // n_seq, -1), SEQ, 0, 0, tiled=False)
         return jnp.sum(sent.astype(jnp.float32), axis=0).astype(jnp.bfloat16)
 
-    out_first = attend(q1, k1, v1, stale[:, 0], stale[:, 1])
+    out_first = attend(q1, k1, v1, stale[:, 0], stale[:, 1], remote_stale)
     out_first, fresh_kv = lax.optimization_barrier((out_first, fresh_kv))
-    out_second = attend(q2, k2, v2, fresh_kv[:, 0], fresh_kv[:, 1])
+    out_second = attend(q2, k2, v2, fresh_kv[:, 0], fresh_kv[:, 1], remote)
     return (out_first, out_second)
 
 

time: 208 us -> 204 us (0.981)
  waiting for transfers between devices: 33.7 us -> 42.3 us
  starting transfers between devices: 28.2 us -> 21.4 us
  blocking collectives: 83 us -> 78.9 us
    all_to_all x1, starting transfers between devices: 13.9 us -> 6.97 us  [attend(): lax.all_to_all(part.reshape(n_seq, tokens // n_seq, -1), SEQ, 0, 0, tiled...]
    all_gather x2, waiting for transfers between devices: 17.2 us -> 23.2 us  [gather_pipe(): piece = lax.all_gather(piece, name, axis=0, tiled=True)]
    all_gather x2, blocking collectives: 52.6 us -> 47.2 us  [gather_pipe(): piece = lax.all_gather(piece, name, axis=0, tiled=True)]
    all_to_all x1, waiting for transfers between devices: 16.5 us -> 19.1 us  [attend(): lax.all_to_all(part.reshape(n_seq, tokens // n_seq, -1), SEQ, 0, 0, tiled...]
    reduce_sum x3, other arithmetic: 4.86 us -> 2.51 us  [partial_attend(): total = jnp.sum(weights, axis=(3, 4))]
    slice x6 -> x4, local copies, waits for them, and re-layouts: 10.3 us -> 8.49 us  [the longest x3 5.62 us: on_device(): out_second = attend(q2, k2, v2, fresh_kv[:, 0], fresh_kv[:, 1], remote)]
where the time goes in v3:
time: 204 us; the launch traced here: 200 us
  blocking collectives  78.9 us (39%)
  waiting for transfers between devices  42.3 us (21%)
  starting transfers between devices  21.4 us (10%)
  local copies, waits for them, and re-layouts  20 us (10%)
  matrix products  17 us (8%)
  between operations  14.3 us (7%)
  other arithmetic  6.01 us (3%)
    all_gather x2, blocking collectives, gather_pipe(): piece = lax.all_gather(piece, name, axis=0, tiled=True)  47.2 us
    all_to_all x1, blocking collectives, attend(): lax.all_to_all(part.reshape(n_seq, tokens // n_seq, -1), SEQ, 0, 0, tiled...  31.8 us
    all_gather x2, waiting for transfers between devices, gather_pipe(): piece = lax.all_gather(piece, name, axis=0, tiled=True)  23.2 us
    all_to_all x1, waiting for transfers between devices, attend(): lax.all_to_all(part.reshape(n_seq, tokens // n_seq, -1), SEQ, 0, 0, tiled...  19.1 us
    all_to_all x1, starting transfers between devices, on_device(): xs = lax.all_to_all(spread, SEQ, 1, 1, tiled=False).reshape(2, tokens, -1)  14.4 us
    dot_general x4, matrix products, partial_attend(): jnp.einsum('hqk,khd->qhd', weights, values.astype(jnp.float32), precision...  7.82 us
    all_to_all x1, starting transfers between devices, attend(): lax.all_to_all(part.reshape(n_seq, tokens // n_seq, -1), SEQ, 0, 0, tiled...  6.97 us
    slice x3, local copies, waits for them, and re-layouts, on_device(): out_second = attend(q2, k2, v2, fresh_kv[:, 0], fresh_kv[:, 1], remote)  5.62 us
  transfers between devices with their start and end apart: 4, of which 2 were waited for; matrix products, arithmetic and copies ran while one was open for 13% of the time, Pallas kernels for 0%

profile of v3, /device:TPU:1, one launch (start us, length us, event | category | flops | bytes accessed | tf_op | source)
XLA Modules:
  0.0 200.1 jit_solution(6478874123204979022)
XLA Ops:
  7.2 0.0 copy-start
  7.2 0.0 copy-start.3
  7.2 0.0 copy-start.6
  7.2 0.0 copy-start.4
  7.2 0.9 pad_maximum_fusion
  8.1 1.2 broadcast_in_dim.109
  9.3 14.4 %all-to-all-start = ((bf16[2,16,8,2560]{3,2,0,1:T(8,128)(2,1)}), bf16[2,16,8,2560]{3,2,0,1:T(8,128)(2,1)}, u32[]{:S(2)}, u32[]{:S(2)}) async-start(bf16[2,16,8,2560]{3,2,0,1:T(8,128)(2,1)} %broadcast_in_dim.109), calls=%async_computation | async-start | bytes 2621440 | tf_op jit(solution)/shard_map/all_to_all | solution.py:100
  23.7 0.0 all-gather.5.cloned.1.call-start
  23.7 0.0 copy-done.3
  23.7 23.1 %all-gather = bf16[16,128,128]{2,1,0:T(8,128)(2,1)S(1)} all-gather(bf16[2,128,128]{2,1,0:T(8,128)(2,1)S(1)} %copy-done.3), channel_id=2, replica_groups=mesh['y'=8,'zl'=4,'zh'=2,'x'=4,'c'=2] {'y'}, dimensions={0}, use_global_device_ids=true | all-gather | bytes 589824 | tf_op jit(solution)/shard_map/all_gather | solution.py:73
  46.8 1.1 copy.44
  47.9 0.0 all-gather.5.cloned.1.call-update
  48.0 0.0 all-gather.7.cloned.1.call-start
  48.0 0.0 copy-done.6
  48.0 0.1 iota_compare_fusion.1
  48.1 0.1 copy.41
  48.2 2.7 %copy.40 = bf16[3,2560,128]{1,2,0:T(8,128)(2,1)S(1)} copy(bf16[3,2560,128]{2,1,0:T(8,128)(2,1)} %param.13) | data formatting | bytes 3932160 | tf_op args[3]
  50.9 0.1 mul.181
  50.9 0.1 mul.187
  51.0 0.2 convert_reduce_fusion
  51.3 0.2 fusion.45
  51.4 0.2 convolution_compare_fusion
  51.7 0.6 dynamic_slice.6
  52.3 0.5 broadcast.213
  52.8 0.7 fusion.62
  53.5 0.1 reshape.234
  53.6 0.1 copy.43
  53.7 0.1 broadcast_in_dim.114
  53.7 0.1 broadcast_bitcast_fusion.1
  53.8 0.0 all-to-all-done
  53.8 1.8 fusion.29
  55.7 0.1 fusion.34
  55.8 0.1 copy.45
  55.9 24.1 %all-gather.1 = bf16[8,128,128]{2,1,0:T(8,128)(2,1)} all-gather(bf16[2,128,128]{2,1,0:T(8,128)(2,1)S(1)} %copy.45), channel_id=3, replica_groups=mesh['y'=8,'zl'=4,'zh'=2,'x'=4,'c'=2] {'zl'}, dimensions={0}, use_global_device_ids=true | all-gather | bytes 327680 | tf_op jit(solution)/shard_map/all_gather | solution.py:73
  80.0 1.8 fusion.28
  81.8 0.0 all-gather.7.cloned.1.call-update
  81.9 0.9 fusion.67
  82.8 0.9 fusion.69
  83.7 0.7 fusion.31
  84.4 23.2 %all-gather.5.cloned.1.call-done = bf16[32,2,128,128]{2,0,3,1:T(8,128)(2,1)} async-done(((bf16[8,2,128,128]{2,0,3,1:T(8,128)(2,1)}), bf16[32,2,128,128]{2,0,3,1:T(8,128)(2,1)}) %all-gather.5.cloned.1.call-update) | async-done | bytes 2097168 | tf_op jit(solution)/shard_map/all_gather | solution.py:73
  107.6 2.9 %fusion.64 = (bf16[32,1,128,128]{2,0,3,1:T(8,128)(2,1)}, bf16[32,1,128,128]{2,0,3,1:T(8,128)(2,1)S(1)}) fusion(bf16[32,2,128,128]{2,0,3,1:T(8,128)(2,1)} %all-gather.5.cloned.1.call-done), kind=kLoop, calls=%fused_computation.107 | loop fusion | bytes 4194304 | tf_op jit(solution)/shard_map/slice | solution.py:134
  110.5 1.5 reshape_squeeze.26
  112.0 1.3 reshape_squeeze.27
  113.3 0.9 fusion.66
  114.2 0.9 fusion.4
  115.2 3.1 %fusion.24 = f32[128,2,64]{0,2,1:T(8,128)S(1)} fusion(bf16[4096,2,64]{0,2,1:T(8,128)(2,1)S(1)} %copy-done.2, f32[2,128,4096]{2,1,0:T(8,128)S(1)} %get-tuple-element.23, f32[2,128]{1,0:T(2,128)S(1)} %get-tuple-element.22, pred[4096]{0:T(1024)(128)(4,1)S(1)} %broadcast_bitcast_fusion.1, f32[128,2]{0,1:T(2,128)S(1)} %get-tuple-element.11), kind=kOutput, calls=%fused_computation.34 | convolution fusion | flops 807419904 | bytes 5314560 | tf_op jit(solution)/shard_map/hqk,khd->qhd/dot_general | solution.py:57
  118.2 0.8 fusion.27
  119.1 1.2 fusion.2
  120.3 7.0 %all-to-all-start.1 = ((bf16[16,8,2560]{2,1,0:T(8,128)(2,1)}), bf16[16,8,2560]{2,1,0:T(8,128)(2,1)S(1)}, u32[]{:S(2)}, u32[]{:S(2)}) async-start(bf16[16,8,2560]{2,1,0:T(8,128)(2,1)} %fusion.2), calls=%async_computation.1 | async-start | bytes 1310720 | tf_op jit(solution)/shard_map/all_to_all | solution.py:131
  127.3 0.1 broadcast_bitcast_fusion
  127.3 19.1 %all-to-all-done.1 = bf16[16,8,2560]{2,1,0:T(8,128)(2,1)S(1)} async-done(((bf16[16,8,2560]{2,1,0:T(8,128)(2,1)}), bf16[16,8,2560]{2,1,0:T(8,128)(2,1)S(1)}, u32[]{:S(2)}, u32[]{:S(2)}) %all-to-all-start.1) | async-done | bytes 655392 | tf_op jit(solution)/shard_map/all_to_all | solution.py:131
  146.4 0.7 reduce_sum.120
  147.1 2.7 %fusion.63 = (bf16[32,1,128,128]{3,2,1,0:T(8,128)(2,1)S(1)}, bf16[32,1,128,128]{3,2,1,0:T(8,128)(2,1)}) fusion(bf16[32,2,128,128]{3,2,1,0:T(8,128)(2,1)} %all-gather.7.cloned.1.call-done), kind=kLoop, calls=%fused_computation.106 | loop fusion | bytes 4194304 | tf_op jit(solution)/shard_map/slice | solution.py:136
  149.9 1.0 copy.48
  150.8 0.5 reshape_squeeze.30
  151.3 1.9 copy.49
  153.3 1.3 reshape_squeeze.31
  154.6 0.9 fusion.68
  155.5 0.9 fusion.6
  156.4 3.1 %fusion.25 = f32[128,2,64]{0,2,1:T(8,128)S(1)} fusion(bf16[4096,2,64]{0,2,1:T(8,128)(2,1)S(1)} %copy-done.1, f32[2,128,4096]{2,1,0:T(8,128)S(1)} %get-tuple-element.27, f32[2,128]{1,0:T(2,128)S(1)} %get-tuple-element.26, pred[4096]{0:T(1024)(128)(4,1)S(1)} %broadcast_bitcast_fusion, f32[128,2]{0,1:T(2,128)S(1)} %get-tuple-element.8), kind=kOutput, calls=%fused_computation.35 | convolution fusion | flops 807419904 | bytes 5314560 | tf_op jit(solution)/shard_map/hqk,khd->qhd/dot_general | solution.py:57
  159.5 0.8 fusion.26
  160.4 0.4 fusion.3
  160.8 31.8 %all_to_all.15 = bf16[16,8,2560]{2,1,0:T(8,128)(2,1)S(1)} all-to-all(bf16[16,8,2560]{2,1,0:T(8,128)(2,1)S(1)} %fusion.3), channel_id=1, replica_groups=mesh['y'=8,'zl'=4,'zh'=2,'x'=4,'c'=2] {'zh','x','c'}, dimensions={0} | all-to-all | bytes 1310720 | tf_op jit(solution)/shard_map/all_to_all | solution.py:131
  192.5 0.7 reduce_sum.127
  (28 shorter events, 0.2 us)
Async XLA Ops:
  7.2 111.9 %copy-start = (bf16[128,2560]{1,0:T(8,128)(2,1)S(1)}, bf16[128,2560]{1,0:T(8,128)(2,1)}, u32[]{:S(2)}) copy-start(bf16[128,2560]{1,0:T(8,128)(2,1)} %param.14) | copy-start | bytes 1966084
  7.2 16.5 %copy-start.3 = (bf16[2,128,128]{2,1,0:T(8,128)(2,1)S(1)}, bf16[2,128,128]{2,1,0:T(8,128)(2,1)}, u32[]{:S(2)}) copy-start(bf16[2,128,128]{2,1,0:T(8,128)(2,1)} %param.12) | copy-start | bytes 196612
  7.2 40.8 %copy-start.6 = (s32[32]{0:T(128)S(1)}, s32[32]{0:T(128)}, u32[]{:S(2)}) copy-start(s32[32]{0:T(128)} %param.18) | copy-start | bytes 388
  7.2 40.9 %copy-start.4 = (s32[32,16]{0,1:T(8,128)S(1)}, s32[32,16]{0,1:T(8,128)}, u32[]{:S(2)}) copy-start(s32[32,16]{0,1:T(8,128)} %param.17) | copy-start | bytes 6148
  9.3 41.6 %copy-start.7 = (f32[128]{0:T(128)S(1)}, f32[128]{0:T(128)}, u32[]{:S(2)}) copy-start(f32[128]{0:T(128)} %param.15) | copy-start | bytes 1540
  9.3 41.7 %copy-start.5 = (f32[128]{0:T(128)S(1)}, f32[128]{0:T(128)}, u32[]{:S(2)}) copy-start(f32[128]{0:T(128)} %param.16) | copy-start | bytes 1540
  9.3 42.0 %copy-start.8 = (s32[32]{0:T(128)S(1)}, s32[32]{0:T(128)}, u32[]{:S(2)}) copy-start(s32[32]{0:T(128)} %param.19) | copy-start | bytes 388
  9.3 44.6 %all-to-all-start = ((bf16[2,16,8,2560]{3,2,0,1:T(8,128)(2,1)}), bf16[2,16,8,2560]{3,2,0,1:T(8,128)(2,1)}, u32[]{:S(2)}, u32[]{:S(2)}) async-start(bf16[2,16,8,2560]{3,2,0,1:T(8,128)(2,1)} %broadcast_in_dim.109), calls=%async_computation | async-start | bytes 2621440 | tf_op jit(solution)/shard_map/all_to_all | solution.py:100
  23.7 83.9 %all-gather.5.cloned.1.call-start = ((), (), s32[]{:S(2)}) async-start(), calls=%async_computation.3 | async-start | bytes 2621440 | tf_op jit(solution)/shard_map/all_gather | solution.py:73
  48.0 99.2 %all-gather.7.cloned.1.call-start = ((), (), s32[]{:S(2)}) async-start(), calls=%async_computation.4 | async-start | bytes 2359296 | tf_op jit(solution)/shard_map/all_gather | solution.py:73
  113.3 1.9 copy-start.2
  120.3 26.1 %all-to-all-start.1 = ((bf16[16,8,2560]{2,1,0:T(8,128)(2,1)}), bf16[16,8,2560]{2,1,0:T(8,128)(2,1)S(1)}, u32[]{:S(2)}, u32[]{:S(2)}) async-start(bf16[16,8,2560]{2,1,0:T(8,128)(2,1)} %fusion.2), calls=%async_computation.1 | async-start | bytes 1310720 | tf_op jit(solution)/shard_map/all_to_all | solution.py:131
  154.6 1.9 copy-start.1
Sparse Core Ops, SparseCore 0:
  48.1 59.4 all-gather.4
  109.7 37.3 all-gather.6

commit v4 on v3

--- a/solution.py
+++ b/solution.py
@@ -95,9 +95,9 @@
     sizes = [s for _, s in PIPE_PARTS]
     remote_stale = remote.reshape(BPM, *sizes).transpose(0, 2, 1).reshape(BPM, -1)
 
-    pair = jnp.stack([x_first, x_second])
-    spread = jnp.broadcast_to(pair[:, None], (2, n_seq) + x_first.shape)
-    xs = lax.all_to_all(spread, SEQ, 1, 1, tiled=False).reshape(2, tokens, -1)
+    def exchange_rows(x):
+        spread = jnp.broadcast_to(x[None], (n_seq,) + x.shape)
+        return lax.all_to_all(spread, SEQ, 0, 0, tiled=False).reshape(tokens, -1)
 
     def project(x):
         raw = jnp.einsum("rd,cdh->crh", x, w_qkv, preferred_element_type=jnp.float32)
@@ -106,11 +106,11 @@
         values = raw[2].astype(jnp.bfloat16)
         return (query, keys, values)
 
-    q1, k1, v1 = project(xs[0])
-    q2, k2, v2 = project(xs[1])
+    q1, k1, v1 = project(exchange_rows(x_first))
 
     fresh_kv = gather_pipe(jnp.stack([k1, v1])[None], tuple(reversed(PIPE)))
     count = fresh_kv.shape[0] * tokens
+    q2, k2, v2 = project(exchange_rows(x_second))
 
     def attend(query, keys, values, piece_k, piece_v, remote):
         query_h = query.reshape(tokens, heads, HS)

time: 204 us -> 221 us (1.083)
  starting transfers between devices: 21.4 us -> 38 us
  waiting for transfers between devices: 42.3 us -> 31.9 us
  blocking collectives: 78.9 us -> 88.4 us
  local copies, waits for them, and re-layouts: 20 us -> 22.4 us
    all_to_all x1 -> x2, starting transfers between devices: 14.4 us -> 28.2 us  [exchange_rows(): return lax.all_to_all(spread, SEQ, 0, 0, tiled=False).reshape(tokens, -1)]
    all_gather x2, blocking collectives: 47.2 us -> 56.3 us  [gather_pipe(): piece = lax.all_gather(piece, name, axis=0, tiled=True)]
    all_gather x2, waiting for transfers between devices: 23.2 us -> 16.9 us  [gather_pipe(): piece = lax.all_gather(piece, name, axis=0, tiled=True)]
    all_to_all x1, waiting for transfers between devices: 19.1 us -> 15 us  [attend(): lax.all_to_all(part.reshape(n_seq, tokens // n_seq, -1), SEQ, 0, 0, tiled...]
    unnamed x2 -> x0, matrix products: 3.5 us -> none
    all_to_all x1, starting transfers between devices: 6.97 us -> 9.68 us  [attend(): lax.all_to_all(part.reshape(n_seq, tokens // n_seq, -1), SEQ, 0, 0, tiled...]
  transfers between devices with their start and end apart: 4 -> 5, of which waited for: 2 -> 3; matrix products, arithmetic and copies ran while one was open for 13% -> 11% of each run, Pallas kernels for 0% -> 0%
where the time goes in v4:
time: 221 us; the launch traced here: 217 us
  blocking collectives  88.4 us (40%)
  starting transfers between devices  38 us (17%)
  waiting for transfers between devices  31.9 us (14%)
  local copies, waits for them, and re-layouts  22.4 us (10%)
  matrix products  15.5 us (7%)
  between operations  14.5 us (7%)
  other arithmetic  6.83 us (3%)
    all_gather x2, blocking collectives, gather_pipe(): piece = lax.all_gather(piece, name, axis=0, tiled=True)  56.3 us
    all_to_all x1, blocking collectives, attend(): lax.all_to_all(part.reshape(n_seq, tokens // n_seq, -1), SEQ, 0, 0, tiled...  32.1 us
    all_to_all x2, starting transfers between devices, exchange_rows(): return lax.all_to_all(spread, SEQ, 0, 0, tiled=False).reshape(tokens, -1)  28.2 us
    all_gather x2, waiting for transfers between devices, gather_pipe(): piece = lax.all_gather(piece, name, axis=0, tiled=True)  16.9 us
    all_to_all x1, waiting for transfers between devices, attend(): lax.all_to_all(part.reshape(n_seq, tokens // n_seq, -1), SEQ, 0, 0, tiled...  15 us
    all_to_all x1, starting transfers between devices, attend(): lax.all_to_all(part.reshape(n_seq, tokens // n_seq, -1), SEQ, 0, 0, tiled...  9.68 us
    dot_general x4, matrix products, partial_attend(): jnp.einsum('hqk,khd->qhd', weights, values.astype(jnp.float32), precision...  7.73 us
    slice x3, local copies, waits for them, and re-layouts, on_device(): out_second = attend(q2, k2, v2, fresh_kv[:, 0], fresh_kv[:, 1], remote)  7.67 us
  transfers between devices with their start and end apart: 5, of which 3 were waited for; matrix products, arithmetic and copies ran while one was open for 11% of the time, Pallas kernels for 0%

profile of v4, /device:TPU:1, one launch (start us, length us, event | category | flops | bytes accessed | tf_op | source)
XLA Modules:
  0.0 217.5 jit_solution(8189089348842671414)
XLA Ops:
  7.2 0.0 copy-start
  7.2 1.8 broadcast_in_dim.115
  9.0 14.2 %all-to-all-start = ((bf16[16,8,2560]{2,1,0:T(8,128)(2,1)}), bf16[16,8,2560]{2,1,0:T(8,128)(2,1)S(1)}, u32[]{:S(2)}, u32[]{:S(2)}) async-start(bf16[16,8,2560]{2,1,0:T(8,128)(2,1)} %broadcast_in_dim.115), calls=%async_computation | async-start | bytes 1310720 | tf_op jit(solution)/shard_map/all_to_all | solution.py:100
  23.3 0.0 all-gather.5.cloned.1.call-start
  23.3 22.7 %all-gather = bf16[16,128,128]{2,1,0:T(8,128)(2,1)S(1)} all-gather(bf16[2,128,128]{2,1,0:T(8,128)(2,1)} %param.12), channel_id=2, replica_groups=mesh['y'=8,'zl'=4,'zh'=2,'x'=4,'c'=2] {'y'}, dimensions={0}, use_global_device_ids=true | all-gather | bytes 589824 | tf_op jit(solution)/shard_map/all_gather | solution.py:73
  46.0 1.1 copy.44
  47.1 0.0 all-gather.5.cloned.1.call-update
  47.2 0.7 iota_compare_fusion.1
  47.9 0.1 copy.41
  48.0 0.2 convert_reduce_fusion
  48.2 0.2 fusion.45
  48.4 0.2 convolution_compare_fusion
  48.6 0.0 all-to-all-done
  48.6 0.9 broadcast_in_dim.128
  49.5 14.0 %all-to-all-start.2 = ((bf16[16,8,2560]{2,1,0:T(8,128)(2,1)}), bf16[16,8,2560]{2,1,0:T(8,128)(2,1)S(1)}, u32[]{:S(2)}, u32[]{:S(2)}) async-start(bf16[16,8,2560]{2,1,0:T(8,128)(2,1)} %broadcast_in_dim.128), calls=%async_computation.2 | async-start | bytes 1310720 | tf_op jit(solution)/shard_map/all_to_all | solution.py:100
  63.5 0.0 all-gather.7.cloned.1.call-start
  63.5 0.5 broadcast.214
  64.0 1.2 fusion.62
  65.2 0.1 mul.181
  65.3 0.1 reshape.237
  65.4 0.1 copy.43
  65.5 0.1 broadcast_in_dim.120
  65.6 0.1 mul.187
  65.7 0.6 dynamic_slice.6
  66.3 0.1 broadcast_bitcast_fusion.1
  66.3 0.7 convolution_bitcast_fusion.1
  67.1 0.0 copy-start.7
  67.1 0.1 fusion.34
  67.2 0.5 copy-done.7
  67.7 0.1 copy.45
  67.8 33.5 %all-gather.1 = bf16[8,128,128]{2,1,0:T(8,128)(2,1)} all-gather(bf16[2,128,128]{2,1,0:T(8,128)(2,1)S(1)} %copy.45), channel_id=3, replica_groups=mesh['y'=8,'zl'=4,'zh'=2,'x'=4,'c'=2] {'zl'}, dimensions={0}, use_global_device_ids=true | all-gather | bytes 327680 | tf_op jit(solution)/shard_map/all_gather | solution.py:73
  101.4 0.7 convolution_bitcast_fusion
  102.2 0.0 all-gather.7.cloned.1.call-update
  102.3 0.9 fusion.67
  103.2 1.6 fusion.69
  104.8 1.2 fusion.31
  106.0 14.2 %all-gather.5.cloned.1.call-done = bf16[32,2,128,128]{2,0,3,1:T(8,128)(2,1)} async-done(((bf16[8,2,128,128]{2,0,3,1:T(8,128)(2,1)}), bf16[32,2,128,128]{2,0,3,1:T(8,128)(2,1)}) %all-gather.5.cloned.1.call-update) | async-done | bytes 2097168 | tf_op jit(solution)/shard_map/all_gather | solution.py:73
  120.2 2.9 %fusion.64 = (bf16[32,1,128,128]{2,0,3,1:T(8,128)(2,1)}, bf16[32,1,128,128]{2,0,3,1:T(8,128)(2,1)S(1)}) fusion(bf16[32,2,128,128]{2,0,3,1:T(8,128)(2,1)} %all-gather.5.cloned.1.call-done), kind=kLoop, calls=%fused_computation.106 | loop fusion | bytes 4194304 | tf_op jit(solution)/shard_map/slice | solution.py:134
  123.1 1.3 reshape_squeeze.27
  124.4 1.5 reshape_squeeze.26
  125.9 0.9 fusion.66
  126.9 0.0 copy-start.8
  126.9 0.0 copy-start.2
  126.9 0.9 fusion.4
  127.9 3.0 %fusion.24 = f32[128,2,64]{0,2,1:T(8,128)S(1)} fusion(bf16[4096,2,64]{0,2,1:T(8,128)(2,1)S(1)} %copy-done.4, f32[2,128,4096]{2,1,0:T(8,128)S(1)} %get-tuple-element.23, f32[2,128]{1,0:T(2,128)S(1)} %get-tuple-element.22, pred[4096]{0:T(1024)(128)(4,1)S(1)} %broadcast_bitcast_fusion.1, f32[128,2]{0,1:T(2,128)S(1)} %get-tuple-element.11), kind=kOutput, calls=%fused_computation.36 | convolution fusion | flops 807419904 | bytes 5314560 | tf_op jit(solution)/shard_map/hqk,khd->qhd/dot_general | solution.py:57
  130.9 0.8 fusion.27
  131.7 1.2 fusion.2
  132.9 9.7 %all-to-all-start.1 = ((bf16[16,8,2560]{2,1,0:T(8,128)(2,1)}), bf16[16,8,2560]{2,1,0:T(8,128)(2,1)S(1)}, u32[]{:S(2)}, u32[]{:S(2)}) async-start(bf16[16,8,2560]{2,1,0:T(8,128)(2,1)} %fusion.2), calls=%async_computation.1 | async-start | bytes 1310720 | tf_op jit(solution)/shard_map/all_to_all | solution.py:131
  142.6 0.1 broadcast_bitcast_fusion
  142.7 15.0 %all-to-all-done.1 = bf16[16,8,2560]{2,1,0:T(8,128)(2,1)S(1)} async-done(((bf16[16,8,2560]{2,1,0:T(8,128)(2,1)}), bf16[16,8,2560]{2,1,0:T(8,128)(2,1)S(1)}, u32[]{:S(2)}, u32[]{:S(2)}) %all-to-all-start.1) | async-done | bytes 655392 | tf_op jit(solution)/shard_map/all_to_all | solution.py:131
  157.7 0.7 reduce_sum.120
  158.4 2.6 %all-gather.7.cloned.1.call-done = bf16[32,2,128,128]{3,2,1,0:T(8,128)(2,1)} async-done(((bf16[4,2,128,128]{3,2,1,0:T(8,128)(2,1)}), bf16[32,2,128,128]{3,2,1,0:T(8,128)(2,1)}) %all-gather.7.cloned.1.call-update) | async-done | bytes 2097168 | tf_op jit(solution)/shard_map/all_gather | solution.py:73
  161.1 3.1 %fusion.63 = (bf16[32,1,128,128]{3,2,1,0:T(8,128)(2,1)}, bf16[32,1,128,128]{3,2,1,0:T(8,128)(2,1)}) fusion(bf16[32,2,128,128]{3,2,1,0:T(8,128)(2,1)} %all-gather.7.cloned.1.call-done), kind=kLoop, calls=%fused_computation.105 | loop fusion | bytes 4194304 | tf_op jit(solution)/shard_map/slice | solution.py:136
  164.2 1.9 copy.49
  166.1 1.3 reshape_squeeze.31
  167.4 2.7 %copy.48 = bf16[32,1,128,128]{2,0,3,1:T(8,128)(2,1)} copy(bf16[32,1,128,128]{3,2,1,0:T(8,128)(2,1)} %get-tuple-element.14) | data formatting | bytes 2097152 | tf_op jit(solution)/shard_map/slice | solution.py:136
  170.1 1.5 reshape_squeeze.30
  171.6 0.9 fusion.68
  172.6 0.9 fusion.6
  173.5 3.1 %fusion.25 = f32[128,2,64]{0,2,1:T(8,128)S(1)} fusion(bf16[4096,2,64]{0,2,1:T(8,128)(2,1)S(1)} %copy-done.1, f32[2,128,4096]{2,1,0:T(8,128)S(1)} %get-tuple-element.27, f32[2,128]{1,0:T(2,128)S(1)} %get-tuple-element.26, pred[4096]{0:T(1024)(128)(4,1)S(1)} %broadcast_bitcast_fusion, f32[128,2]{0,1:T(2,128)S(1)} %get-tuple-element.8), kind=kOutput, calls=%fused_computation.37 | convolution fusion | flops 807419904 | bytes 5314560 | tf_op jit(solution)/shard_map/hqk,khd->qhd/dot_general | solution.py:57
  176.6 0.8 fusion.26
  177.4 0.4 fusion.3
  177.8 32.1 %all_to_all.20 = bf16[16,8,2560]{2,1,0:T(8,128)(2,1)S(1)} all-to-all(bf16[16,8,2560]{2,1,0:T(8,128)(2,1)S(1)} %fusion.3), channel_id=1, replica_groups=mesh['y'=8,'zl'=4,'zh'=2,'x'=4,'c'=2] {'zh','x','c'}, dimensions={0} | all-to-all | bytes 1310720 | tf_op jit(solution)/shard_map/all_to_all | solution.py:131
  209.9 0.7 reduce_sum.127
  (53 shorter events, 0.3 us)
Async XLA Ops:
  7.2 59.2 %copy-start = (bf16[3,2560,128]{2,1,0:T(8,128)(2,1)S(1)}, bf16[3,2560,128]{2,1,0:T(8,128)(2,1)}, u32[]{:S(2)}) copy-start(bf16[3,2560,128]{2,1,0:T(8,128)(2,1)} %param.13) | copy-start | bytes 5898244
  7.2 40.7 %copy-start.14 = (s32[32,16]{0,1:T(8,128)S(1)}, s32[32,16]{0,1:T(8,128)}, u32[]{:S(2)}) copy-start(s32[32,16]{0,1:T(8,128)} %param.17) | copy-start | bytes 6148
  7.2 41.0 %copy-start.19 = (s32[32]{0:T(128)S(1)}, s32[32]{0:T(128)}, u32[]{:S(2)}) copy-start(s32[32]{0:T(128)} %param.19) | copy-start | bytes 388
  7.2 41.4 %copy-start.9 = (bf16[8,2560]{1,0:T(8,128)(2,1)S(1)}, bf16[8,2560]{1,0:T(8,128)(2,1)}, u32[]{:S(2)}) copy-start(bf16[8,2560]{1,0:T(8,128)(2,1)} %param.11) | copy-start | bytes 122884
  7.2 58.0 %copy-start.20 = (f32[128]{0:T(128)S(1)}, f32[128]{0:T(128)}, u32[]{:S(2)}) copy-start(f32[128]{0:T(128)} %param.15) | copy-start | bytes 1540
  7.2 58.4 %copy-start.18 = (f32[128]{0:T(128)S(1)}, f32[128]{0:T(128)}, u32[]{:S(2)}) copy-start(f32[128]{0:T(128)} %param.16) | copy-start | bytes 1540
  9.0 39.6 %all-to-all-start = ((bf16[16,8,2560]{2,1,0:T(8,128)(2,1)}), bf16[16,8,2560]{2,1,0:T(8,128)(2,1)S(1)}, u32[]{:S(2)}, u32[]{:S(2)}) async-start(bf16[16,8,2560]{2,1,0:T(8,128)(2,1)} %broadcast_in_dim.115), calls=%async_computation | async-start | bytes 1310720 | tf_op jit(solution)/shard_map/all_to_all | solution.py:100
  23.3 97.0 %all-gather.5.cloned.1.call-start = ((), (), s32[]{:S(2)}) async-start(), calls=%async_computation.4 | async-start | bytes 2621440 | tf_op jit(solution)/shard_map/all_gather | solution.py:73
  49.5 51.9 %all-to-all-start.2 = ((bf16[16,8,2560]{2,1,0:T(8,128)(2,1)}), bf16[16,8,2560]{2,1,0:T(8,128)(2,1)S(1)}, u32[]{:S(2)}, u32[]{:S(2)}) async-start(bf16[16,8,2560]{2,1,0:T(8,128)(2,1)} %broadcast_in_dim.128), calls=%async_computation.2 | async-start | bytes 1310720 | tf_op jit(solution)/shard_map/all_to_all | solution.py:100
  63.5 97.6 %all-gather.7.cloned.1.call-start = ((), (), s32[]{:S(2)}) async-start(), calls=%async_computation.5 | async-start | bytes 2359296 | tf_op jit(solution)/shard_map/all_gather | solution.py:73
  65.7 36.6 %copy-start.15 = (f32[2,64]{1,0:T(2,128)}, f32[2,64]{1,0:T(2,128)S(1)}, u32[]{:S(2)}) copy-start(f32[2,64]{1,0:T(2,128)S(1)} %mul.187) | copy-start | bytes 1540
  67.1 0.6 copy-start.7
  103.1 2.9 %copy-start.5 = (f32[2,128,128]{1,2,0:T(8,128)}, f32[2,128,128]{1,2,0:T(8,128)S(1)}, u32[]{:S(2)}) copy-start(f32[2,128,128]{1,2,0:T(8,128)S(1)} %get-tuple-element.25) | copy-start | bytes 393220
  103.1 2.9 %copy-start.12 = (f32[2,128]{1,0:T(2,128)}, f32[2,128]{1,0:T(2,128)S(1)}, u32[]{:S(2)}) copy-start(f32[2,128]{1,0:T(2,128)S(1)} %get-tuple-element.24) | copy-start | bytes 3076
  104.8 1.2 copy-start.10
  125.9 1.9 copy-start.13
  125.9 1.9 copy-start.4
  126.9 4.0 %copy-start.6 = (f32[2,128,128]{1,2,0:T(8,128)S(1)}, f32[2,128,128]{1,2,0:T(8,128)}, u32[]{:S(2)}) copy-start(f32[2,128,128]{1,2,0:T(8,128)} %copy-done.5) | copy-start | bytes 393220
  126.9 4.0 %copy-start.8 = (bf16[1,128,128]{1,2,0:T(8,128)(2,1)S(1)}, bf16[1,128,128]{1,2,0:T(8,128)(2,1)}, u32[]{:S(2)}) copy-start(bf16[1,128,128]{1,2,0:T(8,128)(2,1)} %copy-done.7) | copy-start | bytes 98308
  126.9 4.8 %copy-start.2 = (bf16[128,2560]{1,0:T(8,128)(2,1)S(1)}, bf16[128,2560]{1,0:T(8,128)(2,1)}, u32[]{:S(2)}) copy-start(bf16[128,2560]{1,0:T(8,128)(2,1)} %param.14) | copy-start | bytes 1966084
  127.8 14.8 %copy-start.17 = (pred[1,32]{1,0:T(4,128)(4,1)S(1)}, pred[1,32]{1,0:T(4,128)(4,1)}, u32[]{:S(2)}) copy-start(pred[1,32]{1,0:T(4,128)(4,1)} %get-tuple-element.13) | copy-start | bytes 100
  132.9 24.8 %all-to-all-start.1 = ((bf16[16,8,2560]{2,1,0:T(8,128)(2,1)}), bf16[16,8,2560]{2,1,0:T(8,128)(2,1)S(1)}, u32[]{:S(2)}, u32[]{:S(2)}) async-start(bf16[16,8,2560]{2,1,0:T(8,128)(2,1)} %fusion.2), calls=%async_computation.1 | async-start | bytes 1310720 | tf_op jit(solution)/shard_map/all_to_all | solution.py:131
  171.6 1.9 copy-start.11
  171.6 1.9 copy-start.16
  171.6 1.9 copy-start.1
  172.6 4.9 %copy-start.3 = (bf16[128,2560]{1,0:T(8,128)(2,1)S(1)}, bf16[128,2560]{1,0:T(8,128)(2,1)}, u32[]{:S(2)}) copy-start(bf16[128,2560]{1,0:T(8,128)(2,1)} %param.14) | copy-start | bytes 1966084
Sparse Core Ops, SparseCore 0:
  47.3 72.9 all-gather.4
  122.3 38.7 all-gather.6

commit v5 on v3

--- a/solution.py
+++ b/solution.py
@@ -91,13 +91,13 @@
     own = lax.dynamic_slice_in_dim(mine, me * BPM, BPM, 1)
     remote = mine & (batch_of != me)[None, :]
 
-    stale = gather_pipe(stale_kv[None], PIPE)
-    sizes = [s for _, s in PIPE_PARTS]
-    remote_stale = remote.reshape(BPM, *sizes).transpose(0, 2, 1).reshape(BPM, -1)
+    near = lax.all_gather(stale_kv[None], PIPE[1], axis=0, tiled=True)
+    pair, near = lax.optimization_barrier((jnp.stack([x_first, x_second]), near))
+    stale = lax.all_gather(near, PIPE[0], axis=0, tiled=True)
 
-    pair = jnp.stack([x_first, x_second])
-    spread = jnp.broadcast_to(pair[:, None], (2, n_seq) + x_first.shape)
-    xs = lax.all_to_all(spread, SEQ, 1, 1, tiled=False).reshape(2, tokens, -1)
+    def exchange_rows(x):
+        spread = jnp.broadcast_to(x[:, None], (x.shape[0], n_seq) + x.shape[1:])
+        return lax.all_to_all(spread, SEQ, 1, 1, tiled=False).reshape(x.shape[0], tokens, -1)
 
     def project(x):
         raw = jnp.einsum("rd,cdh->crh", x, w_qkv, preferred_element_type=jnp.float32)
@@ -106,6 +106,7 @@
         values = raw[2].astype(jnp.bfloat16)
         return (query, keys, values)
 
+    xs = exchange_rows(pair)
     q1, k1, v1 = project(xs[0])
     q2, k2, v2 = project(xs[1])
 
@@ -131,7 +132,7 @@
         sent = lax.all_to_all(part.reshape(n_seq, tokens // n_seq, -1), SEQ, 0, 0, tiled=False)
         return jnp.sum(sent.astype(jnp.float32), axis=0).astype(jnp.bfloat16)
 
-    out_first = attend(q1, k1, v1, stale[:, 0], stale[:, 1], remote_stale)
+    out_first = attend(q1, k1, v1, stale[:, 0], stale[:, 1], remote)
     out_first, fresh_kv = lax.optimization_barrier((out_first, fresh_kv))
     out_second = attend(q2, k2, v2, fresh_kv[:, 0], fresh_kv[:, 1], remote)
     return (out_first, out_second)

time: 204 us -> 188 us (0.922)
  blocking collectives: 78.9 us -> 62.3 us
    all_gather x2 -> x1, blocking collectives: 47.2 us -> 16.2 us  [gather_pipe(): piece = lax.all_gather(piece, name, axis=0, tiled=True)]
    all_to_all x1, waiting for transfers between devices: 0.01 us -> 25.4 us  [exchange_rows(): lax.all_to_all(spread, SEQ, 1, 1, tiled=False)]
    all_gather x2 -> x1, waiting for transfers between devices: 23.2 us -> 0.01 us  [gather_pipe(): piece = lax.all_gather(piece, name, axis=0, tiled=True)]
    all_gather x0 -> x1, blocking collectives: none -> 17.5 us  [on_device(): near = lax.all_gather(stale_kv[None], PIPE[1], axis=0, tiled=True)]
    all_to_all x1, blocking collectives: 31.8 us -> 28.6 us  [attend(): lax.all_to_all(part.reshape(n_seq, tokens // n_seq, -1), SEQ, 0, 0, tiled...]
    slice x1 -> x3, local copies, waits for them, and re-layouts: 2.88 us -> 5.61 us  [on_device(): out_first = attend(q1, k1, v1, stale[:, 0], stale[:, 1], remote)]
    reduce_sum x3, other arithmetic: 2.51 us -> 4.86 us  [partial_attend(): total = jnp.sum(weights, axis=(3, 4))]
  transfers between devices with their start and end apart: 4 -> 4, of which waited for: 2 -> 2; matrix products, arithmetic and copies ran while one was open for 13% -> 14% of each run, Pallas kernels for 0% -> 0%
where the time goes in v5:
time: 188 us; the launch traced here: 185 us
  blocking collectives  62.3 us (33%)
  waiting for transfers between devices  43.4 us (23%)
  starting transfers between devices  19.6 us (10%)
  matrix products  19 us (10%)
  local copies, waits for them, and re-layouts  18.2 us (10%)
  between operations  14.4 us (8%)
  other arithmetic  7.68 us (4%)
    all_to_all x1, blocking collectives, attend(): lax.all_to_all(part.reshape(n_seq, tokens // n_seq, -1), SEQ, 0, 0, tiled...  28.6 us
    all_to_all x1, waiting for transfers between devices, exchange_rows(): lax.all_to_all(spread, SEQ, 1, 1, tiled=False)  25.4 us
    all_gather x1, blocking collectives, on_device(): near = lax.all_gather(stale_kv[None], PIPE[1], axis=0, tiled=True)  17.5 us
    all_to_all x1, waiting for transfers between devices, attend(): lax.all_to_all(part.reshape(n_seq, tokens // n_seq, -1), SEQ, 0, 0, tiled...  17.3 us
    all_gather x1, blocking collectives, gather_pipe(): piece = lax.all_gather(piece, name, axis=0, tiled=True)  16.2 us
    all_to_all x1, starting transfers between devices, exchange_rows(): lax.all_to_all(spread, SEQ, 1, 1, tiled=False)  12.6 us
    dot_general x4, matrix products, partial_attend(): jnp.einsum('hqk,khd->qhd', weights, values.astype(jnp.float32), precision...  7.93 us
    all_to_all x1, starting transfers between devices, attend(): lax.all_to_all(part.reshape(n_seq, tokens // n_seq, -1), SEQ, 0, 0, tiled...  7 us
  transfers between devices with their start and end apart: 4, of which 2 were waited for; matrix products, arithmetic and copies ran while one was open for 14% of the time, Pallas kernels for 0%

profile of v5, /device:TPU:1, one launch (start us, length us, event | category | flops | bytes accessed | tf_op | source)
XLA Modules:
  0.0 184.5 jit_solution(14396416417959707580)
XLA Ops:
  7.2 0.0 copy-start
  7.2 0.0 copy-start.4
  7.2 17.5 %all-gather = bf16[8,128,128]{2,1,0:T(8,128)(2,1)} all-gather(bf16[2,128,128]{2,1,0:T(8,128)(2,1)} %param.12), channel_id=2, replica_groups=mesh['y'=8,'zl'=4,'zh'=2,'x'=4,'c'=2] {'zl'}, dimensions={0}, use_global_device_ids=true | all-gather | bytes 327680 | tf_op jit(solution)/shard_map/all_gather | solution.py:94
  24.7 0.8 pad_maximum_fusion
  25.6 0.0 copy-start.8
  25.6 1.2 broadcast_in_dim.103
  26.8 12.6 %all-to-all-start = ((bf16[2,16,8,2560]{3,2,0,1:T(8,128)(2,1)}), bf16[2,16,8,2560]{3,2,0,1:T(8,128)(2,1)}, u32[]{:S(2)}, u32[]{:S(2)}) async-start(bf16[2,16,8,2560]{3,2,0,1:T(8,128)(2,1)} %broadcast_in_dim.103), calls=%async_computation | async-start | bytes 2621440 | tf_op jit(solution)/shard_map/all_to_all | solution.py:100
  39.3 0.0 all-gather.5.cloned.1.call-start
  39.4 0.7 all-gather.5.cloned.1.call-update
  40.1 0.0 all-gather.7.cloned.1.call-start
  40.1 0.0 copy-done.4
  40.1 0.1 copy.31
  40.2 2.7 %copy.30 = bf16[3,2560,128]{1,2,0:T(8,128)(2,1)S(1)} copy(bf16[3,2560,128]{2,1,0:T(8,128)(2,1)} %param.13) | data formatting | bytes 3932160 | tf_op args[3]
  42.9 0.0 copy-done.7
  42.9 0.1 mul.181
  43.0 0.0 copy-done.5
  43.0 0.1 mul.187
  43.1 0.0 copy-done.6
  43.1 0.1 iota_compare_fusion.1
  43.2 0.2 convert_reduce_fusion
  43.4 0.0 copy-done.8
  43.4 0.2 fusion.45
  43.6 0.2 convolution_compare_fusion
  43.8 0.6 dynamic_slice.6
  44.4 0.1 broadcast_bitcast_fusion
  44.5 25.4 %all-to-all-done = bf16[2,16,8,2560]{3,2,0,1:T(8,128)(2,1)} async-done(((bf16[2,16,8,2560]{3,2,0,1:T(8,128)(2,1)}), bf16[2,16,8,2560]{3,2,0,1:T(8,128)(2,1)}, u32[]{:S(2)}, u32[]{:S(2)}) %all-to-all-start) | async-done | bytes 1310752 | tf_op jit(solution)/shard_map/all_to_all | solution.py:100
  69.9 1.8 fusion.29
  71.7 0.1 fusion.34
  71.9 0.1 copy.35
  72.0 16.2 %all-gather.1 = bf16[8,128,128]{2,1,0:T(8,128)(2,1)} all-gather(bf16[2,128,128]{2,1,0:T(8,128)(2,1)S(1)} %copy.35), channel_id=3, replica_groups=mesh['y'=8,'zl'=4,'zh'=2,'x'=4,'c'=2] {'zl'}, dimensions={0}, use_global_device_ids=true | all-gather | bytes 327680 | tf_op jit(solution)/shard_map/all_gather | solution.py:73
  88.2 1.7 fusion.28
  90.0 0.0 all-gather.7.cloned.1.call-update
  90.0 0.9 fusion.66
  91.0 1.0 fusion.68
  92.0 0.7 fusion.31
  92.7 0.0 all-gather.5.cloned.1.call-done
  92.7 2.7 %fusion.63 = (bf16[32,1,128,128]{3,2,1,0:T(8,128)(2,1)S(1)}, bf16[32,1,128,128]{3,2,1,0:T(8,128)(2,1)}) fusion(bf16[32,2,128,128]{3,2,1,0:T(8,128)(2,1)} %all-gather.5.cloned.1.call-done), kind=kLoop, calls=%fused_computation.105 | loop fusion | bytes 4194304 | tf_op jit(solution)/shard_map/slice | solution.py:135
  95.4 1.0 copy.33
  96.4 0.5 reshape_squeeze.26
  96.9 1.9 %copy.34 = bf16[32,1,128,128]{2,0,3,1:T(8,128)(2,1)S(1)} copy(bf16[32,1,128,128]{3,2,1,0:T(8,128)(2,1)} %get-tuple-element.19) | data formatting | bytes 2097152 | tf_op jit(solution)/shard_map/slice | solution.py:135
  98.8 1.3 reshape_squeeze.27
  100.1 0.9 fusion.65
  101.1 0.9 fusion.4
  102.0 0.0 copy-done.2
  102.0 3.1 %fusion.24 = f32[128,2,64]{0,2,1:T(8,128)S(1)} fusion(bf16[4096,2,64]{0,2,1:T(8,128)(2,1)S(1)} %copy-done.2, f32[2,128,4096]{2,1,0:T(8,128)S(1)} %get-tuple-element.25, f32[2,128]{1,0:T(2,128)S(1)} %get-tuple-element.24, pred[4096]{0:T(1024)(128)(4,1)S(1)} %broadcast_bitcast_fusion, f32[128,2]{0,1:T(2,128)S(1)} %get-tuple-element.15), kind=kOutput, calls=%fused_computation.34 | convolution fusion | flops 807419904 | bytes 5314560 | tf_op jit(solution)/shard_map/hqk,khd->qhd/dot_general | solution.py:57
  105.1 0.9 fusion.27
  106.0 0.0 copy-done
  106.0 1.2 fusion.2
  107.2 7.0 %all-to-all-start.1 = ((bf16[16,8,2560]{2,1,0:T(8,128)(2,1)}), bf16[16,8,2560]{2,1,0:T(8,128)(2,1)S(1)}, u32[]{:S(2)}, u32[]{:S(2)}) async-start(bf16[16,8,2560]{2,1,0:T(8,128)(2,1)} %fusion.2), calls=%async_computation.1 | async-start | bytes 1310720 | tf_op jit(solution)/shard_map/all_to_all | solution.py:132
  114.2 17.3 %all-to-all-done.1 = bf16[16,8,2560]{2,1,0:T(8,128)(2,1)S(1)} async-done(((bf16[16,8,2560]{2,1,0:T(8,128)(2,1)}), bf16[16,8,2560]{2,1,0:T(8,128)(2,1)S(1)}, u32[]{:S(2)}, u32[]{:S(2)}) %all-to-all-start.1) | async-done | bytes 655392 | tf_op jit(solution)/shard_map/all_to_all | solution.py:132
  131.4 0.7 reduce_sum.120
  132.2 2.7 %fusion.62 = (bf16[32,1,128,128]{3,2,1,0:T(8,128)(2,1)S(1)}, bf16[32,1,128,128]{3,2,1,0:T(8,128)(2,1)}) fusion(bf16[32,2,128,128]{3,2,1,0:T(8,128)(2,1)} %all-gather.7.cloned.1.call-done), kind=kLoop, calls=%fused_computation.104 | loop fusion | bytes 4194304 | tf_op jit(solution)/shard_map/slice | solution.py:137
  134.9 1.0 copy.38
  135.8 0.5 reshape_squeeze.30
  136.4 2.8 %fusion.67 = (f32[2,128]{1,0:T(2,128)S(1)}, f32[2,128,4096]{2,1,0:T(8,128)}) fusion(bf16[4096,2,64]{0,2,1:T(8,128)(2,1)S(1)} %reshape_squeeze.30, f32[128,2,64]{0,2,1:T(8,128)S(1)} %bitcast.145, f32[128,2]{0,1:T(2,128)S(1)} %add_rsqrt_fusion.1, f32[2,64]{1,0:T(2,128)S(1)} %mul.181, pred[4096]{0:T(1024)(128)(4,1)S(1)} %broadcast_bitcast_fusion), kind=kOutput, calls=%fused_computation.109 | convolution fusion | flops 137412352 | bytes 5315072 | tf_op jit(solution)/shard_map/qhd,khd->hqk/dot_general | solution.py:49
  139.1 1.0 copy.39
  140.1 0.5 reshape_squeeze.31
  140.6 3.2 %fusion.6 = f32[2,128]{1,0:T(2,128)S(1)} fusion(f32[2,128,4096]{2,1,0:T(8,128)} %get-tuple-element.29, f32[2,128]{1,0:T(2,128)S(1)} %get-tuple-element.28, pred[4096]{0:T(1024)(128)(4,1)S(1)} %broadcast_bitcast_fusion), kind=kLoop, calls=%fused_computation.12 | loop fusion | flops 3145472 | bytes 4200448 | tf_op jit(solution)/shard_map/reduce_sum | solution.py:55
  143.9 0.2 copy-done.1
  144.1 3.1 %fusion.25 = f32[128,2,64]{0,2,1:T(8,128)S(1)} fusion(bf16[4096,2,64]{0,2,1:T(8,128)(2,1)S(1)} %reshape_squeeze.31, f32[2,128,4096]{2,1,0:T(8,128)S(1)} %copy-done.1, f32[2,128]{1,0:T(2,128)S(1)} %get-tuple-element.28, pred[4096]{0:T(1024)(128)(4,1)S(1)} %broadcast_bitcast_fusion, f32[128,2]{0,1:T(2,128)S(1)} %get-tuple-element.12), kind=kOutput, calls=%fused_computation.35 | convolution fusion | flops 807419904 | bytes 5314560 | tf_op jit(solution)/shard_map/hqk,khd->qhd/dot_general | solution.py:57
  147.2 0.9 fusion.26
  148.0 0.4 fusion.3
  148.4 28.6 %all_to_all.15 = bf16[16,8,2560]{2,1,0:T(8,128)(2,1)S(1)} all-to-all(bf16[16,8,2560]{2,1,0:T(8,128)(2,1)S(1)} %fusion.3), channel_id=1, replica_groups=mesh['y'=8,'zl'=4,'zh'=2,'x'=4,'c'=2] {'zh','x','c'}, dimensions={0} | all-to-all | bytes 1310720 | tf_op jit(solution)/shard_map/all_to_all | solution.py:132
  177.0 0.7 reduce_sum.127
  (24 shorter events, 0.2 us)
Async XLA Ops:
  7.2 98.8 %copy-start = (bf16[128,2560]{1,0:T(8,128)(2,1)S(1)}, bf16[128,2560]{1,0:T(8,128)(2,1)}, u32[]{:S(2)}) copy-start(bf16[128,2560]{1,0:T(8,128)(2,1)} %param.14) | copy-start | bytes 1966084
  7.2 33.0 %copy-start.4 = (s32[32,16]{0,1:T(8,128)S(1)}, s32[32,16]{0,1:T(8,128)}, u32[]{:S(2)}) copy-start(s32[32,16]{0,1:T(8,128)} %param.17) | copy-start | bytes 6148
  24.7 18.2 %copy-start.7 = (f32[128]{0:T(128)S(1)}, f32[128]{0:T(128)}, u32[]{:S(2)}) copy-start(f32[128]{0:T(128)} %param.15) | copy-start | bytes 1540
  24.7 18.3 %copy-start.5 = (f32[128]{0:T(128)S(1)}, f32[128]{0:T(128)}, u32[]{:S(2)}) copy-start(f32[128]{0:T(128)} %param.16) | copy-start | bytes 1540
  24.7 18.3 %copy-start.6 = (s32[32]{0:T(128)S(1)}, s32[32]{0:T(128)}, u32[]{:S(2)}) copy-start(s32[32]{0:T(128)} %param.18) | copy-start | bytes 388
  25.6 17.8 %copy-start.8 = (s32[32]{0:T(128)S(1)}, s32[32]{0:T(128)}, u32[]{:S(2)}) copy-start(s32[32]{0:T(128)} %param.19) | copy-start | bytes 388
  26.8 43.1 %all-to-all-start = ((bf16[2,16,8,2560]{3,2,0,1:T(8,128)(2,1)}), bf16[2,16,8,2560]{3,2,0,1:T(8,128)(2,1)}, u32[]{:S(2)}, u32[]{:S(2)}) async-start(bf16[2,16,8,2560]{3,2,0,1:T(8,128)(2,1)} %broadcast_in_dim.103), calls=%async_computation | async-start | bytes 2621440 | tf_op jit(solution)/shard_map/all_to_all | solution.py:100
  39.3 53.3 %all-gather.5.cloned.1.call-start = ((), (), s32[]{:S(2)}) async-start(), calls=%async_computation.3 | async-start | bytes 2359296 | tf_op jit(solution)/shard_map/all_gather | solution.py:96
  40.1 92.1 %all-gather.7.cloned.1.call-start = ((), (), s32[]{:S(2)}) async-start(), calls=%async_computation.4 | async-start | bytes 2359296 | tf_op jit(solution)/shard_map/all_gather | solution.py:73
  100.1 1.9 %copy-start.2 = (bf16[4096,2,64]{0,2,1:T(8,128)(2,1)S(1)}, bf16[4096,2,64]{0,2,1:T(8,128)(2,1)}, u32[]{:S(2)}) copy-start(bf16[4096,2,64]{0,2,1:T(8,128)(2,1)} %reshape_squeeze.27) | copy-start | bytes 3145732
  107.2 24.3 %all-to-all-start.1 = ((bf16[16,8,2560]{2,1,0:T(8,128)(2,1)}), bf16[16,8,2560]{2,1,0:T(8,128)(2,1)S(1)}, u32[]{:S(2)}, u32[]{:S(2)}) async-start(bf16[16,8,2560]{2,1,0:T(8,128)(2,1)} %fusion.2), calls=%async_computation.1 | async-start | bytes 1310720 | tf_op jit(solution)/shard_map/all_to_all | solution.py:132
  136.3 2.8 %copy-start.3 = (bf16[32,1,128,128]{3,2,1,0:T(8,128)(2,1)S(1)}, bf16[32,1,128,128]{3,2,1,0:T(8,128)(2,1)}, u32[]{:S(2)}) copy-start(bf16[32,1,128,128]{3,2,1,0:T(8,128)(2,1)} %get-tuple-element.17) | copy-start | bytes 3145732
  140.6 3.5 %copy-start.1 = (f32[2,128,4096]{2,1,0:T(8,128)S(1)}, f32[2,128,4096]{2,1,0:T(8,128)}, u32[]{:S(2)}) copy-start(f32[2,128,4096]{2,1,0:T(8,128)} %get-tuple-element.29) | copy-start | bytes 12582916
Sparse Core Ops, SparseCore 0:
  42.2 40.0 all-gather.4
  90.2 38.8 all-gather.6

commit v6 on v5

--- a/solution.py
+++ b/solution.py
@@ -1,9 +1,12 @@
+import functools
 import math
 
 import jax
 import jax.numpy as jnp
 import numpy as np
 from jax import lax
+from jax.experimental import pallas as pl
+from jax.experimental.pallas import tpu as pltpu
 from jax.sharding import Mesh
 from jax.sharding import PartitionSpec as P
 
@@ -42,30 +45,66 @@
     return (grid * factor).reshape(count, -1) * gain[None, :]
 
 
-def partial_attend(query, keys, values, allowed, scale):
-    heads = query.shape[1]
-    qrows = query.shape[0]
-    krows = keys.shape[0]
-    scores = jnp.einsum("qhd,khd->hqk", query, keys, preferred_element_type=jnp.float32) * scale
-    grid = scores.reshape(heads, qrows // BLOCK, BLOCK, krows // BLOCK, BLOCK)
-    keep = allowed[None, :, None, :, None]
-    grid = jnp.where(keep, grid, NEG)
-    top = jnp.max(grid, axis=(3, 4))
-    weights = jnp.where(keep, jnp.exp(grid - top[:, :, :, None, None]), 0.0)
-    total = jnp.sum(weights, axis=(3, 4))
-    weights = weights.reshape(heads, qrows, krows)
-    summed = jnp.einsum("hqk,khd->qhd", weights, values.astype(jnp.float32), precision=HIGH)
-    return (top.reshape(heads, qrows), total.reshape(heads, qrows), summed)
+def attn_kernel(allowed_ref, q_ref, k_ref, v_ref, kv_ref, o_ref, *, scale, n_blocks):
+    q = q_ref[...]
+    rows, width = q.shape
+    lane = lax.broadcasted_iota(jnp.int32, (rows, width), 1)
+    first = lane < HS
+    zero = jnp.zeros_like(q)
+    q0 = jnp.where(first, q, zero)
+    q1 = jnp.where(first, zero, q)
+
+    def scores(kb):
+        dims = (((1,), (1,)), ((), ()))
+        s0 = lax.dot_general(q0, kb, dims, preferred_element_type=jnp.float32) * scale
+        s1 = lax.dot_general(q1, kb, dims, preferred_element_type=jnp.float32) * scale
+        return s0, s1
+
+    def update(carry, s0, s1, vb):
+        m0, m1, l0, l1, acc = carry
+        n0 = jnp.maximum(m0, jnp.max(s0, axis=1, keepdims=True))
+        n1 = jnp.maximum(m1, jnp.max(s1, axis=1, keepdims=True))
+        a0 = jnp.exp(m0 - n0)
+        a1 = jnp.exp(m1 - n1)
+        p0 = jnp.exp(s0 - n0)
+        p1 = jnp.exp(s1 - n1)
+        l0 = l0 * a0 + jnp.sum(p0, axis=1, keepdims=True)
+        l1 = l1 * a1 + jnp.sum(p1, axis=1, keepdims=True)
+        pv0 = jnp.dot(p0.astype(vb.dtype), vb, preferred_element_type=jnp.float32)
+        pv1 = jnp.dot(p1.astype(vb.dtype), vb, preferred_element_type=jnp.float32)
+        acc = acc * jnp.where(first, a0, a1) + jnp.where(first, pv0, pv1)
+        return (n0, n1, l0, l1, acc)
+
+    init = (
+        jnp.full((rows, 1), NEG, jnp.float32),
+        jnp.full((rows, 1), NEG, jnp.float32),
+        jnp.zeros((rows, 1), jnp.float32),
+        jnp.zeros((rows, 1), jnp.float32),
+        jnp.zeros((rows, width), jnp.float32),
+    )
+    s0, s1 = scores(k_ref[...])
+    carry = update(init, s0, s1, v_ref[...])
+
+    def body(b, carry):
+        keep = allowed_ref[b] > 0
+        s0, s1 = scores(kv_ref[b, 0])
+        s0 = jnp.where(keep, s0, NEG)
+        s1 = jnp.where(keep, s1, NEG)
+        return update(carry, s0, s1, kv_ref[b, 1])
+
+    m0, m1, l0, l1, acc = lax.fori_loop(0, n_blocks, body, carry)
+    o_ref[...] = (acc / jnp.where(first, l0, l1)).astype(o_ref.dtype)
 
 
-def merge_parts(first, second):
-    top_a, total_a, summed_a = first
-    top_b, total_b, summed_b = second
-    best = jnp.maximum(top_a, top_b)
-    keep_a = jnp.exp(top_a - best)
-    keep_b = jnp.exp(top_b - best)
-    merged = summed_a * keep_a.T[:, :, None] + summed_b * keep_b.T[:, :, None]
-    return (best, total_a * keep_a + total_b * keep_b, merged)
+def block_attend(allowed, query, keys, values, kv, scale):
+    n_blocks = kv.shape[0]
+    vmem = pltpu.MemorySpace.VMEM
+    return pl.pallas_call(
+        functools.partial(attn_kernel, scale=scale, n_blocks=n_blocks),
+        out_shape=jax.ShapeDtypeStruct(query.shape, jnp.bfloat16),
+        in_specs=[pl.BlockSpec(memory_space=pltpu.MemorySpace.SMEM)] + [pl.BlockSpec(memory_space=vmem)] * 4,
+        out_specs=pl.BlockSpec(memory_space=vmem),
+    )(allowed, query, keys, values, kv)
 
 
 def gather_pipe(piece, order):
@@ -88,7 +127,6 @@
     block_ids = jnp.arange(total_blocks, dtype=jnp.int32)
     batch_of = block_ids // BPM
     mine = lax.dynamic_slice_in_dim(linked, me * BPM, BPM, 0)
-    own = lax.dynamic_slice_in_dim(mine, me * BPM, BPM, 1)
     remote = mine & (batch_of != me)[None, :]
 
     near = lax.all_gather(stale_kv[None], PIPE[1], axis=0, tiled=True)
@@ -111,30 +149,17 @@
     q2, k2, v2 = project(xs[1])
 
     fresh_kv = gather_pipe(jnp.stack([k1, v1])[None], tuple(reversed(PIPE)))
-    count = fresh_kv.shape[0] * tokens
 
-    def attend(query, keys, values, piece_k, piece_v, remote):
-        query_h = query.reshape(tokens, heads, HS)
-        start_part = partial_attend(
-            query_h, keys.reshape(tokens, heads, HS), values.reshape(tokens, heads, HS), own, scale
-        )
-        fresh = partial_attend(
-            query_h,
-            piece_k.reshape(count, heads, HS),
-            piece_v.reshape(count, heads, HS),
-            remote,
-            scale,
-        )
-        best, denom_h, numer = merge_parts(start_part, fresh)
-        denom = denom_h.T
-        attn = (numer / denom[:, :, None]).reshape(tokens, width).astype(jnp.bfloat16)
+    def attend(query, keys, values, kv, remote):
+        allowed = remote[0].astype(jnp.int32)
+        attn = block_attend(allowed, query, keys, values, kv, scale)
         part = jnp.dot(attn, w_out, preferred_element_type=jnp.float32).astype(jnp.bfloat16)
         sent = lax.all_to_all(part.reshape(n_seq, tokens // n_seq, -1), SEQ, 0, 0, tiled=False)
         return jnp.sum(sent.astype(jnp.float32), axis=0).astype(jnp.bfloat16)
 
-    out_first = attend(q1, k1, v1, stale[:, 0], stale[:, 1], remote)
+    out_first = attend(q1, k1, v1, stale, remote)
     out_first, fresh_kv = lax.optimization_barrier((out_first, fresh_kv))
-    out_second = attend(q2, k2, v2, fresh_kv[:, 0], fresh_kv[:, 1], remote)
+    out_second = attend(q2, k2, v2, fresh_kv, remote)
     return (out_first, out_second)
 
 

time: 188 us -> 190 us (1.011)
  the two profiles are of different devices: /device:TPU:1 before, /device:TPU:80 now
where the time goes in v6:
time: 190 us; the launch traced here: 189 us
  waiting for transfers between devices  56.9 us (30%)
  blocking collectives  54.8 us (29%)
  Pallas kernels  31.8 us (17%)
  between operations  14.4 us (8%)
  starting transfers between devices  13.9 us (7%)
  matrix products  6.88 us (4%)
  local copies, waits for them, and re-layouts  6.31 us (3%)
  other arithmetic  3.92 us (2%)
    all_to_all x1, waiting for transfers between devices, exchange_rows(): lax.all_to_all(spread, SEQ, 1, 1, tiled=False)  34.3 us
    pallas_call x2, Pallas kernels, block_attend(): pl.pallas_call(functools.partial(attn_kernel, scale=scale, n_blocks=n_blo...  31.8 us
    all_to_all x1, blocking collectives, attend(): lax.all_to_all(part.reshape(n_seq, tokens // n_seq, -1), SEQ, 0, 0, tiled...  25.1 us
    all_to_all x1, waiting for transfers between devices, attend(): lax.all_to_all(part.reshape(n_seq, tokens // n_seq, -1), SEQ, 0, 0, tiled...  22.5 us
    all_gather x1, blocking collectives, on_device(): near = lax.all_gather(stale_kv[None], PIPE[1], axis=0, tiled=True)  16.7 us
    all_gather x1, blocking collectives, gather_pipe(): piece = lax.all_gather(piece, name, axis=0, tiled=True)  12.9 us
    all_to_all x1, starting transfers between devices, exchange_rows(): lax.all_to_all(spread, SEQ, 1, 1, tiled=False)  10.2 us
  transfers between devices with their start and end apart: 4, of which 2 were waited for; matrix products, arithmetic and copies ran while one was open for 8% of the time, Pallas kernels for 8%

profile of v6, /device:TPU:80, one launch (start us, length us, event | category | flops | bytes accessed | tf_op | source)
XLA Modules:
  0.0 188.8 jit_solution(15907997718753991451)
XLA Ops:
  7.2 0.0 copy-start
  7.2 0.0 all-gather.5.cloned.1.call-start
  7.2 16.7 %all-gather = bf16[8,128,128]{2,1,0:T(8,128)(2,1)} all-gather(bf16[2,128,128]{2,1,0:T(8,128)(2,1)} %param.12), channel_id=2, replica_groups=mesh['y'=8,'zl'=4,'zh'=2,'x'=4,'c'=2] {'zl'}, dimensions={0}, use_global_device_ids=true | all-gather | bytes 327680 | tf_op jit(solution)/shard_map/all_gather | solution.py:132
  23.9 0.8 pad_maximum_fusion
  24.7 0.0 all-gather.5.cloned.1.call-update
  24.8 1.2 broadcast_in_dim.7
  25.9 10.2 %all-to-all-start = ((bf16[2,16,8,2560]{3,2,0,1:T(8,128)(2,1)}), bf16[2,16,8,2560]{3,2,0,1:T(8,128)(2,1)}, u32[]{:S(2)}, u32[]{:S(2)}) async-start(bf16[2,16,8,2560]{3,2,0,1:T(8,128)(2,1)} %broadcast_in_dim.7), calls=%async_computation | async-start | bytes 2621440 | tf_op jit(solution)/shard_map/all_to_all | solution.py:138
  36.1 0.0 all-gather.7.cloned.1.call-start
  36.2 0.0 copy-start.1
  36.2 0.0 copy-start.4
  36.2 2.7 %copy.46 = bf16[3,2560,128]{1,2,0:T(8,128)(2,1)S(1)} copy(bf16[3,2560,128]{2,1,0:T(8,128)(2,1)} %param.13) | data formatting | bytes 3932160 | tf_op args[3]
  38.9 0.0 copy-start.2
  38.9 0.0 copy-done.1
  38.9 0.1 copy.45
  39.0 0.0 copy-done.4
  39.0 0.1 iota_compare_fusion.1
  39.1 34.3 %all-to-all-done = bf16[2,16,8,2560]{3,2,0,1:T(8,128)(2,1)} async-done(((bf16[2,16,8,2560]{3,2,0,1:T(8,128)(2,1)}), bf16[2,16,8,2560]{3,2,0,1:T(8,128)(2,1)}, u32[]{:S(2)}, u32[]{:S(2)}) %all-to-all-start) | async-done | bytes 1310752 | tf_op jit(solution)/shard_map/all_to_all | solution.py:138
  73.4 0.0 copy-start.5
  73.4 1.8 fusion.3
  75.2 0.1 copy.47
  75.4 0.1 copy.50
  75.5 0.1 copy.52
  75.6 0.0 copy-done.2
  75.7 12.9 %all-gather.1 = bf16[8,128,128]{2,1,0:T(8,128)(2,1)} all-gather(bf16[2,128,128]{2,1,0:T(8,128)(2,1)S(1)} %pad_maximum_fusion.1), channel_id=3, replica_groups=mesh['y'=8,'zl'=4,'zh'=2,'x'=4,'c'=2] {'zl'}, dimensions={0}, use_global_device_ids=true | all-gather | bytes 327680 | tf_op jit(solution)/shard_map/all_gather | solution.py:112
  88.6 0.0 all-gather.7.cloned.1.call-update
  88.6 0.2 convert_reduce_fusion
  88.9 0.0 copy-done.5
  88.9 0.2 fusion.15
  89.1 0.2 fusion.14
  89.3 0.6 fusion.18.allowed_ref
  89.8 0.1 copy.48
  90.0 0.1 copy.49
  90.1 0.1 copy.51
  90.2 0.0 copy-start.3
  90.2 1.8 fusion.2
  91.9 0.1 copy.54
  92.1 0.1 copy.55
  92.2 0.1 copy.56
  92.3 0.1 copy.57
  92.5 0.1 copy.58
  92.6 0.6 slice_bitcast_fusion.4.v_ref
  93.2 0.0 copy-done.3
  93.2 0.7 fusion.10
  93.9 0.0 all-gather.5.cloned.1.call-done.kv_ref
  93.9 15.9 %shard_map.113 = bf16[128,128]{1,0:T(8,128)(2,1)} custom-call(s32[32]{0:T(128)} %fusion.18.allowed_ref, bf16[128,128]{1,0:T(8,128)(2,1)} %get-tuple-element.17.q_ref, bf16[128,128]{1,0:T(8,128)(2,1)} %get-tuple-element.16.k_ref, bf16[128,128]{1,0:T(8,128)(2,1)} %slice_bitcast_fusion.4.v_ref, bf16[32,2,128,128]{3,2,1,0:T(8,128)(2,1)} %all-gather.5.cloned.1.call-done.kv_ref), custom_call_target="tpu_custom_call" | custom-call | tf_op jit(solution)/shard_map/pallas_call | solution.py:102
  109.8 0.0 copy-done
  109.8 1.9 %fusion = bf16[16,8,2560]{2,1,0:T(8,128)(2,1)} fusion(bf16[128,128]{1,0:T(8,128)(2,1)} %shard_map.113, bf16[128,2560]{1,0:T(8,128)(2,1)S(1)} %copy-done), kind=kOutput, calls=%fused_computation.2 | convolution fusion | flops 84213760 | bytes 1343488 | tf_op jit(solution)/shard_map/dot_general | solution.py:156
  111.7 3.6 %all-to-all-start.1 = ((bf16[16,8,2560]{2,1,0:T(8,128)(2,1)}), bf16[16,8,2560]{2,1,0:T(8,128)(2,1)S(1)}, u32[]{:S(2)}, u32[]{:S(2)}) async-start(bf16[16,8,2560]{2,1,0:T(8,128)(2,1)} %fusion), calls=%async_computation.1 | async-start | bytes 1310720 | tf_op jit(solution)/shard_map/all_to_all | solution.py:157
  115.3 0.6 fusion.13.v_ref
  115.9 22.5 %all-to-all-done.1 = bf16[16,8,2560]{2,1,0:T(8,128)(2,1)S(1)} async-done(((bf16[16,8,2560]{2,1,0:T(8,128)(2,1)}), bf16[16,8,2560]{2,1,0:T(8,128)(2,1)S(1)}, u32[]{:S(2)}, u32[]{:S(2)}) %all-to-all-start.1) | async-done | bytes 655392 | tf_op jit(solution)/shard_map/all_to_all | solution.py:157
  138.4 0.7 reduce_sum.72
  139.1 0.0 all-gather.7.cloned.1.call-done.kv_ref
  139.1 15.9 %shard_map.114 = bf16[128,128]{1,0:T(8,128)(2,1)} custom-call(s32[32]{0:T(128)} %fusion.18.allowed_ref, bf16[128,128]{1,0:T(8,128)(2,1)} %get-tuple-element.18.q_ref, bf16[128,128]{1,0:T(8,128)(2,1)} %get-tuple-element.19.k_ref, bf16[128,128]{1,0:T(8,128)(2,1)} %fusion.13.v_ref, bf16[32,2,128,128]{3,2,1,0:T(8,128)(2,1)} %all-gather.7.cloned.1.call-done.kv_ref), custom_call_target="tpu_custom_call" | custom-call | tf_op jit(solution)/shard_map/pallas_call | solution.py:102
  155.0 1.1 fusion.1
  156.1 25.1 %all_to_all.15 = bf16[16,8,2560]{2,1,0:T(8,128)(2,1)S(1)} all-to-all(bf16[16,8,2560]{2,1,0:T(8,128)(2,1)S(1)} %fusion.1), channel_id=1, replica_groups=mesh['y'=8,'zl'=4,'zh'=2,'x'=4,'c'=2] {'zh','x','c'}, dimensions={0} | all-to-all | bytes 1310720 | tf_op jit(solution)/shard_map/all_to_all | solution.py:157
  181.2 0.7 reduce_sum.75
  (17 shorter events, 0.2 us)
Async XLA Ops:
  7.2 102.6 %copy-start = (bf16[128,2560]{1,0:T(8,128)(2,1)S(1)}, bf16[128,2560]{1,0:T(8,128)(2,1)}, u32[]{:S(2)}) copy-start(bf16[128,2560]{1,0:T(8,128)(2,1)} %param.14) | copy-start | bytes 1966084
  7.2 86.7 %all-gather.5.cloned.1.call-start = ((), (), s32[]{:S(2)}) async-start(), calls=%async_computation.3 | async-start | bytes 2359296 | tf_op jit(solution)/shard_map/all_gather | solution.py:134
  25.9 47.5 %all-to-all-start = ((bf16[2,16,8,2560]{3,2,0,1:T(8,128)(2,1)}), bf16[2,16,8,2560]{3,2,0,1:T(8,128)(2,1)}, u32[]{:S(2)}, u32[]{:S(2)}) async-start(bf16[2,16,8,2560]{3,2,0,1:T(8,128)(2,1)} %broadcast_in_dim.7), calls=%async_computation | async-start | bytes 2621440 | tf_op jit(solution)/shard_map/all_to_all | solution.py:138
  36.1 103.0 %all-gather.7.cloned.1.call-start = ((), (), s32[]{:S(2)}) async-start(), calls=%async_computation.4 | async-start | bytes 2359296 | tf_op jit(solution)/shard_map/all_gather | solution.py:112
  36.2 2.7 %copy-start.1 = (s32[32,16]{0,1:T(8,128)S(1)}, s32[32,16]{0,1:T(8,128)}, u32[]{:S(2)}) copy-start(s32[32,16]{0,1:T(8,128)} %param.17) | copy-start | bytes 6148
  36.2 2.8 %copy-start.4 = (s32[32]{0:T(128)S(1)}, s32[32]{0:T(128)}, u32[]{:S(2)}) copy-start(s32[32]{0:T(128)} %param.18) | copy-start | bytes 388
  38.9 36.7 %copy-start.2 = (f32[128]{0:T(128)S(1)}, f32[128]{0:T(128)}, u32[]{:S(2)}) copy-start(f32[128]{0:T(128)} %param.16) | copy-start | bytes 1540
  73.4 15.4 %copy-start.5 = (s32[32]{0:T(128)S(1)}, s32[32]{0:T(128)}, u32[]{:S(2)}) copy-start(s32[32]{0:T(128)} %param.19) | copy-start | bytes 388
  90.2 3.0 %copy-start.3 = (f32[128]{0:T(128)S(1)}, f32[128]{0:T(128)}, u32[]{:S(2)}) copy-start(f32[128]{0:T(128)} %param.15) | copy-start | bytes 1540
  111.7 26.7 %all-to-all-start.1 = ((bf16[16,8,2560]{2,1,0:T(8,128)(2,1)}), bf16[16,8,2560]{2,1,0:T(8,128)(2,1)S(1)}, u32[]{:S(2)}, u32[]{:S(2)}) async-start(bf16[16,8,2560]{2,1,0:T(8,128)(2,1)} %fusion), calls=%async_computation.1 | async-start | bytes 1310720 | tf_op jit(solution)/shard_map/all_to_all | solution.py:157
Sparse Core Ops, SparseCore 0:
  24.9 45.1 all-gather.4
  88.8 39.8 all-gather.6

commit v7 on v6

--- a/solution.py
+++ b/solution.py
@@ -46,7 +46,7 @@
 
 
 def attn_kernel(allowed_ref, q_ref, k_ref, v_ref, kv_ref, o_ref, *, scale, n_blocks):
-    q = q_ref[...]
+    q = q_ref[...] * jnp.asarray(scale, q_ref.dtype)
     rows, width = q.shape
     lane = lax.broadcasted_iota(jnp.int32, (rows, width), 1)
     first = lane < HS
@@ -56,8 +56,8 @@
 
     def scores(kb):
         dims = (((1,), (1,)), ((), ()))
-        s0 = lax.dot_general(q0, kb, dims, preferred_element_type=jnp.float32) * scale
-        s1 = lax.dot_general(q1, kb, dims, preferred_element_type=jnp.float32) * scale
+        s0 = lax.dot_general(q0, kb, dims, preferred_element_type=jnp.float32)
+        s1 = lax.dot_general(q1, kb, dims, preferred_element_type=jnp.float32)
         return s0, s1
 
     def update(carry, s0, s1, vb):
@@ -85,12 +85,12 @@
     s0, s1 = scores(k_ref[...])
     carry = update(init, s0, s1, v_ref[...])
 
+    def visit(b, carry):
+        s0, s1 = scores(kv_ref[b, 0])
+        return update(carry, s0, s1, kv_ref[b, 1])
+
     def body(b, carry):
-        keep = allowed_ref[b] > 0
-        s0, s1 = scores(kv_ref[b, 0])
-        s0 = jnp.where(keep, s0, NEG)
-        s1 = jnp.where(keep, s1, NEG)
-        return update(carry, s0, s1, kv_ref[b, 1])
+        return lax.cond(allowed_ref[b] > 0, functools.partial(visit, b), lambda c: c, carry)
 
     m0, m1, l0, l1, acc = lax.fori_loop(0, n_blocks, body, carry)
     o_ref[...] = (acc / jnp.where(first, l0, l1)).astype(o_ref.dtype)

time: 190 us -> 180 us (0.947)
  the two profiles are of different devices: /device:TPU:80 before, /device:TPU:1 now
where the time goes in v7:
time: 180 us; the launch traced here: 179 us
  blocking collectives  62.9 us (35%)
  waiting for transfers between devices  47.2 us (26%)
  starting transfers between devices  19.6 us (11%)
  Pallas kernels  17.9 us (10%)
  between operations  14.3 us (8%)
  matrix products  6.88 us (4%)
  local copies, waits for them, and re-layouts  6.31 us (4%)
  other arithmetic  3.92 us (2%)
    all_to_all x1, blocking collectives, attend(): lax.all_to_all(part.reshape(n_seq, tokens // n_seq, -1), SEQ, 0, 0, tiled...  29.2 us
    all_to_all x1, waiting for transfers between devices, exchange_rows(): lax.all_to_all(spread, SEQ, 1, 1, tiled=False)  27.6 us
    all_to_all x1, waiting for transfers between devices, attend(): lax.all_to_all(part.reshape(n_seq, tokens // n_seq, -1), SEQ, 0, 0, tiled...  19.5 us
    pallas_call x2, Pallas kernels, block_attend(): pl.pallas_call(functools.partial(attn_kernel, scale=scale, n_blocks=n_blo...  17.9 us
    all_gather x1, blocking collectives, on_device(): near = lax.all_gather(stale_kv[None], PIPE[1], axis=0, tiled=True)  17.5 us
    all_gather x1, blocking collectives, gather_pipe(): piece = lax.all_gather(piece, name, axis=0, tiled=True)  16.2 us
    all_to_all x1, starting transfers between devices, exchange_rows(): lax.all_to_all(spread, SEQ, 1, 1, tiled=False)  12.6 us
    all_to_all x1, starting transfers between devices, attend(): lax.all_to_all(part.reshape(n_seq, tokens // n_seq, -1), SEQ, 0, 0, tiled...  7 us
  transfers between devices with their start and end apart: 4, of which 2 were waited for; matrix products, arithmetic and copies ran while one was open for 8% of the time, Pallas kernels for 5%

profile of v7, /device:TPU:1, one launch (start us, length us, event | category | flops | bytes accessed | tf_op | source)
XLA Modules:
  0.0 179.1 jit_solution(6229130718113206403)
XLA Ops:
  7.2 0.0 copy-start
  7.2 0.0 all-gather.5.cloned.1.call-start
  7.2 17.5 %all-gather = bf16[8,128,128]{2,1,0:T(8,128)(2,1)} all-gather(bf16[2,128,128]{2,1,0:T(8,128)(2,1)} %param.12), channel_id=2, replica_groups=mesh['y'=8,'zl'=4,'zh'=2,'x'=4,'c'=2] {'zl'}, dimensions={0}, use_global_device_ids=true | all-gather | bytes 327680 | tf_op jit(solution)/shard_map/all_gather | solution.py:132
  24.8 0.8 pad_maximum_fusion
  25.6 0.0 all-gather.5.cloned.1.call-update
  25.6 1.2 broadcast_in_dim.7
  26.8 12.6 %all-to-all-start = ((bf16[2,16,8,2560]{3,2,0,1:T(8,128)(2,1)}), bf16[2,16,8,2560]{3,2,0,1:T(8,128)(2,1)}, u32[]{:S(2)}, u32[]{:S(2)}) async-start(bf16[2,16,8,2560]{3,2,0,1:T(8,128)(2,1)} %broadcast_in_dim.7), calls=%async_computation | async-start | bytes 2621440 | tf_op jit(solution)/shard_map/all_to_all | solution.py:138
  39.4 0.0 all-gather.7.cloned.1.call-start
  39.4 0.0 copy-start.1
  39.4 0.0 copy-start.4
  39.4 2.7 %copy.46 = bf16[3,2560,128]{1,2,0:T(8,128)(2,1)S(1)} copy(bf16[3,2560,128]{2,1,0:T(8,128)(2,1)} %param.13) | data formatting | bytes 3932160 | tf_op args[3]
  42.1 0.0 copy-start.2
  42.1 0.0 copy-done.1
  42.1 0.1 copy.45
  42.2 0.0 copy-done.4
  42.2 0.1 iota_compare_fusion.1
  42.3 27.6 %all-to-all-done = bf16[2,16,8,2560]{3,2,0,1:T(8,128)(2,1)} async-done(((bf16[2,16,8,2560]{3,2,0,1:T(8,128)(2,1)}), bf16[2,16,8,2560]{3,2,0,1:T(8,128)(2,1)}, u32[]{:S(2)}, u32[]{:S(2)}) %all-to-all-start) | async-done | bytes 1310752 | tf_op jit(solution)/shard_map/all_to_all | solution.py:138
  69.9 0.0 copy-start.5
  69.9 1.8 fusion.3
  71.7 0.1 copy.47
  71.9 0.1 copy.50
  72.0 0.1 copy.52
  72.1 0.0 copy-done.2
  72.2 16.2 %all-gather.1 = bf16[8,128,128]{2,1,0:T(8,128)(2,1)} all-gather(bf16[2,128,128]{2,1,0:T(8,128)(2,1)S(1)} %pad_maximum_fusion.1), channel_id=3, replica_groups=mesh['y'=8,'zl'=4,'zh'=2,'x'=4,'c'=2] {'zl'}, dimensions={0}, use_global_device_ids=true | all-gather | bytes 327680 | tf_op jit(solution)/shard_map/all_gather | solution.py:112
  88.3 0.0 all-gather.7.cloned.1.call-update
  88.4 0.2 convert_reduce_fusion
  88.6 0.0 copy-done.5
  88.6 0.2 fusion.15
  88.8 0.2 fusion.14
  89.0 0.6 fusion.18.allowed_ref
  89.5 0.1 copy.48
  89.7 0.1 copy.49
  89.8 0.1 copy.51
  89.9 0.0 copy-start.3
  89.9 1.8 fusion.2
  91.7 0.1 copy.54
  91.8 0.1 copy.55
  92.0 0.1 copy.56
  92.1 0.1 copy.57
  92.2 0.1 copy.58
  92.3 0.6 slice_bitcast_fusion.4.v_ref
  92.9 0.0 copy-done.3
  92.9 0.7 fusion.10
  93.6 0.0 all-gather.5.cloned.1.call-done.kv_ref
  93.6 9.0 %shard_map.113 = bf16[128,128]{1,0:T(8,128)(2,1)} custom-call(s32[32]{0:T(128)} %fusion.18.allowed_ref, bf16[128,128]{1,0:T(8,128)(2,1)} %get-tuple-element.17.q_ref, bf16[128,128]{1,0:T(8,128)(2,1)} %get-tuple-element.16.k_ref, bf16[128,128]{1,0:T(8,128)(2,1)} %slice_bitcast_fusion.4.v_ref, bf16[32,2,128,128]{3,2,1,0:T(8,128)(2,1)} %all-gather.5.cloned.1.call-done.kv_ref), custom_call_target="tpu_custom_call" | custom-call | tf_op jit(solution)/shard_map/pallas_call | solution.py:102
  102.6 0.0 copy-done
  102.6 1.9 %fusion = bf16[16,8,2560]{2,1,0:T(8,128)(2,1)} fusion(bf16[128,128]{1,0:T(8,128)(2,1)} %shard_map.113, bf16[128,2560]{1,0:T(8,128)(2,1)S(1)} %copy-done), kind=kOutput, calls=%fused_computation.2 | convolution fusion | flops 84213760 | bytes 1343488 | tf_op jit(solution)/shard_map/dot_general | solution.py:156
  104.5 7.0 %all-to-all-start.1 = ((bf16[16,8,2560]{2,1,0:T(8,128)(2,1)}), bf16[16,8,2560]{2,1,0:T(8,128)(2,1)S(1)}, u32[]{:S(2)}, u32[]{:S(2)}) async-start(bf16[16,8,2560]{2,1,0:T(8,128)(2,1)} %fusion), calls=%async_computation.1 | async-start | bytes 1310720 | tf_op jit(solution)/shard_map/all_to_all | solution.py:157
  111.5 0.6 fusion.13.v_ref
  112.1 19.5 %all-to-all-done.1 = bf16[16,8,2560]{2,1,0:T(8,128)(2,1)S(1)} async-done(((bf16[16,8,2560]{2,1,0:T(8,128)(2,1)}), bf16[16,8,2560]{2,1,0:T(8,128)(2,1)S(1)}, u32[]{:S(2)}, u32[]{:S(2)}) %all-to-all-start.1) | async-done | bytes 655392 | tf_op jit(solution)/shard_map/all_to_all | solution.py:157
  131.6 0.7 reduce_sum.72
  132.3 0.0 all-gather.7.cloned.1.call-done.kv_ref
  132.3 9.0 %shard_map.114 = bf16[128,128]{1,0:T(8,128)(2,1)} custom-call(s32[32]{0:T(128)} %fusion.18.allowed_ref, bf16[128,128]{1,0:T(8,128)(2,1)} %get-tuple-element.18.q_ref, bf16[128,128]{1,0:T(8,128)(2,1)} %get-tuple-element.19.k_ref, bf16[128,128]{1,0:T(8,128)(2,1)} %fusion.13.v_ref, bf16[32,2,128,128]{3,2,1,0:T(8,128)(2,1)} %all-gather.7.cloned.1.call-done.kv_ref), custom_call_target="tpu_custom_call" | custom-call | tf_op jit(solution)/shard_map/pallas_call | solution.py:102
  141.3 1.1 fusion.1
  142.4 29.2 %all_to_all.15 = bf16[16,8,2560]{2,1,0:T(8,128)(2,1)S(1)} all-to-all(bf16[16,8,2560]{2,1,0:T(8,128)(2,1)S(1)} %fusion.1), channel_id=1, replica_groups=mesh['y'=8,'zl'=4,'zh'=2,'x'=4,'c'=2] {'zh','x','c'}, dimensions={0} | all-to-all | bytes 1310720 | tf_op jit(solution)/shard_map/all_to_all | solution.py:157
  171.6 0.7 reduce_sum.75
  (17 shorter events, 0.2 us)
Async XLA Ops:
  7.2 95.4 %copy-start = (bf16[128,2560]{1,0:T(8,128)(2,1)S(1)}, bf16[128,2560]{1,0:T(8,128)(2,1)}, u32[]{:S(2)}) copy-start(bf16[128,2560]{1,0:T(8,128)(2,1)} %param.14) | copy-start | bytes 1966084
  7.2 86.4 %all-gather.5.cloned.1.call-start = ((), (), s32[]{:S(2)}) async-start(), calls=%async_computation.3 | async-start | bytes 2359296 | tf_op jit(solution)/shard_map/all_gather | solution.py:134
  26.8 43.1 %all-to-all-start = ((bf16[2,16,8,2560]{3,2,0,1:T(8,128)(2,1)}), bf16[2,16,8,2560]{3,2,0,1:T(8,128)(2,1)}, u32[]{:S(2)}, u32[]{:S(2)}) async-start(bf16[2,16,8,2560]{3,2,0,1:T(8,128)(2,1)} %broadcast_in_dim.7), calls=%async_computation | async-start | bytes 2621440 | tf_op jit(solution)/shard_map/all_to_all | solution.py:138
  39.4 93.0 %all-gather.7.cloned.1.call-start = ((), (), s32[]{:S(2)}) async-start(), calls=%async_computation.4 | async-start | bytes 2359296 | tf_op jit(solution)/shard_map/all_gather | solution.py:112
  39.4 2.7 %copy-start.1 = (s32[32,16]{0,1:T(8,128)S(1)}, s32[32,16]{0,1:T(8,128)}, u32[]{:S(2)}) copy-start(s32[32,16]{0,1:T(8,128)} %param.17) | copy-start | bytes 6148
  39.4 2.8 %copy-start.4 = (s32[32]{0:T(128)S(1)}, s32[32]{0:T(128)}, u32[]{:S(2)}) copy-start(s32[32]{0:T(128)} %param.18) | copy-start | bytes 388
  42.1 30.0 %copy-start.2 = (f32[128]{0:T(128)S(1)}, f32[128]{0:T(128)}, u32[]{:S(2)}) copy-start(f32[128]{0:T(128)} %param.16) | copy-start | bytes 1540
  69.9 18.7 %copy-start.5 = (s32[32]{0:T(128)S(1)}, s32[32]{0:T(128)}, u32[]{:S(2)}) copy-start(s32[32]{0:T(128)} %param.19) | copy-start | bytes 388
  89.9 3.0 %copy-start.3 = (f32[128]{0:T(128)S(1)}, f32[128]{0:T(128)}, u32[]{:S(2)}) copy-start(f32[128]{0:T(128)} %param.15) | copy-start | bytes 1540
  104.5 27.1 %all-to-all-start.1 = ((bf16[16,8,2560]{2,1,0:T(8,128)(2,1)}), bf16[16,8,2560]{2,1,0:T(8,128)(2,1)S(1)}, u32[]{:S(2)}, u32[]{:S(2)}) async-start(bf16[16,8,2560]{2,1,0:T(8,128)(2,1)} %fusion), calls=%async_computation.1 | async-start | bytes 1310720 | tf_op jit(solution)/shard_map/all_to_all | solution.py:157
Sparse Core Ops, SparseCore 0:
  25.7 42.9 all-gather.4
  88.5 38.7 all-gather.6

commit v8 on v7

--- a/solution.py
+++ b/solution.py
@@ -49,51 +49,46 @@
     q = q_ref[...] * jnp.asarray(scale, q_ref.dtype)
     rows, width = q.shape
     lane = lax.broadcasted_iota(jnp.int32, (rows, width), 1)
-    first = lane < HS
     zero = jnp.zeros_like(q)
-    q0 = jnp.where(first, q, zero)
-    q1 = jnp.where(first, zero, q)
+    qt0 = jnp.where(lane < HS, q, zero).T
+    qt1 = jnp.where(lane < HS, zero, q).T
+    first = lax.broadcasted_iota(jnp.int32, (width, rows), 0) < HS
 
-    def scores(kb):
-        dims = (((1,), (1,)), ((), ()))
-        s0 = lax.dot_general(q0, kb, dims, preferred_element_type=jnp.float32)
-        s1 = lax.dot_general(q1, kb, dims, preferred_element_type=jnp.float32)
-        return s0, s1
-
-    def update(carry, s0, s1, vb):
+    def update(carry, kb, vb):
         m0, m1, l0, l1, acc = carry
-        n0 = jnp.maximum(m0, jnp.max(s0, axis=1, keepdims=True))
-        n1 = jnp.maximum(m1, jnp.max(s1, axis=1, keepdims=True))
+        s0 = jnp.dot(kb, qt0, preferred_element_type=jnp.float32)
+        s1 = jnp.dot(kb, qt1, preferred_element_type=jnp.float32)
+        n0 = jnp.maximum(m0, jnp.max(s0, axis=0, keepdims=True))
+        n1 = jnp.maximum(m1, jnp.max(s1, axis=0, keepdims=True))
         a0 = jnp.exp(m0 - n0)
         a1 = jnp.exp(m1 - n1)
         p0 = jnp.exp(s0 - n0)
         p1 = jnp.exp(s1 - n1)
-        l0 = l0 * a0 + jnp.sum(p0, axis=1, keepdims=True)
-        l1 = l1 * a1 + jnp.sum(p1, axis=1, keepdims=True)
-        pv0 = jnp.dot(p0.astype(vb.dtype), vb, preferred_element_type=jnp.float32)
-        pv1 = jnp.dot(p1.astype(vb.dtype), vb, preferred_element_type=jnp.float32)
+        l0 = l0 * a0 + jnp.sum(p0, axis=0, keepdims=True)
+        l1 = l1 * a1 + jnp.sum(p1, axis=0, keepdims=True)
+        vt = vb.T
+        pv0 = jnp.dot(vt, p0.astype(vb.dtype), preferred_element_type=jnp.float32)
+        pv1 = jnp.dot(vt, p1.astype(vb.dtype), preferred_element_type=jnp.float32)
         acc = acc * jnp.where(first, a0, a1) + jnp.where(first, pv0, pv1)
         return (n0, n1, l0, l1, acc)
 
     init = (
-        jnp.full((rows, 1), NEG, jnp.float32),
-        jnp.full((rows, 1), NEG, jnp.float32),
-        jnp.zeros((rows, 1), jnp.float32),
-        jnp.zeros((rows, 1), jnp.float32),
-        jnp.zeros((rows, width), jnp.float32),
+        jnp.full((1, rows), NEG, jnp.float32),
+        jnp.full((1, rows), NEG, jnp.float32),
+        jnp.zeros((1, rows), jnp.float32),
+        jnp.zeros((1, rows), jnp.float32),
+        jnp.zeros((width, rows), jnp.float32),
     )
-    s0, s1 = scores(k_ref[...])
-    carry = update(init, s0, s1, v_ref[...])
+    carry = update(init, k_ref[...], v_ref[...])
 
     def visit(b, carry):
-        s0, s1 = scores(kv_ref[b, 0])
-        return update(carry, s0, s1, kv_ref[b, 1])
+        return update(carry, kv_ref[b, 0], kv_ref[b, 1])
 
     def body(b, carry):
         return lax.cond(allowed_ref[b] > 0, functools.partial(visit, b), lambda c: c, carry)
 
     m0, m1, l0, l1, acc = lax.fori_loop(0, n_blocks, body, carry)
-    o_ref[...] = (acc / jnp.where(first, l0, l1)).astype(o_ref.dtype)
+    o_ref[...] = (acc / jnp.where(first, l0, l1)).T.astype(o_ref.dtype)
 
 
 def block_attend(allowed, query, keys, values, kv, scale):

time: 180 us -> 178 us (0.989)
  Pallas kernels: 17.9 us -> 12.6 us
  blocking collectives: 62.9 us -> 66.2 us
    pallas_call x2, Pallas kernels: 17.9 us -> 12.6 us  [block_attend(): pl.pallas_call(functools.partial(attn_kernel, scale=scale, n_blocks=n_blo...]
    all_to_all x1, blocking collectives: 29.2 us -> 32.4 us  [attend(): lax.all_to_all(part.reshape(n_seq, tokens // n_seq, -1), SEQ, 0, 0, tiled...]
  transfers between devices with their start and end apart: 4 -> 4, of which waited for: 2 -> 2; matrix products, arithmetic and copies ran while one was open for 8% -> 8% of each run, Pallas kernels for 5% -> 4%
where the time goes in v8:
time: 178 us; the launch traced here: 177 us
  blocking collectives  66.2 us (37%)
  waiting for transfers between devices  46.9 us (26%)
  starting transfers between devices  19.6 us (11%)
  between operations  14.3 us (8%)
  Pallas kernels  12.6 us (7%)
  matrix products  6.88 us (4%)
  local copies, waits for them, and re-layouts  6.31 us (4%)
  other arithmetic  3.92 us (2%)
    all_to_all x1, blocking collectives, attend(): lax.all_to_all(part.reshape(n_seq, tokens // n_seq, -1), SEQ, 0, 0, tiled...  32.4 us
    all_to_all x1, waiting for transfers between devices, exchange_rows(): lax.all_to_all(spread, SEQ, 1, 1, tiled=False)  27.6 us
    all_to_all x1, waiting for transfers between devices, attend(): lax.all_to_all(part.reshape(n_seq, tokens // n_seq, -1), SEQ, 0, 0, tiled...  19.2 us
    all_gather x1, blocking collectives, on_device(): near = lax.all_gather(stale_kv[None], PIPE[1], axis=0, tiled=True)  17.5 us
    all_gather x1, blocking collectives, gather_pipe(): piece = lax.all_gather(piece, name, axis=0, tiled=True)  16.2 us
    pallas_call x2, Pallas kernels, block_attend(): pl.pallas_call(functools.partial(attn_kernel, scale=scale, n_blocks=n_blo...  12.6 us
    all_to_all x1, starting transfers between devices, exchange_rows(): lax.all_to_all(spread, SEQ, 1, 1, tiled=False)  12.6 us
    all_to_all x1, starting transfers between devices, attend(): lax.all_to_all(part.reshape(n_seq, tokens // n_seq, -1), SEQ, 0, 0, tiled...  7 us
  transfers between devices with their start and end apart: 4, of which 2 were waited for; matrix products, arithmetic and copies ran while one was open for 8% of the time, Pallas kernels for 4%

profile of v8, /device:TPU:1, one launch (start us, length us, event | category | flops | bytes accessed | tf_op | source)
XLA Modules:
  0.0 176.7 jit_solution(16219307234798224610)
XLA Ops:
  7.2 0.0 copy-start
  7.2 0.0 all-gather.5.cloned.1.call-start
  7.2 17.5 %all-gather = bf16[8,128,128]{2,1,0:T(8,128)(2,1)} all-gather(bf16[2,128,128]{2,1,0:T(8,128)(2,1)} %param.12), channel_id=2, replica_groups=mesh['y'=8,'zl'=4,'zh'=2,'x'=4,'c'=2] {'zl'}, dimensions={0}, use_global_device_ids=true | all-gather | bytes 327680 | tf_op jit(solution)/shard_map/all_gather | solution.py:127
  24.8 0.8 pad_maximum_fusion
  25.6 0.0 all-gather.5.cloned.1.call-update
  25.6 1.2 broadcast_in_dim.7
  26.8 12.6 %all-to-all-start = ((bf16[2,16,8,2560]{3,2,0,1:T(8,128)(2,1)}), bf16[2,16,8,2560]{3,2,0,1:T(8,128)(2,1)}, u32[]{:S(2)}, u32[]{:S(2)}) async-start(bf16[2,16,8,2560]{3,2,0,1:T(8,128)(2,1)} %broadcast_in_dim.7), calls=%async_computation | async-start | bytes 2621440 | tf_op jit(solution)/shard_map/all_to_all | solution.py:133
  39.4 0.0 all-gather.7.cloned.1.call-start
  39.4 0.0 copy-start.1
  39.4 0.0 copy-start.4
  39.4 2.7 %copy.46 = bf16[3,2560,128]{1,2,0:T(8,128)(2,1)S(1)} copy(bf16[3,2560,128]{2,1,0:T(8,128)(2,1)} %param.13) | data formatting | bytes 3932160 | tf_op args[3]
  42.1 0.0 copy-start.2
  42.1 0.0 copy-done.1
  42.1 0.1 copy.45
  42.2 0.0 copy-done.4
  42.2 0.1 iota_compare_fusion.1
  42.3 27.6 %all-to-all-done = bf16[2,16,8,2560]{3,2,0,1:T(8,128)(2,1)} async-done(((bf16[2,16,8,2560]{3,2,0,1:T(8,128)(2,1)}), bf16[2,16,8,2560]{3,2,0,1:T(8,128)(2,1)}, u32[]{:S(2)}, u32[]{:S(2)}) %all-to-all-start) | async-done | bytes 1310752 | tf_op jit(solution)/shard_map/all_to_all | solution.py:133
  69.9 0.0 copy-start.5
  69.9 1.8 fusion.3
  71.7 0.1 copy.47
  71.9 0.1 copy.50
  72.0 0.1 copy.52
  72.1 0.0 copy-done.2
  72.2 16.2 %all-gather.1 = bf16[8,128,128]{2,1,0:T(8,128)(2,1)} all-gather(bf16[2,128,128]{2,1,0:T(8,128)(2,1)S(1)} %pad_maximum_fusion.1), channel_id=3, replica_groups=mesh['y'=8,'zl'=4,'zh'=2,'x'=4,'c'=2] {'zl'}, dimensions={0}, use_global_device_ids=true | all-gather | bytes 327680 | tf_op jit(solution)/shard_map/all_gather | solution.py:107
  88.3 0.0 all-gather.7.cloned.1.call-update
  88.4 0.2 convert_reduce_fusion
  88.6 0.0 copy-done.5
  88.6 0.2 fusion.15
  88.8 0.2 fusion.14
  89.0 0.6 fusion.18.allowed_ref
  89.5 0.1 copy.48
  89.7 0.1 copy.49
  89.8 0.1 copy.51
  89.9 0.0 copy-start.3
  89.9 1.8 fusion.2
  91.7 0.1 copy.54
  91.8 0.1 copy.55
  92.0 0.1 copy.56
  92.1 0.1 copy.57
  92.2 0.1 copy.58
  92.3 0.6 slice_bitcast_fusion.4.v_ref
  92.9 0.0 copy-done.3
  92.9 0.7 fusion.10
  93.6 0.0 all-gather.5.cloned.1.call-done.kv_ref
  93.6 6.3 %shard_map.113 = bf16[128,128]{1,0:T(8,128)(2,1)} custom-call(s32[32]{0:T(128)} %fusion.18.allowed_ref, bf16[128,128]{1,0:T(8,128)(2,1)} %get-tuple-element.17.q_ref, bf16[128,128]{1,0:T(8,128)(2,1)} %get-tuple-element.16.k_ref, bf16[128,128]{1,0:T(8,128)(2,1)} %slice_bitcast_fusion.4.v_ref, bf16[32,2,128,128]{3,2,1,0:T(8,128)(2,1)} %all-gather.5.cloned.1.call-done.kv_ref), custom_call_target="tpu_custom_call" | custom-call | tf_op jit(solution)/shard_map/pallas_call | solution.py:97
  99.9 0.0 copy-done
  99.9 1.9 %fusion = bf16[16,8,2560]{2,1,0:T(8,128)(2,1)} fusion(bf16[128,128]{1,0:T(8,128)(2,1)} %shard_map.113, bf16[128,2560]{1,0:T(8,128)(2,1)S(1)} %copy-done), kind=kOutput, calls=%fused_computation.2 | convolution fusion | flops 84213760 | bytes 1343488 | tf_op jit(solution)/shard_map/dot_general | solution.py:151
  101.8 7.0 %all-to-all-start.1 = ((bf16[16,8,2560]{2,1,0:T(8,128)(2,1)}), bf16[16,8,2560]{2,1,0:T(8,128)(2,1)S(1)}, u32[]{:S(2)}, u32[]{:S(2)}) async-start(bf16[16,8,2560]{2,1,0:T(8,128)(2,1)} %fusion), calls=%async_computation.1 | async-start | bytes 1310720 | tf_op jit(solution)/shard_map/all_to_all | solution.py:152
  108.8 0.6 fusion.13.v_ref
  109.4 19.2 %all-to-all-done.1 = bf16[16,8,2560]{2,1,0:T(8,128)(2,1)S(1)} async-done(((bf16[16,8,2560]{2,1,0:T(8,128)(2,1)}), bf16[16,8,2560]{2,1,0:T(8,128)(2,1)S(1)}, u32[]{:S(2)}, u32[]{:S(2)}) %all-to-all-start.1) | async-done | bytes 655392 | tf_op jit(solution)/shard_map/all_to_all | solution.py:152
  128.6 0.7 reduce_sum.72
  129.3 0.0 all-gather.7.cloned.1.call-done.kv_ref
  129.3 6.3 %shard_map.114 = bf16[128,128]{1,0:T(8,128)(2,1)} custom-call(s32[32]{0:T(128)} %fusion.18.allowed_ref, bf16[128,128]{1,0:T(8,128)(2,1)} %get-tuple-element.18.q_ref, bf16[128,128]{1,0:T(8,128)(2,1)} %get-tuple-element.19.k_ref, bf16[128,128]{1,0:T(8,128)(2,1)} %fusion.13.v_ref, bf16[32,2,128,128]{3,2,1,0:T(8,128)(2,1)} %all-gather.7.cloned.1.call-done.kv_ref), custom_call_target="tpu_custom_call" | custom-call | tf_op jit(solution)/shard_map/pallas_call | solution.py:97
  135.6 1.1 fusion.1
  136.7 32.4 %all_to_all.15 = bf16[16,8,2560]{2,1,0:T(8,128)(2,1)S(1)} all-to-all(bf16[16,8,2560]{2,1,0:T(8,128)(2,1)S(1)} %fusion.1), channel_id=1, replica_groups=mesh['y'=8,'zl'=4,'zh'=2,'x'=4,'c'=2] {'zh','x','c'}, dimensions={0} | all-to-all | bytes 1310720 | tf_op jit(solution)/shard_map/all_to_all | solution.py:152
  169.2 0.7 reduce_sum.75
  (17 shorter events, 0.2 us)
Async XLA Ops:
  7.2 92.7 %copy-start = (bf16[128,2560]{1,0:T(8,128)(2,1)S(1)}, bf16[128,2560]{1,0:T(8,128)(2,1)}, u32[]{:S(2)}) copy-start(bf16[128,2560]{1,0:T(8,128)(2,1)} %param.14) | copy-start | bytes 1966084
  7.2 86.4 %all-gather.5.cloned.1.call-start = ((), (), s32[]{:S(2)}) async-start(), calls=%async_computation.3 | async-start | bytes 2359296 | tf_op jit(solution)/shard_map/all_gather | solution.py:129
  26.8 43.1 %all-to-all-start = ((bf16[2,16,8,2560]{3,2,0,1:T(8,128)(2,1)}), bf16[2,16,8,2560]{3,2,0,1:T(8,128)(2,1)}, u32[]{:S(2)}, u32[]{:S(2)}) async-start(bf16[2,16,8,2560]{3,2,0,1:T(8,128)(2,1)} %broadcast_in_dim.7), calls=%async_computation | async-start | bytes 2621440 | tf_op jit(solution)/shard_map/all_to_all | solution.py:133
  39.4 90.0 %all-gather.7.cloned.1.call-start = ((), (), s32[]{:S(2)}) async-start(), calls=%async_computation.4 | async-start | bytes 2359296 | tf_op jit(solution)/shard_map/all_gather | solution.py:107
  39.4 2.7 %copy-start.1 = (s32[32,16]{0,1:T(8,128)S(1)}, s32[32,16]{0,1:T(8,128)}, u32[]{:S(2)}) copy-start(s32[32,16]{0,1:T(8,128)} %param.17) | copy-start | bytes 6148
  39.4 2.8 %copy-start.4 = (s32[32]{0:T(128)S(1)}, s32[32]{0:T(128)}, u32[]{:S(2)}) copy-start(s32[32]{0:T(128)} %param.18) | copy-start | bytes 388
  42.1 30.0 %copy-start.2 = (f32[128]{0:T(128)S(1)}, f32[128]{0:T(128)}, u32[]{:S(2)}) copy-start(f32[128]{0:T(128)} %param.16) | copy-start | bytes 1540
  69.9 18.7 %copy-start.5 = (s32[32]{0:T(128)S(1)}, s32[32]{0:T(128)}, u32[]{:S(2)}) copy-start(s32[32]{0:T(128)} %param.19) | copy-start | bytes 388
  89.9 3.0 %copy-start.3 = (f32[128]{0:T(128)S(1)}, f32[128]{0:T(128)}, u32[]{:S(2)}) copy-start(f32[128]{0:T(128)} %param.15) | copy-start | bytes 1540
  101.8 26.8 %all-to-all-start.1 = ((bf16[16,8,2560]{2,1,0:T(8,128)(2,1)}), bf16[16,8,2560]{2,1,0:T(8,128)(2,1)S(1)}, u32[]{:S(2)}, u32[]{:S(2)}) async-start(bf16[16,8,2560]{2,1,0:T(8,128)(2,1)} %fusion), calls=%async_computation.1 | async-start | bytes 1310720 | tf_op jit(solution)/shard_map/all_to_all | solution.py:152
Sparse Core Ops, SparseCore 0:
  25.7 42.9 all-gather.4
  88.5 38.7 all-gather.6

commit v9 on v8

--- a/solution.py
+++ b/solution.py
@@ -102,12 +102,6 @@
     )(allowed, query, keys, values, kv)
 
 
-def gather_pipe(piece, order):
-    for name in order:
-        piece = lax.all_gather(piece, name, axis=0, tiled=True)
-    return piece
-
-
 def on_device(
     x_first, x_second, stale_kv, w_qkv, w_out, q_gain, k_gain, layout, counts, slot_block
 ):
@@ -125,7 +119,7 @@
     remote = mine & (batch_of != me)[None, :]
 
     near = lax.all_gather(stale_kv[None], PIPE[1], axis=0, tiled=True)
-    pair, near = lax.optimization_barrier((jnp.stack([x_first, x_second]), near))
+    first_rows, near = lax.optimization_barrier((x_first, near))
     stale = lax.all_gather(near, PIPE[0], axis=0, tiled=True)
 
     def exchange_rows(x):
@@ -139,11 +133,12 @@
         values = raw[2].astype(jnp.bfloat16)
         return (query, keys, values)
 
-    xs = exchange_rows(pair)
-    q1, k1, v1 = project(xs[0])
-    q2, k2, v2 = project(xs[1])
+    q1, k1, v1 = project(exchange_rows(first_rows[None])[0])
 
-    fresh_kv = gather_pipe(jnp.stack([k1, v1])[None], tuple(reversed(PIPE)))
+    near_fresh = lax.all_gather(jnp.stack([k1, v1])[None], PIPE[1], axis=0, tiled=True)
+    second_rows, near_fresh = lax.optimization_barrier((x_second, near_fresh))
+    fresh_kv = lax.all_gather(near_fresh, PIPE[0], axis=0, tiled=True)
+    q2, k2, v2 = project(exchange_rows(second_rows[None])[0])
 
     def attend(query, keys, values, kv, remote):
         allowed = remote[0].astype(jnp.int32)

time: 178 us -> 186 us (1.045)
  the two profiles are of different devices: /device:TPU:1 before, /device:TPU:120 now
where the time goes in v9:
time: 186 us; the launch traced here: 185 us
  blocking collectives  55.6 us (30%)
  waiting for transfers between devices  55.4 us (30%)
  starting transfers between devices  17.4 us (9%)
  local copies, waits for them, and re-layouts  14.4 us (8%)
  between operations  14.3 us (8%)
  Pallas kernels  14 us (8%)
  matrix products  7.37 us (4%)
  other arithmetic  6.74 us (4%)
    all_to_all x2, waiting for transfers between devices, exchange_rows(): lax.all_to_all(spread, SEQ, 1, 1, tiled=False)  32.9 us
    all_to_all x1, blocking collectives, attend(): lax.all_to_all(part.reshape(n_seq, tokens // n_seq, -1), SEQ, 0, 0, tiled...  25.6 us
    all_to_all x1, waiting for transfers between devices, attend(): lax.all_to_all(part.reshape(n_seq, tokens // n_seq, -1), SEQ, 0, 0, tiled...  22.5 us
    all_gather x1, blocking collectives, on_device(): near = lax.all_gather(stale_kv[None], PIPE[1], axis=0, tiled=True)  16.7 us
    pallas_call x2, Pallas kernels, block_attend(): pl.pallas_call(functools.partial(attn_kernel, scale=scale, n_blocks=n_blo...  14 us
    all_to_all x2, starting transfers between devices, exchange_rows(): lax.all_to_all(spread, SEQ, 1, 1, tiled=False)  13.7 us
    all_gather x1, blocking collectives, on_device(): lax.all_gather(jnp.stack([k1, v1])[None], PIPE[1], axis=0, tiled=True)  13.3 us
  transfers between devices with their start and end apart: 5, of which 3 were waited for; matrix products, arithmetic and copies ran while one was open for 14% of the time, Pallas kernels for 4%

profile of v9, /device:TPU:120, one launch (start us, length us, event | category | flops | bytes accessed | tf_op | source)
XLA Modules:
  0.0 185.2 jit_solution(16585586463556223003)
XLA Ops:
  7.2 0.0 copy-start
  7.2 0.0 all-gather.5.cloned.1.call-start
  7.2 16.7 %all-gather = bf16[8,128,128]{2,1,0:T(8,128)(2,1)} all-gather(bf16[2,128,128]{2,1,0:T(8,128)(2,1)} %param.12), channel_id=2, replica_groups=mesh['y'=8,'zl'=4,'zh'=2,'x'=4,'c'=2] {'zl'}, dimensions={0}, use_global_device_ids=true | all-gather | bytes 327680 | tf_op jit(solution)/shard_map/all_gather | solution.py:121
  23.9 0.0 all-gather.5.cloned.1.call-update
  23.9 1.7 broadcast_in_dim.9
  25.6 10.2 %all-to-all-start = ((bf16[1,16,8,2560]{3,2,0,1:T(8,128)(2,1)}), bf16[1,16,8,2560]{3,2,0,1:T(8,128)(2,1)S(1)}, u32[]{:S(2)}, u32[]{:S(2)}) async-start(bf16[1,16,8,2560]{3,2,0,1:T(8,128)(2,1)} %broadcast_in_dim.9), calls=%async_computation | async-start | bytes 1310720 | tf_op jit(solution)/shard_map/all_to_all | solution.py:127
  35.8 2.7 %copy.46 = bf16[3,2560,128]{1,2,0:T(8,128)(2,1)S(1)} copy(bf16[3,2560,128]{2,1,0:T(8,128)(2,1)} %param.13) | data formatting | bytes 3932160 | tf_op args[3]
  38.5 0.0 copy-start.3
  38.5 20.5 %all-to-all-done = bf16[1,16,8,2560]{3,2,0,1:T(8,128)(2,1)S(1)} async-done(((bf16[1,16,8,2560]{3,2,0,1:T(8,128)(2,1)}), bf16[1,16,8,2560]{3,2,0,1:T(8,128)(2,1)S(1)}, u32[]{:S(2)}, u32[]{:S(2)}) %all-to-all-start) | async-done | bytes 655392 | tf_op jit(solution)/shard_map/all_to_all | solution.py:127
  58.9 0.0 copy-start.2
  58.9 1.4 fusion.4
  60.3 0.0 copy-start.6
  60.3 1.1 copy.47
  61.4 0.1 copy.50
  61.5 0.1 copy.52
  61.6 0.0 copy-done.3
  61.7 0.6 multiply_convert_fusion
  62.3 13.3 %all-gather.1 = bf16[8,128,128]{2,1,0:T(8,128)(2,1)} all-gather(bf16[2,128,128]{2,1,0:T(8,128)(2,1)S(1)} %pad_maximum_fusion), channel_id=3, replica_groups=mesh['y'=8,'zl'=4,'zh'=2,'x'=4,'c'=2] {'zl'}, dimensions={0}, use_global_device_ids=true | all-gather | bytes 327680 | tf_op jit(solution)/shard_map/all_gather | solution.py:138
  75.5 0.0 copy-done.2
  75.5 0.9 broadcast_in_dim.11
  76.4 3.6 %all-to-all-start.2 = ((bf16[1,16,8,2560]{3,2,0,1:T(8,128)(2,1)}), bf16[1,16,8,2560]{3,2,0,1:T(8,128)(2,1)S(1)}, u32[]{:S(2)}, u32[]{:S(2)}) async-start(bf16[1,16,8,2560]{3,2,0,1:T(8,128)(2,1)} %broadcast_in_dim.11), calls=%async_computation.2 | async-start | bytes 1310720 | tf_op jit(solution)/shard_map/all_to_all | solution.py:127
  80.0 0.0 all-gather.7.cloned.1.call-start
  80.1 0.0 copy-done.6
  80.1 0.7 iota_compare_fusion.1
  80.8 0.8 copy.45
  81.5 0.0 all-gather.7.cloned.1.call-update
  81.6 0.9 convert_reduce_fusion
  82.5 0.8 fusion.17
  83.3 0.9 fusion.16
  84.2 0.6 fusion.20.allowed_ref
  84.8 1.6 copy.48
  86.4 0.9 reduce_sum.70
  87.2 0.6 mul.128
  87.9 1.6 copy.49
  89.4 0.7 copy.51
  90.1 0.6 slice_bitcast_fusion.v_ref
  90.8 0.0 copy-start.1
  90.8 0.0 copy-start.4
  90.8 0.0 copy-start.5
  90.8 12.4 %all-to-all-done.2 = bf16[1,16,8,2560]{3,2,0,1:T(8,128)(2,1)S(1)} async-done(((bf16[1,16,8,2560]{3,2,0,1:T(8,128)(2,1)}), bf16[1,16,8,2560]{3,2,0,1:T(8,128)(2,1)S(1)}, u32[]{:S(2)}, u32[]{:S(2)}) %all-to-all-start.2) | async-done | bytes 655392 | tf_op jit(solution)/shard_map/all_to_all | solution.py:127
  103.2 1.3 fusion.2
  104.5 1.1 copy.54
  105.6 0.1 copy.55
  105.7 0.1 copy.56
  105.8 0.1 copy.57
  106.0 0.1 copy.58
  106.1 0.0 copy-done.1
  106.1 0.0 copy-done.4
  106.1 0.0 copy-done.5
  106.1 1.5 fusion.12
  107.6 0.0 all-gather.5.cloned.1.call-done.kv_ref
  107.6 7.0 %shard_map.113 = bf16[128,128]{1,0:T(8,128)(2,1)} custom-call(s32[32]{0:T(128)} %fusion.20.allowed_ref, bf16[128,128]{1,0:T(8,128)(2,1)} %get-tuple-element.21.q_ref, bf16[128,128]{1,0:T(8,128)(2,1)} %get-tuple-element.20.k_ref, bf16[128,128]{1,0:T(8,128)(2,1)} %slice_bitcast_fusion.v_ref, bf16[32,2,128,128]{3,2,1,0:T(8,128)(2,1)} %all-gather.5.cloned.1.call-done.kv_ref), custom_call_target="tpu_custom_call" | custom-call | tf_op jit(solution)/shard_map/pallas_call | solution.py:97
  114.6 0.0 copy-done
  114.6 1.9 %fusion = bf16[16,8,2560]{2,1,0:T(8,128)(2,1)} fusion(bf16[128,128]{1,0:T(8,128)(2,1)} %shard_map.113, bf16[128,2560]{1,0:T(8,128)(2,1)S(1)} %copy-done), kind=kOutput, calls=%fused_computation.2 | convolution fusion | flops 84213760 | bytes 1343488 | tf_op jit(solution)/shard_map/dot_general | solution.py:146
  116.5 3.6 %all-to-all-start.1 = ((bf16[16,8,2560]{2,1,0:T(8,128)(2,1)}), bf16[16,8,2560]{2,1,0:T(8,128)(2,1)S(1)}, u32[]{:S(2)}, u32[]{:S(2)}) async-start(bf16[16,8,2560]{2,1,0:T(8,128)(2,1)} %fusion), calls=%async_computation.1 | async-start | bytes 1310720 | tf_op jit(solution)/shard_map/all_to_all | solution.py:147
  120.1 0.6 fusion.15.v_ref
  120.7 22.5 %all-to-all-done.1 = bf16[16,8,2560]{2,1,0:T(8,128)(2,1)S(1)} async-done(((bf16[16,8,2560]{2,1,0:T(8,128)(2,1)}), bf16[16,8,2560]{2,1,0:T(8,128)(2,1)S(1)}, u32[]{:S(2)}, u32[]{:S(2)}) %all-to-all-start.1) | async-done | bytes 655392 | tf_op jit(solution)/shard_map/all_to_all | solution.py:147
  143.2 0.7 reduce_sum.72
  144.0 0.0 all-gather.7.cloned.1.call-done.kv_ref
  144.0 7.0 %shard_map.114 = bf16[128,128]{1,0:T(8,128)(2,1)} custom-call(s32[32]{0:T(128)} %fusion.20.allowed_ref, bf16[128,128]{1,0:T(8,128)(2,1)} %get-tuple-element.22.q_ref, bf16[128,128]{1,0:T(8,128)(2,1)} %get-tuple-element.23.k_ref, bf16[128,128]{1,0:T(8,128)(2,1)} %fusion.15.v_ref, bf16[32,2,128,128]{3,2,1,0:T(8,128)(2,1)} %all-gather.7.cloned.1.call-done.kv_ref), custom_call_target="tpu_custom_call" | custom-call | tf_op jit(solution)/shard_map/pallas_call | solution.py:97
  150.9 1.1 fusion.1
  152.0 25.6 %all_to_all.20 = bf16[16,8,2560]{2,1,0:T(8,128)(2,1)S(1)} all-to-all(bf16[16,8,2560]{2,1,0:T(8,128)(2,1)S(1)} %fusion.1), channel_id=1, replica_groups=mesh['y'=8,'zl'=4,'zh'=2,'x'=4,'c'=2] {'zh','x','c'}, dimensions={0} | all-to-all | bytes 1310720 | tf_op jit(solution)/shard_map/all_to_all | solution.py:147
  177.6 0.7 reduce_sum.75
  (14 shorter events, 0.2 us)
Async XLA Ops:
  7.2 107.4 %copy-start = (bf16[128,2560]{1,0:T(8,128)(2,1)S(1)}, bf16[128,2560]{1,0:T(8,128)(2,1)}, u32[]{:S(2)}) copy-start(bf16[128,2560]{1,0:T(8,128)(2,1)} %param.14) | copy-start | bytes 1966084
  7.2 100.4 %all-gather.5.cloned.1.call-start = ((), (), s32[]{:S(2)}) async-start(), calls=%async_computation.4 | async-start | bytes 2359296 | tf_op jit(solution)/shard_map/all_gather | solution.py:123
  25.6 33.3 %all-to-all-start = ((bf16[1,16,8,2560]{3,2,0,1:T(8,128)(2,1)}), bf16[1,16,8,2560]{3,2,0,1:T(8,128)(2,1)S(1)}, u32[]{:S(2)}, u32[]{:S(2)}) async-start(bf16[1,16,8,2560]{3,2,0,1:T(8,128)(2,1)} %broadcast_in_dim.9), calls=%async_computation | async-start | bytes 1310720 | tf_op jit(solution)/shard_map/all_to_all | solution.py:127
  38.5 23.2 %copy-start.3 = (f32[128]{0:T(128)S(1)}, f32[128]{0:T(128)}, u32[]{:S(2)}) copy-start(f32[128]{0:T(128)} %param.16) | copy-start | bytes 1540
  58.9 16.6 %copy-start.2 = (bf16[8,2560]{1,0:T(8,128)(2,1)S(1)}, bf16[8,2560]{1,0:T(8,128)(2,1)}, u32[]{:S(2)}) copy-start(bf16[8,2560]{1,0:T(8,128)(2,1)} %param.11) | copy-start | bytes 122884
  60.3 19.8 %copy-start.6 = (s32[32]{0:T(128)S(1)}, s32[32]{0:T(128)}, u32[]{:S(2)}) copy-start(s32[32]{0:T(128)} %param.18) | copy-start | bytes 388
  76.4 26.7 %all-to-all-start.2 = ((bf16[1,16,8,2560]{3,2,0,1:T(8,128)(2,1)}), bf16[1,16,8,2560]{3,2,0,1:T(8,128)(2,1)S(1)}, u32[]{:S(2)}, u32[]{:S(2)}) async-start(bf16[1,16,8,2560]{3,2,0,1:T(8,128)(2,1)} %broadcast_in_dim.11), calls=%async_computation.2 | async-start | bytes 1310720 | tf_op jit(solution)/shard_map/all_to_all | solution.py:127
  80.0 63.9 %all-gather.7.cloned.1.call-start = ((), (), s32[]{:S(2)}) async-start(), calls=%async_computation.5 | async-start | bytes 2359296 | tf_op jit(solution)/shard_map/all_gather | solution.py:140
  90.8 15.3 %copy-start.1 = (f32[128,128]{1,0:T(8,128)S(1)}, f32[128,128]{1,0:T(8,128)}, u32[]{:S(2)}) copy-start(f32[128,128]{1,0:T(8,128)} %copy.49) | copy-start | bytes 196612
  90.8 15.3 %copy-start.4 = (f32[128]{0:T(128)S(1)}, f32[128]{0:T(128)}, u32[]{:S(2)}) copy-start(f32[128]{0:T(128)} %param.16) | copy-start | bytes 1540
  90.8 15.3 %copy-start.5 = (f32[128]{0:T(128)S(1)}, f32[128]{0:T(128)}, u32[]{:S(2)}) copy-start(f32[128]{0:T(128)} %param.15) | copy-start | bytes 1540
  116.5 26.7 %all-to-all-start.1 = ((bf16[16,8,2560]{2,1,0:T(8,128)(2,1)}), bf16[16,8,2560]{2,1,0:T(8,128)(2,1)S(1)}, u32[]{:S(2)}, u32[]{:S(2)}) async-start(bf16[16,8,2560]{2,1,0:T(8,128)(2,1)} %fusion), calls=%async_computation.1 | async-start | bytes 1310720 | tf_op jit(solution)/shard_map/all_to_all | solution.py:147
Sparse Core Ops, SparseCore 0:
  24.1 45.0 all-gather.4
  82.9 44.2 all-gather.6

commit v10 on v8

--- a/solution.py
+++ b/solution.py
@@ -102,10 +102,34 @@
     )(allowed, query, keys, values, kv)
 
 
-def gather_pipe(piece, order):
-    for name in order:
-        piece = lax.all_gather(piece, name, axis=0, tiled=True)
-    return piece
+def ring_gather(piece, name, size):
+    left = [(i, (i + 1) % size) for i in range(size)]
+    right = [(i, (i - 1) % size) for i in range(size)]
+    got = {0: piece}
+    from_left = piece
+    from_right = piece
+    for d in range(1, size // 2 + 1):
+        from_left = lax.ppermute(from_left, name, left)
+        got[-d % size] = from_left
+        if d < size - d:
+            from_right = lax.ppermute(from_right, name, right)
+            got[d] = from_right
+    return jnp.stack([got[m] for m in range(size)])
+
+
+def ring_gather(piece, name, size):
+    left = [(i, (i + 1) % size) for i in range(size)]
+    right = [(i, (i - 1) % size) for i in range(size)]
+    got = {0: piece}
+    from_left = piece
+    from_right = piece
+    for d in range(1, size // 2 + 1):
+        from_left = lax.ppermute(from_left, name, left)
+        got[-d % size] = from_left
+        if d < size - d:
+            from_right = lax.ppermute(from_right, name, right)
+            got[d] = from_right
+    return jnp.stack([got[m] for m in range(size)])
 
 
 def on_device(
@@ -126,7 +150,11 @@
 
     near = lax.all_gather(stale_kv[None], PIPE[1], axis=0, tiled=True)
     pair, near = lax.optimization_barrier((jnp.stack([x_first, x_second]), near))
-    stale = lax.all_gather(near, PIPE[0], axis=0, tiled=True)
+    ny = PIPE_PARTS[0][1]
+    stale = ring_gather(near, PIPE[0], ny).reshape((-1,) + near.shape[1:])
+    ring = (lax.axis_index(PIPE[0]) + jnp.arange(ny, dtype=jnp.int32)) % ny
+    order = (ring[:, None] * PIPE_PARTS[1][1] + jnp.arange(PIPE_PARTS[1][1], dtype=jnp.int32)[None, :]).reshape(-1)
+    remote_ring = remote[:, order]
 
     def exchange_rows(x):
         spread = jnp.broadcast_to(x[:, None], (x.shape[0], n_seq) + x.shape[1:])
@@ -143,7 +171,8 @@
     q1, k1, v1 = project(xs[0])
     q2, k2, v2 = project(xs[1])
 
-    fresh_kv = gather_pipe(jnp.stack([k1, v1])[None], tuple(reversed(PIPE)))
+    near_fresh = lax.all_gather(jnp.stack([k1, v1])[None], PIPE[1], axis=0, tiled=True)
+    fresh_kv = ring_gather(near_fresh, PIPE[0], ny).reshape((-1,) + near_fresh.shape[1:])
 
     def attend(query, keys, values, kv, remote):
         allowed = remote[0].astype(jnp.int32)
@@ -152,9 +181,9 @@
         sent = lax.all_to_all(part.reshape(n_seq, tokens // n_seq, -1), SEQ, 0, 0, tiled=False)
         return jnp.sum(sent.astype(jnp.float32), axis=0).astype(jnp.bfloat16)
 
-    out_first = attend(q1, k1, v1, stale, remote)
+    out_first = attend(q1, k1, v1, stale, remote_ring)
     out_first, fresh_kv = lax.optimization_barrier((out_first, fresh_kv))
-    out_second = attend(q2, k2, v2, fresh_kv, remote)
+    out_second = attend(q2, k2, v2, fresh_kv, remote_ring)
     return (out_first, out_second)
 
 

time: 178 us -> 200 us (1.12)
  the two profiles are of different devices: /device:TPU:1 before, /device:TPU:65 now
where the time goes in v10:
time: 200 us; the launch traced here: 199 us
  starting transfers between devices  71.5 us (36%)
  blocking collectives  59 us (30%)
  waiting for transfers between devices  23.7 us (12%)
  local copies, waits for them, and re-layouts  19.4 us (10%)
  Pallas kernels  12.6 us (6%)
  matrix products  6.89 us (3%)
  other arithmetic  4.27 us (2%)
    all_to_all x1, blocking collectives, attend(): lax.all_to_all(part.reshape(n_seq, tokens // n_seq, -1), SEQ, 0, 0, tiled...  33.5 us
    ppermute x6, starting transfers between devices, ring_gather(): from_right = lax.ppermute(from_right, name, right)  25.3 us
    ppermute x8, waiting for transfers between devices, ring_gather(): from_left = lax.ppermute(from_left, name, left)  19.5 us
    ppermute x8, starting transfers between devices, ring_gather(): from_left = lax.ppermute(from_left, name, left)  16.8 us
    all_to_all x1, starting transfers between devices, attend(): lax.all_to_all(part.reshape(n_seq, tokens // n_seq, -1), SEQ, 0, 0, tiled...  15 us
    all_to_all x1, starting transfers between devices, exchange_rows(): lax.all_to_all(spread, SEQ, 1, 1, tiled=False)  14.4 us
    all_gather x1, blocking collectives, on_device(): near = lax.all_gather(stale_kv[None], PIPE[1], axis=0, tiled=True)  14.3 us
    unnamed x32, local copies, waits for them, and re-layouts  13.3 us
  transfers between devices with their start and end apart: 16, of which 6 were waited for; matrix products, arithmetic and copies ran while one was open for 12% of the time, Pallas kernels for 3%

profile of v10, /device:TPU:65, one launch (start us, length us, event | category | flops | bytes accessed | tf_op | source)
XLA Modules:
  0.0 198.5 jit_solution(4958205177846814245)
XLA Ops:
  0.6 14.3 %all-gather = bf16[8,128,128]{2,1,0:T(8,128)(2,1)S(1)} all-gather(bf16[2,128,128]{2,1,0:T(8,128)(2,1)} %param.12), channel_id=2, replica_groups=mesh['y'=8,'zl'=4,'zh'=2,'x'=4,'c'=2] {'zl'}, dimensions={0}, use_global_device_ids=true | all-gather | bytes 327680 | tf_op jit(solution)/shard_map/all_gather | solution.py:151
  15.0 0.8 pad_maximum_fusion
  15.8 4.0 %collective-permute-start = (bf16[4,2,128,128]{3,2,1,0:T(8,128)(2,1)S(1)}, bf16[4,2,128,128]{3,2,1,0:T(8,128)(2,1)S(1)}, u32[]{:S(2)}, u32[]{:S(2)}) collective-permute-start(bf16[4,2,128,128]{3,2,1,0:T(8,128)(2,1)S(1)} %bitcast.120), channel_id=1, source_target_pairs={{0,448},{64,0},{128,64},{192,128},{256,192},{320,256},{384,320},{4... | collective-permute-start | bytes 786440 | tf_op jit(solution)/shard_map/ppermute | solution.py:130
  19.8 1.9 collective-permute-start.3
  21.7 1.2 broadcast_in_dim.7
  23.0 14.4 %all-to-all-start = ((bf16[2,16,8,2560]{3,2,0,1:T(8,128)(2,1)}), bf16[2,16,8,2560]{3,2,0,1:T(8,128)(2,1)}, u32[]{:S(2)}, u32[]{:S(2)}) async-start(bf16[2,16,8,2560]{3,2,0,1:T(8,128)(2,1)} %broadcast_in_dim.7), calls=%async_computation | async-start | bytes 2621440 | tf_op jit(solution)/shard_map/all_to_all | solution.py:161
  37.5 0.2 convert_reduce_fusion
  37.7 0.2 fusion.15
  37.9 0.2 fusion.14
  38.3 0.7 bitcast_dynamic-update-slice_fusion.14
  39.0 4.8 %collective-permute-start.1 = (bf16[4,2,128,128]{3,2,1,0:T(8,128)(2,1)S(1)}, bf16[4,2,128,128]{3,2,1,0:T(8,128)(2,1)}, u32[]{:S(2)}, u32[]{:S(2)}) collective-permute-start(bf16[4,2,128,128]{3,2,1,0:T(8,128)(2,1)S(1)} %collective-permute-done), channel_id=1, source_target_pairs={{0,448},{64,0},{128,64},{192,128},{256,192},{320,256},{384,320},{4... | collective-permute-start | bytes 786440 | tf_op jit(solution)/shard_map/ppermute | solution.py:130
  43.9 1.9 collective-permute-start.4
  45.8 8.6 %collective-permute-done.4 = bf16[4,2,128,128]{3,2,1,0:T(8,128)(2,1)S(1)} collective-permute-done((bf16[4,2,128,128]{3,2,1,0:T(8,128)(2,1)S(1)}, bf16[4,2,128,128]{3,2,1,0:T(8,128)(2,1)S(1)}, u32[]{:S(2)}, u32[]{:S(2)}) %collective-permute-start.4) | collective-permute-done | bytes 262176 | tf_op jit(solution)/shard_map/ppermute | solution.py:127
  54.4 1.9 collective-permute-start.5
  56.4 0.7 gather_fusion
  57.1 0.6 convert_element_type.56.allowed_ref
  57.7 2.7 %copy.46 = bf16[3,2560,128]{1,2,0:T(8,128)(2,1)S(1)} copy(bf16[3,2560,128]{2,1,0:T(8,128)(2,1)} %param.13) | data formatting | bytes 3932160 | tf_op args[3]
  60.4 4.6 %collective-permute-start.2 = (bf16[4,2,128,128]{3,2,1,0:T(8,128)(2,1)}, bf16[4,2,128,128]{3,2,1,0:T(8,128)(2,1)S(1)}, u32[]{:S(2)}, u32[]{:S(2)}) collective-permute-start(bf16[4,2,128,128]{3,2,1,0:T(8,128)(2,1)} %collective-permute-done.1), channel_id=1, source_target_pairs={{0,448},{64,0},{128,64},{192,128},{256,192},{320,256},{384,320},{4... | collective-permute-start | bytes 786440 | tf_op jit(solution)/shard_map/ppermute | solution.py:130
  64.9 0.7 bitcast_dynamic-update-slice_fusion.13
  65.7 1.9 collective-permute-start.6
  67.6 1.7 bitcast_dynamic-update-slice_fusion.12
  69.3 0.7 bitcast_dynamic-update-slice_fusion.11
  70.1 4.9 %collective-permute-done.6 = bf16[4,2,128,128]{3,2,1,0:T(8,128)(2,1)S(1)} collective-permute-done((bf16[4,2,128,128]{3,2,1,0:T(8,128)(2,1)}, bf16[4,2,128,128]{3,2,1,0:T(8,128)(2,1)S(1)}, u32[]{:S(2)}, u32[]{:S(2)}) %collective-permute-start.6) | collective-permute-done | bytes 262176 | tf_op jit(solution)/shard_map/ppermute | solution.py:127
  75.0 0.7 bitcast_dynamic-update-slice_fusion.10
  75.7 1.7 bitcast_dynamic-update-slice_fusion.9
  77.4 0.7 bitcast_dynamic-update-slice_fusion.8
  78.1 0.7 bitcast_dynamic-update-slice_fusion.7
  78.8 1.7 fusion.3
  80.6 0.1 copy.47
  80.8 0.1 copy.50
  80.9 0.1 copy.52
  81.1 11.2 %all-gather.1 = bf16[8,128,128]{2,1,0:T(8,128)(2,1)S(1)} all-gather(bf16[2,128,128]{2,1,0:T(8,128)(2,1)S(1)} %pad_maximum_fusion.1), channel_id=3, replica_groups=mesh['y'=8,'zl'=4,'zh'=2,'x'=4,'c'=2] {'zl'}, dimensions={0}, use_global_device_ids=true | all-gather | bytes 327680 | tf_op jit(solution)/shard_map/all_gather | solution.py:174
  92.3 1.9 collective-permute-start.7
  94.2 3.4 %collective-permute-start.10 = (bf16[4,2,128,128]{3,2,1,0:T(8,128)(2,1)S(1)}, bf16[4,2,128,128]{3,2,1,0:T(8,128)(2,1)}, u32[]{:S(2)}, u32[]{:S(2)}) collective-permute-start(bf16[4,2,128,128]{3,2,1,0:T(8,128)(2,1)S(1)} %bitcast.118), channel_id=1, source_target_pairs={{0,64},{64,128},{128,192},{192,256},{256,320},{320,384},{384,448},... | collective-permute-start | bytes 786440 | tf_op jit(solution)/shard_map/ppermute | solution.py:127
  97.6 0.1 copy.51
  97.7 0.1 copy.48
  97.8 0.1 copy.49
  97.9 1.8 fusion.2
  99.7 0.1 copy.54
  100.1 0.1 copy.57
  100.3 0.7 fusion.10
  101.0 0.6 slice_bitcast_fusion.4.v_ref
  101.6 6.3 %shard_map.113 = bf16[128,128]{1,0:T(8,128)(2,1)} custom-call(s32[32]{0:T(128)} %convert_element_type.56.allowed_ref, bf16[128,128]{1,0:T(8,128)(2,1)} %get-tuple-element.17.q_ref, bf16[128,128]{1,0:T(8,128)(2,1)} %get-tuple-element.16.k_ref, bf16[128,128]{1,0:T(8,128)(2,1)} %slice_bitcast_fusion.4.v_ref, bf16[32,2,128,128]{3,2,1,0:T(8,128)(2,1)} %bitcast.107), custom_call_target="tpu_custom_call" | custom-call | tf_op jit(solution)/shard_map/pallas_call | solution.py:97
  107.9 1.9 collective-permute-start.11
  109.9 1.9 fusion
  111.8 15.0 %all-to-all-start.1 = ((bf16[16,8,2560]{2,1,0:T(8,128)(2,1)}), bf16[16,8,2560]{2,1,0:T(8,128)(2,1)S(1)}, u32[]{:S(2)}, u32[]{:S(2)}) async-start(bf16[16,8,2560]{2,1,0:T(8,128)(2,1)} %fusion), calls=%async_computation.1 | async-start | bytes 1310720 | tf_op jit(solution)/shard_map/all_to_all | solution.py:181
  126.8 4.9 %collective-permute-start.8 = (bf16[4,2,128,128]{3,2,1,0:T(8,128)(2,1)}, bf16[4,2,128,128]{3,2,1,0:T(8,128)(2,1)S(1)}, u32[]{:S(2)}, u32[]{:S(2)}) collective-permute-start(bf16[4,2,128,128]{3,2,1,0:T(8,128)(2,1)} %collective-permute-done.7), channel_id=1, source_target_pairs={{0,448},{64,0},{128,64},{192,128},{256,192},{320,256},{384,320},{4... | collective-permute-start | bytes 786440 | tf_op jit(solution)/shard_map/ppermute | solution.py:130
  131.7 0.6 fusion.13.v_ref
  132.3 1.9 collective-permute-start.12
  134.2 1.0 constant_dynamic-update-slice_fusion
  135.2 2.3 %collective-permute-done.8 = bf16[4,2,128,128]{3,2,1,0:T(8,128)(2,1)S(1)} collective-permute-done((bf16[4,2,128,128]{3,2,1,0:T(8,128)(2,1)}, bf16[4,2,128,128]{3,2,1,0:T(8,128)(2,1)S(1)}, u32[]{:S(2)}, u32[]{:S(2)}) %collective-permute-start.8) | collective-permute-done | bytes 262176 | tf_op jit(solution)/shard_map/ppermute | solution.py:130
  137.6 5.2 %collective-permute-start.9 = (bf16[4,2,128,128]{3,2,1,0:T(8,128)(2,1)S(1)}, bf16[4,2,128,128]{3,2,1,0:T(8,128)(2,1)S(1)}, u32[]{:S(2)}, u32[]{:S(2)}) collective-permute-start(bf16[4,2,128,128]{3,2,1,0:T(8,128)(2,1)S(1)} %collective-permute-done.8), channel_id=1, source_target_pairs={{0,448},{64,0},{128,64},{192,128},{256,192},{320,256},{384,320},{4... | collective-permute-start | bytes 786440 | tf_op jit(solution)/shard_map/ppermute | solution.py:130
  142.8 1.0 bitcast_dynamic-update-slice_fusion.6
  143.8 1.9 collective-permute-start.13
  145.7 1.7 collective-permute-done.9
  147.5 6.0 %collective-permute-done.13 = bf16[4,2,128,128]{3,2,1,0:T(8,128)(2,1)S(1)} collective-permute-done((bf16[4,2,128,128]{3,2,1,0:T(8,128)(2,1)S(1)}, bf16[4,2,128,128]{3,2,1,0:T(8,128)(2,1)S(1)}, u32[]{:S(2)}, u32[]{:S(2)}) %collective-permute-start.13) | collective-permute-done | bytes 262176 | tf_op jit(solution)/shard_map/ppermute | solution.py:127
  153.6 1.0 bitcast_dynamic-update-slice_fusion.1
  154.6 1.0 bitcast_dynamic-update-slice_fusion
  155.6 0.8 reduce_sum.72
  156.4 0.5 copy-done.1
  156.9 6.3 %shard_map.114 = bf16[128,128]{1,0:T(8,128)(2,1)} custom-call(s32[32]{0:T(128)} %convert_element_type.56.allowed_ref, bf16[128,128]{1,0:T(8,128)(2,1)} %get-tuple-element.18.q_ref, bf16[128,128]{1,0:T(8,128)(2,1)} %get-tuple-element.19.k_ref, bf16[128,128]{1,0:T(8,128)(2,1)} %fusion.13.v_ref, bf16[32,2,128,128]{3,2,1,0:T(8,128)(2,1)} %bitcast.108), custom_call_target="tpu_custom_call" | custom-call | tf_op jit(solution)/shard_map/pallas_call | solution.py:97
  163.2 1.1 fusion.1
  164.3 33.5 %all_to_all.15 = bf16[16,8,2560]{2,1,0:T(8,128)(2,1)S(1)} all-to-all(bf16[16,8,2560]{2,1,0:T(8,128)(2,1)S(1)} %fusion.1), channel_id=1, replica_groups=mesh['y'=8,'zl'=4,'zh'=2,'x'=4,'c'=2] {'zh','x','c'}, dimensions={0} | all-to-all | bytes 1310720 | tf_op jit(solution)/shard_map/all_to_all | solution.py:181
  197.8 0.7 reduce_sum.75
  (58 shorter events, 1.1 us)
Async XLA Ops:
  0.6 109.2 %copy-start = (bf16[128,2560]{1,0:T(8,128)(2,1)S(1)}, bf16[128,2560]{1,0:T(8,128)(2,1)}, u32[]{:S(2)}) copy-start(bf16[128,2560]{1,0:T(8,128)(2,1)} %param.14) | copy-start | bytes 1966084
  15.0 22.3 %copy-start.3 = (s32[32,16]{0,1:T(8,128)S(1)}, s32[32,16]{0,1:T(8,128)}, u32[]{:S(2)}) copy-start(s32[32,16]{0,1:T(8,128)} %param.17) | copy-start | bytes 6148
  15.0 22.4 %copy-start.6 = (s32[32]{0:T(128)S(1)}, s32[32]{0:T(128)}, u32[]{:S(2)}) copy-start(s32[32]{0:T(128)} %param.18) | copy-start | bytes 388
  15.0 22.7 %copy-start.7 = (s32[32]{0:T(128)S(1)}, s32[32]{0:T(128)}, u32[]{:S(2)}) copy-start(s32[32]{0:T(128)} %param.19) | copy-start | bytes 388
  15.8 23.2 %collective-permute-start = (bf16[4,2,128,128]{3,2,1,0:T(8,128)(2,1)S(1)}, bf16[4,2,128,128]{3,2,1,0:T(8,128)(2,1)S(1)}, u32[]{:S(2)}, u32[]{:S(2)}) collective-permute-start(bf16[4,2,128,128]{3,2,1,0:T(8,128)(2,1)S(1)} %bitcast.120), channel_id=1, source_target_pairs={{0,448},{64,0},{128,64},{192,128},{256,192},{320,256},{384,320},{4... | collective-permute-start | bytes 786440 | tf_op jit(solution)/shard_map/ppermute | solution.py:130
  19.8 24.1 %collective-permute-start.3 = (bf16[4,2,128,128]{3,2,1,0:T(8,128)(2,1)S(1)}, bf16[4,2,128,128]{3,2,1,0:T(8,128)(2,1)S(1)}, u32[]{:S(2)}, u32[]{:S(2)}) collective-permute-start(bf16[4,2,128,128]{3,2,1,0:T(8,128)(2,1)S(1)} %bitcast.121), channel_id=1, source_target_pairs={{0,64},{64,128},{128,192},{192,256},{256,320},{320,384},{384,448},... | collective-permute-start | bytes 786440 | tf_op jit(solution)/shard_map/ppermute | solution.py:127
  23.0 55.9 %all-to-all-start = ((bf16[2,16,8,2560]{3,2,0,1:T(8,128)(2,1)}), bf16[2,16,8,2560]{3,2,0,1:T(8,128)(2,1)}, u32[]{:S(2)}, u32[]{:S(2)}) async-start(bf16[2,16,8,2560]{3,2,0,1:T(8,128)(2,1)} %broadcast_in_dim.7), calls=%async_computation | async-start | bytes 2621440 | tf_op jit(solution)/shard_map/all_to_all | solution.py:161
  39.0 21.3 %collective-permute-start.1 = (bf16[4,2,128,128]{3,2,1,0:T(8,128)(2,1)S(1)}, bf16[4,2,128,128]{3,2,1,0:T(8,128)(2,1)}, u32[]{:S(2)}, u32[]{:S(2)}) collective-permute-start(bf16[4,2,128,128]{3,2,1,0:T(8,128)(2,1)S(1)} %collective-permute-done), channel_id=1, source_target_pairs={{0,448},{64,0},{128,64},{192,128},{256,192},{320,256},{384,320},{4... | collective-permute-start | bytes 786440 | tf_op jit(solution)/shard_map/ppermute | solution.py:130
  43.9 10.5 %collective-permute-start.4 = (bf16[4,2,128,128]{3,2,1,0:T(8,128)(2,1)S(1)}, bf16[4,2,128,128]{3,2,1,0:T(8,128)(2,1)S(1)}, u32[]{:S(2)}, u32[]{:S(2)}) collective-permute-start(bf16[4,2,128,128]{3,2,1,0:T(8,128)(2,1)S(1)} %collective-permute-done.3), channel_id=1, source_target_pairs={{0,64},{64,128},{128,192},{192,256},{256,320},{320,384},{384,448},... | collective-permute-start | bytes 786440 | tf_op jit(solution)/shard_map/ppermute | solution.py:127
  54.4 11.3 %collective-permute-start.5 = (bf16[4,2,128,128]{3,2,1,0:T(8,128)(2,1)S(1)}, bf16[4,2,128,128]{3,2,1,0:T(8,128)(2,1)}, u32[]{:S(2)}, u32[]{:S(2)}) collective-permute-start(bf16[4,2,128,128]{3,2,1,0:T(8,128)(2,1)S(1)} %collective-permute-done.4), channel_id=1, source_target_pairs={{0,64},{64,128},{128,192},{192,256},{256,320},{320,384},{384,448},... | collective-permute-start | bytes 786440 | tf_op jit(solution)/shard_map/ppermute | solution.py:127
  60.4 9.0 %collective-permute-start.2 = (bf16[4,2,128,128]{3,2,1,0:T(8,128)(2,1)}, bf16[4,2,128,128]{3,2,1,0:T(8,128)(2,1)S(1)}, u32[]{:S(2)}, u32[]{:S(2)}) collective-permute-start(bf16[4,2,128,128]{3,2,1,0:T(8,128)(2,1)} %collective-permute-done.1), channel_id=1, source_target_pairs={{0,448},{64,0},{128,64},{192,128},{256,192},{320,256},{384,320},{4... | collective-permute-start | bytes 786440 | tf_op jit(solution)/shard_map/ppermute | solution.py:130
  65.7 9.3 %collective-permute-start.6 = (bf16[4,2,128,128]{3,2,1,0:T(8,128)(2,1)}, bf16[4,2,128,128]{3,2,1,0:T(8,128)(2,1)S(1)}, u32[]{:S(2)}, u32[]{:S(2)}) collective-permute-start(bf16[4,2,128,128]{3,2,1,0:T(8,128)(2,1)} %collective-permute-done.5), channel_id=1, source_target_pairs={{0,64},{64,128},{128,192},{192,256},{256,320},{320,384},{384,448},... | collective-permute-start | bytes 786440 | tf_op jit(solution)/shard_map/ppermute | solution.py:127
  78.1 2.9 %copy-start.4 = (f32[128]{0:T(128)S(1)}, f32[128]{0:T(128)}, u32[]{:S(2)}) copy-start(f32[128]{0:T(128)} %param.16) | copy-start | bytes 1540
  92.3 42.0 %copy-start.2 = (bf16[8,128,128]{2,1,0:T(8,128)(2,1)}, bf16[8,128,128]{2,1,0:T(8,128)(2,1)S(1)}, u32[]{:S(2)}) copy-start(bf16[8,128,128]{2,1,0:T(8,128)(2,1)S(1)} %all-gather.1) | copy-start | bytes 786436
  92.3 34.6 %collective-permute-start.7 = (bf16[4,2,128,128]{3,2,1,0:T(8,128)(2,1)S(1)}, bf16[4,2,128,128]{3,2,1,0:T(8,128)(2,1)}, u32[]{:S(2)}, u32[]{:S(2)}) collective-permute-start(bf16[4,2,128,128]{3,2,1,0:T(8,128)(2,1)S(1)} %bitcast.117), channel_id=1, source_target_pairs={{0,448},{64,0},{128,64},{192,128},{256,192},{320,256},{384,320},{4... | collective-permute-start | bytes 786440 | tf_op jit(solution)/shard_map/ppermute | solution.py:130
  94.2 13.7 %collective-permute-start.10 = (bf16[4,2,128,128]{3,2,1,0:T(8,128)(2,1)S(1)}, bf16[4,2,128,128]{3,2,1,0:T(8,128)(2,1)}, u32[]{:S(2)}, u32[]{:S(2)}) collective-permute-start(bf16[4,2,128,128]{3,2,1,0:T(8,128)(2,1)S(1)} %bitcast.118), channel_id=1, source_target_pairs={{0,64},{64,128},{128,192},{192,256},{256,320},{320,384},{384,448},... | collective-permute-start | bytes 786440 | tf_op jit(solution)/shard_map/ppermute | solution.py:127
  97.9 2.4 %copy-start.5 = (f32[128]{0:T(128)S(1)}, f32[128]{0:T(128)}, u32[]{:S(2)}) copy-start(f32[128]{0:T(128)} %param.15) | copy-start | bytes 1540
  107.9 24.4 %collective-permute-start.11 = (bf16[4,2,128,128]{3,2,1,0:T(8,128)(2,1)}, bf16[4,2,128,128]{3,2,1,0:T(8,128)(2,1)}, u32[]{:S(2)}, u32[]{:S(2)}) collective-permute-start(bf16[4,2,128,128]{3,2,1,0:T(8,128)(2,1)} %collective-permute-done.10), channel_id=1, source_target_pairs={{0,64},{64,128},{128,192},{192,256},{256,320},{320,384},{384,448},... | collective-permute-start | bytes 786440 | tf_op jit(solution)/shard_map/ppermute | solution.py:127
  111.8 43.8 %all-to-all-start.1 = ((bf16[16,8,2560]{2,1,0:T(8,128)(2,1)}), bf16[16,8,2560]{2,1,0:T(8,128)(2,1)S(1)}, u32[]{:S(2)}, u32[]{:S(2)}) async-start(bf16[16,8,2560]{2,1,0:T(8,128)(2,1)} %fusion), calls=%async_computation.1 | async-start | bytes 1310720 | tf_op jit(solution)/shard_map/all_to_all | solution.py:181
  126.8 10.7 %collective-permute-start.8 = (bf16[4,2,128,128]{3,2,1,0:T(8,128)(2,1)}, bf16[4,2,128,128]{3,2,1,0:T(8,128)(2,1)S(1)}, u32[]{:S(2)}, u32[]{:S(2)}) collective-permute-start(bf16[4,2,128,128]{3,2,1,0:T(8,128)(2,1)} %collective-permute-done.7), channel_id=1, source_target_pairs={{0,448},{64,0},{128,64},{192,128},{256,192},{320,256},{384,320},{4... | collective-permute-start | bytes 786440 | tf_op jit(solution)/shard_map/ppermute | solution.py:130
  132.3 11.4 %collective-permute-start.12 = (bf16[4,2,128,128]{3,2,1,0:T(8,128)(2,1)}, bf16[4,2,128,128]{3,2,1,0:T(8,128)(2,1)S(1)}, u32[]{:S(2)}, u32[]{:S(2)}) collective-permute-start(bf16[4,2,128,128]{3,2,1,0:T(8,128)(2,1)} %collective-permute-done.11), channel_id=1, source_target_pairs={{0,64},{64,128},{128,192},{192,256},{256,320},{320,384},{384,448},... | collective-permute-start | bytes 786440 | tf_op jit(solution)/shard_map/ppermute | solution.py:127
  137.6 9.9 %collective-permute-start.9 = (bf16[4,2,128,128]{3,2,1,0:T(8,128)(2,1)S(1)}, bf16[4,2,128,128]{3,2,1,0:T(8,128)(2,1)S(1)}, u32[]{:S(2)}, u32[]{:S(2)}) collective-permute-start(bf16[4,2,128,128]{3,2,1,0:T(8,128)(2,1)S(1)} %collective-permute-done.8), channel_id=1, source_target_pairs={{0,448},{64,0},{128,64},{192,128},{256,192},{320,256},{384,320},{4... | collective-permute-start | bytes 786440 | tf_op jit(solution)/shard_map/ppermute | solution.py:130
  143.8 9.7 %collective-permute-start.13 = (bf16[4,2,128,128]{3,2,1,0:T(8,128)(2,1)S(1)}, bf16[4,2,128,128]{3,2,1,0:T(8,128)(2,1)S(1)}, u32[]{:S(2)}, u32[]{:S(2)}) collective-permute-start(bf16[4,2,128,128]{3,2,1,0:T(8,128)(2,1)S(1)} %collective-permute-done.12), channel_id=1, source_target_pairs={{0,64},{64,128},{128,192},{192,256},{256,320},{320,384},{384,448},... | collective-permute-start | bytes 786440 | tf_op jit(solution)/shard_map/ppermute | solution.py:127
  155.6 1.4 copy-start.1

commit v11 on v8

--- a/solution.py
+++ b/solution.py
@@ -45,7 +45,7 @@
     return (grid * factor).reshape(count, -1) * gain[None, :]
 
 
-def attn_kernel(allowed_ref, q_ref, k_ref, v_ref, kv_ref, o_ref, *, scale, n_blocks):
+def attn_kernel(count_ref, listed_ref, q_ref, k_ref, v_ref, kv_ref, o_ref, *, scale):
     q = q_ref[...] * jnp.asarray(scale, q_ref.dtype)
     rows, width = q.shape
     lane = lax.broadcasted_iota(jnp.int32, (rows, width), 1)
@@ -81,25 +81,25 @@
     )
     carry = update(init, k_ref[...], v_ref[...])
 
-    def visit(b, carry):
+    def body(i, carry):
+        b = listed_ref[i]
         return update(carry, kv_ref[b, 0], kv_ref[b, 1])
 
-    def body(b, carry):
-        return lax.cond(allowed_ref[b] > 0, functools.partial(visit, b), lambda c: c, carry)
-
-    m0, m1, l0, l1, acc = lax.fori_loop(0, n_blocks, body, carry)
+    m0, m1, l0, l1, acc = lax.fori_loop(0, count_ref[0], body, carry)
     o_ref[...] = (acc / jnp.where(first, l0, l1)).T.astype(o_ref.dtype)
 
 
 def block_attend(allowed, query, keys, values, kv, scale):
-    n_blocks = kv.shape[0]
+    listed = jnp.argsort(jnp.logical_not(allowed), stable=True).astype(jnp.int32)
+    count = jnp.sum(allowed.astype(jnp.int32)).reshape(1)
+    smem = pltpu.MemorySpace.SMEM
     vmem = pltpu.MemorySpace.VMEM
     return pl.pallas_call(
-        functools.partial(attn_kernel, scale=scale, n_blocks=n_blocks),
+        functools.partial(attn_kernel, scale=scale),
         out_shape=jax.ShapeDtypeStruct(query.shape, jnp.bfloat16),
-        in_specs=[pl.BlockSpec(memory_space=pltpu.MemorySpace.SMEM)] + [pl.BlockSpec(memory_space=vmem)] * 4,
+        in_specs=[pl.BlockSpec(memory_space=smem)] * 2 + [pl.BlockSpec(memory_space=vmem)] * 4,
         out_specs=pl.BlockSpec(memory_space=vmem),
-    )(allowed, query, keys, values, kv)
+    )(count, listed, query, keys, values, kv)
 
 
 def gather_pipe(piece, order):
@@ -146,8 +146,7 @@
     fresh_kv = gather_pipe(jnp.stack([k1, v1])[None], tuple(reversed(PIPE)))
 
     def attend(query, keys, values, kv, remote):
-        allowed = remote[0].astype(jnp.int32)
-        attn = block_attend(allowed, query, keys, values, kv, scale)
+        attn = block_attend(remote[0], query, keys, values, kv, scale)
         part = jnp.dot(attn, w_out, preferred_element_type=jnp.float32).astype(jnp.bfloat16)
         sent = lax.all_to_all(part.reshape(n_seq, tokens // n_seq, -1), SEQ, 0, 0, tiled=False)
         return jnp.sum(sent.astype(jnp.float32), axis=0).astype(jnp.bfloat16)

time: 178 us -> 179 us (level)
  the two profiles are of different devices: /device:TPU:1 before, /device:TPU:64 now
where the time goes in v11:
time: 179 us; the launch traced here: 178 us
  blocking collectives  60.6 us (34%)
  waiting for transfers between devices  56.6 us (32%)
  Pallas kernels  15.2 us (8%)
  between operations  14.4 us (8%)
  starting transfers between devices  12.5 us (7%)
  matrix products  6.89 us (4%)
  local copies, waits for them, and re-layouts  6.31 us (4%)
  other arithmetic  5.67 us (3%)
    all_to_all x1, waiting for transfers between devices, exchange_rows(): lax.all_to_all(spread, SEQ, 1, 1, tiled=False)  34.1 us
    all_to_all x1, blocking collectives, attend(): lax.all_to_all(part.reshape(n_seq, tokens // n_seq, -1), SEQ, 0, 0, tiled...  29.6 us
    all_to_all x1, waiting for transfers between devices, attend(): lax.all_to_all(part.reshape(n_seq, tokens // n_seq, -1), SEQ, 0, 0, tiled...  22.5 us
    all_gather x1, blocking collectives, on_device(): near = lax.all_gather(stale_kv[None], PIPE[1], axis=0, tiled=True)  18 us
    pallas_call x2, Pallas kernels, block_attend(): pl.pallas_call(functools.partial(attn_kernel, scale=scale), out_shape=jax...  15.2 us
    all_gather x1, blocking collectives, gather_pipe(): piece = lax.all_gather(piece, name, axis=0, tiled=True)  12.9 us
    all_to_all x1, starting transfers between devices, exchange_rows(): lax.all_to_all(spread, SEQ, 1, 1, tiled=False)  8.86 us
    all_to_all x1, starting transfers between devices, attend(): lax.all_to_all(part.reshape(n_seq, tokens // n_seq, -1), SEQ, 0, 0, tiled...  3.59 us
  transfers between devices with their start and end apart: 4, of which 2 were waited for; matrix products, arithmetic and copies ran while one was open for 9% of the time, Pallas kernels for 4%

profile of v11, /device:TPU:64, one launch (start us, length us, event | category | flops | bytes accessed | tf_op | source)
XLA Modules:
  0.0 178.2 jit_solution(8687875546766208083)
XLA Ops:
  7.2 0.0 copy-start
  7.2 0.0 all-gather.5.cloned.1.call-start
  7.2 18.0 %all-gather = bf16[8,128,128]{2,1,0:T(8,128)(2,1)} all-gather(bf16[2,128,128]{2,1,0:T(8,128)(2,1)} %param.12), channel_id=2, replica_groups=mesh['y'=8,'zl'=4,'zh'=2,'x'=4,'c'=2] {'zl'}, dimensions={0}, use_global_device_ids=true | all-gather | bytes 327680 | tf_op jit(solution)/shard_map/all_gather | solution.py:127
  25.3 0.8 pad_maximum_fusion
  26.1 0.0 all-gather.5.cloned.1.call-update
  26.1 1.2 broadcast_in_dim.7
  27.3 8.9 %all-to-all-start = ((bf16[2,16,8,2560]{3,2,0,1:T(8,128)(2,1)}), bf16[2,16,8,2560]{3,2,0,1:T(8,128)(2,1)}, u32[]{:S(2)}, u32[]{:S(2)}) async-start(bf16[2,16,8,2560]{3,2,0,1:T(8,128)(2,1)} %broadcast_in_dim.7), calls=%async_computation | async-start | bytes 2621440 | tf_op jit(solution)/shard_map/all_to_all | solution.py:133
  36.1 0.0 all-gather.7.cloned.1.call-start
  36.2 0.0 copy-start.1
  36.2 0.0 copy-start.4
  36.2 2.7 %copy.46 = bf16[3,2560,128]{1,2,0:T(8,128)(2,1)S(1)} copy(bf16[3,2560,128]{2,1,0:T(8,128)(2,1)} %param.13) | data formatting | bytes 3932160 | tf_op args[3]
  38.9 0.0 copy-start.2
  38.9 0.0 copy-done.1
  38.9 0.1 copy.45
  39.0 0.0 copy-done.4
  39.0 0.1 iota_compare_fusion.1
  39.1 0.2 convert_reduce_fusion
  39.3 34.1 %all-to-all-done = bf16[2,16,8,2560]{3,2,0,1:T(8,128)(2,1)} async-done(((bf16[2,16,8,2560]{3,2,0,1:T(8,128)(2,1)}), bf16[2,16,8,2560]{3,2,0,1:T(8,128)(2,1)}, u32[]{:S(2)}, u32[]{:S(2)}) %all-to-all-start) | async-done | bytes 1310752 | tf_op jit(solution)/shard_map/all_to_all | solution.py:133
  73.4 0.0 copy-start.5
  73.4 1.8 fusion.3
  75.2 0.1 copy.47
  75.4 0.1 copy.50
  75.5 0.1 copy.52
  75.6 0.0 copy-done.2
  75.7 12.9 %all-gather.1 = bf16[8,128,128]{2,1,0:T(8,128)(2,1)} all-gather(bf16[2,128,128]{2,1,0:T(8,128)(2,1)S(1)} %pad_maximum_fusion.1), channel_id=3, replica_groups=mesh['y'=8,'zl'=4,'zh'=2,'x'=4,'c'=2] {'zl'}, dimensions={0}, use_global_device_ids=true | all-gather | bytes 327680 | tf_op jit(solution)/shard_map/all_gather | solution.py:107
  88.6 0.0 all-gather.7.cloned.1.call-update
  88.6 0.0 copy-done.5
  88.6 0.2 fusion.15
  88.8 0.2 fusion.14
  89.1 1.6 sort.19
  90.7 0.6 convert_reduce_fusion.1
  91.4 0.1 copy.48
  91.5 0.1 copy.49
  91.6 0.1 copy.51
  91.7 0.0 copy-start.3
  91.7 1.8 fusion.2
  93.5 0.1 copy.54
  93.6 0.1 copy.55
  93.8 0.1 copy.56
  93.9 0.1 copy.57
  94.0 0.1 copy.58
  94.1 0.6 slice_bitcast_fusion.4.v_ref
  94.8 0.0 copy-done.3
  94.8 0.7 fusion.10
  95.4 0.0 all-gather.5.cloned.1.call-done.kv_ref
  95.4 7.6 %shard_map.113 = bf16[128,128]{1,0:T(8,128)(2,1)} custom-call(s32[1]{0:T(128)} %bitcast.count_ref, s32[32]{0:T(128)} %get-tuple-element.7.listed_ref, bf16[128,128]{1,0:T(8,128)(2,1)} %get-tuple-element.21.q_ref, bf16[128,128]{1,0:T(8,128)(2,1)} %get-tuple-element.20.k_ref, bf16[128,128]{1,0:T(8,128)(2,1)} %slice_bitcast_fusion.4.v_ref, ...), custom_call_target="tpu_custom_call" | custom-call | tf_op jit(solution)/shard_map/pallas_call | solution.py:97
  103.0 0.0 copy-done
  103.0 1.9 %fusion = bf16[16,8,2560]{2,1,0:T(8,128)(2,1)} fusion(bf16[128,128]{1,0:T(8,128)(2,1)} %shard_map.113, bf16[128,2560]{1,0:T(8,128)(2,1)S(1)} %copy-done), kind=kOutput, calls=%fused_computation.2 | convolution fusion | flops 84213760 | bytes 1343488 | tf_op jit(solution)/shard_map/dot_general | solution.py:150
  104.9 3.6 %all-to-all-start.1 = ((bf16[16,8,2560]{2,1,0:T(8,128)(2,1)}), bf16[16,8,2560]{2,1,0:T(8,128)(2,1)S(1)}, u32[]{:S(2)}, u32[]{:S(2)}) async-start(bf16[16,8,2560]{2,1,0:T(8,128)(2,1)} %fusion), calls=%async_computation.1 | async-start | bytes 1310720 | tf_op jit(solution)/shard_map/all_to_all | solution.py:151
  108.5 0.6 fusion.13.v_ref
  109.2 22.5 %all-to-all-done.1 = bf16[16,8,2560]{2,1,0:T(8,128)(2,1)S(1)} async-done(((bf16[16,8,2560]{2,1,0:T(8,128)(2,1)}), bf16[16,8,2560]{2,1,0:T(8,128)(2,1)S(1)}, u32[]{:S(2)}, u32[]{:S(2)}) %all-to-all-start.1) | async-done | bytes 655392 | tf_op jit(solution)/shard_map/all_to_all | solution.py:151
  131.6 0.7 reduce_sum.86
  132.3 0.0 all-gather.7.cloned.1.call-done.kv_ref
  132.3 7.6 %shard_map.114 = bf16[128,128]{1,0:T(8,128)(2,1)} custom-call(s32[1]{0:T(128)} %bitcast.count_ref, s32[32]{0:T(128)} %get-tuple-element.7.listed_ref, bf16[128,128]{1,0:T(8,128)(2,1)} %get-tuple-element.22.q_ref, bf16[128,128]{1,0:T(8,128)(2,1)} %get-tuple-element.23.k_ref, bf16[128,128]{1,0:T(8,128)(2,1)} %fusion.13.v_ref, ...), custom_call_target="tpu_custom_call" | custom-call | tf_op jit(solution)/shard_map/pallas_call | solution.py:97
  139.9 1.1 fusion.1
  141.0 29.6 %all_to_all.15 = bf16[16,8,2560]{2,1,0:T(8,128)(2,1)S(1)} all-to-all(bf16[16,8,2560]{2,1,0:T(8,128)(2,1)S(1)} %fusion.1), channel_id=1, replica_groups=mesh['y'=8,'zl'=4,'zh'=2,'x'=4,'c'=2] {'zh','x','c'}, dimensions={0} | all-to-all | bytes 1310720 | tf_op jit(solution)/shard_map/all_to_all | solution.py:151
  170.6 0.7 reduce_sum.89
  (19 shorter events, 0.2 us)
Async XLA Ops:
  7.2 95.9 %copy-start = (bf16[128,2560]{1,0:T(8,128)(2,1)S(1)}, bf16[128,2560]{1,0:T(8,128)(2,1)}, u32[]{:S(2)}) copy-start(bf16[128,2560]{1,0:T(8,128)(2,1)} %param.14) | copy-start | bytes 1966084
  7.2 88.2 %all-gather.5.cloned.1.call-start = ((), (), s32[]{:S(2)}) async-start(), calls=%async_computation.3 | async-start | bytes 2359296 | tf_op jit(solution)/shard_map/all_gather | solution.py:129
  27.3 46.2 %all-to-all-start = ((bf16[2,16,8,2560]{3,2,0,1:T(8,128)(2,1)}), bf16[2,16,8,2560]{3,2,0,1:T(8,128)(2,1)}, u32[]{:S(2)}, u32[]{:S(2)}) async-start(bf16[2,16,8,2560]{3,2,0,1:T(8,128)(2,1)} %broadcast_in_dim.7), calls=%async_computation | async-start | bytes 2621440 | tf_op jit(solution)/shard_map/all_to_all | solution.py:133
  36.1 96.2 %all-gather.7.cloned.1.call-start = ((), (), s32[]{:S(2)}) async-start(), calls=%async_computation.4 | async-start | bytes 2359296 | tf_op jit(solution)/shard_map/all_gather | solution.py:107
  36.2 2.7 %copy-start.1 = (s32[32,16]{0,1:T(8,128)S(1)}, s32[32,16]{0,1:T(8,128)}, u32[]{:S(2)}) copy-start(s32[32,16]{0,1:T(8,128)} %param.17) | copy-start | bytes 6148
  36.2 2.8 %copy-start.4 = (s32[32]{0:T(128)S(1)}, s32[32]{0:T(128)}, u32[]{:S(2)}) copy-start(s32[32]{0:T(128)} %param.18) | copy-start | bytes 388
  38.9 36.7 %copy-start.2 = (f32[128]{0:T(128)S(1)}, f32[128]{0:T(128)}, u32[]{:S(2)}) copy-start(f32[128]{0:T(128)} %param.16) | copy-start | bytes 1540
  73.4 15.2 %copy-start.5 = (s32[32]{0:T(128)S(1)}, s32[32]{0:T(128)}, u32[]{:S(2)}) copy-start(s32[32]{0:T(128)} %param.19) | copy-start | bytes 388
  91.7 3.0 %copy-start.3 = (f32[128]{0:T(128)S(1)}, f32[128]{0:T(128)}, u32[]{:S(2)}) copy-start(f32[128]{0:T(128)} %param.15) | copy-start | bytes 1540
  104.9 26.7 %all-to-all-start.1 = ((bf16[16,8,2560]{2,1,0:T(8,128)(2,1)}), bf16[16,8,2560]{2,1,0:T(8,128)(2,1)S(1)}, u32[]{:S(2)}, u32[]{:S(2)}) async-start(bf16[16,8,2560]{2,1,0:T(8,128)(2,1)} %fusion), calls=%async_computation.1 | async-start | bytes 1310720 | tf_op jit(solution)/shard_map/all_to_all | solution.py:151
Sparse Core Ops, SparseCore 0:
  26.2 44.7 all-gather.4
  88.8 41.2 all-gather.6

commit v12 on v11

--- a/solution.py
+++ b/solution.py
@@ -50,33 +50,24 @@
     rows, width = q.shape
     lane = lax.broadcasted_iota(jnp.int32, (rows, width), 1)
     zero = jnp.zeros_like(q)
-    qt0 = jnp.where(lane < HS, q, zero).T
-    qt1 = jnp.where(lane < HS, zero, q).T
+    both = jnp.concatenate([jnp.where(lane < HS, q, zero).T, jnp.where(lane < HS, zero, q).T], axis=1)
     first = lax.broadcasted_iota(jnp.int32, (width, rows), 0) < HS
 
     def update(carry, kb, vb):
-        m0, m1, l0, l1, acc = carry
-        s0 = jnp.dot(kb, qt0, preferred_element_type=jnp.float32)
-        s1 = jnp.dot(kb, qt1, preferred_element_type=jnp.float32)
-        n0 = jnp.maximum(m0, jnp.max(s0, axis=0, keepdims=True))
-        n1 = jnp.maximum(m1, jnp.max(s1, axis=0, keepdims=True))
-        a0 = jnp.exp(m0 - n0)
-        a1 = jnp.exp(m1 - n1)
-        p0 = jnp.exp(s0 - n0)
-        p1 = jnp.exp(s1 - n1)
-        l0 = l0 * a0 + jnp.sum(p0, axis=0, keepdims=True)
-        l1 = l1 * a1 + jnp.sum(p1, axis=0, keepdims=True)
-        vt = vb.T
-        pv0 = jnp.dot(vt, p0.astype(vb.dtype), preferred_element_type=jnp.float32)
-        pv1 = jnp.dot(vt, p1.astype(vb.dtype), preferred_element_type=jnp.float32)
-        acc = acc * jnp.where(first, a0, a1) + jnp.where(first, pv0, pv1)
-        return (n0, n1, l0, l1, acc)
+        m, l, acc = carry
+        s = jnp.dot(kb, both, preferred_element_type=jnp.float32)
+        n = jnp.maximum(m, jnp.max(s, axis=0, keepdims=True))
+        a = jnp.exp(m - n)
+        p = jnp.exp(s - n)
+        l = l * a + jnp.sum(p, axis=0, keepdims=True)
+        pv = jnp.dot(vb.T, p.astype(vb.dtype), preferred_element_type=jnp.float32)
+        scaled = jnp.where(first, a[:, :rows], a[:, rows:])
+        acc = acc * scaled + jnp.where(first, pv[:, :rows], pv[:, rows:])
+        return (n, l, acc)
 
     init = (
-        jnp.full((1, rows), NEG, jnp.float32),
-        jnp.full((1, rows), NEG, jnp.float32),
-        jnp.zeros((1, rows), jnp.float32),
-        jnp.zeros((1, rows), jnp.float32),
+        jnp.full((1, 2 * rows), NEG, jnp.float32),
+        jnp.zeros((1, 2 * rows), jnp.float32),
         jnp.zeros((width, rows), jnp.float32),
     )
     carry = update(init, k_ref[...], v_ref[...])
@@ -85,8 +76,8 @@
         b = listed_ref[i]
         return update(carry, kv_ref[b, 0], kv_ref[b, 1])
 
-    m0, m1, l0, l1, acc = lax.fori_loop(0, count_ref[0], body, carry)
-    o_ref[...] = (acc / jnp.where(first, l0, l1)).T.astype(o_ref.dtype)
+    m, l, acc = lax.fori_loop(0, count_ref[0], body, carry)
+    o_ref[...] = (acc / jnp.where(first, l[:, :rows], l[:, rows:])).T.astype(o_ref.dtype)
 
 
 def block_attend(allowed, query, keys, values, kv, scale):

time: 179 us -> 179 us (level)
  the two profiles are of different devices: /device:TPU:64 before, /device:TPU:65 now
where the time goes in v12:
time: 179 us; the launch traced here: 178 us
  blocking collectives  55 us (31%)
  waiting for transfers between devices  54.8 us (31%)
  starting transfers between devices  20 us (11%)
  Pallas kernels  15.4 us (9%)
  between operations  14.4 us (8%)
  matrix products  6.88 us (4%)
  local copies, waits for them, and re-layouts  6.31 us (4%)
  other arithmetic  5.67 us (3%)
    all_to_all x1, waiting for transfers between devices, exchange_rows(): lax.all_to_all(spread, SEQ, 1, 1, tiled=False)  33.3 us
    all_to_all x1, blocking collectives, attend(): lax.all_to_all(part.reshape(n_seq, tokens // n_seq, -1), SEQ, 0, 0, tiled...  30.2 us
    all_to_all x1, waiting for transfers between devices, attend(): lax.all_to_all(part.reshape(n_seq, tokens // n_seq, -1), SEQ, 0, 0, tiled...  21.5 us
    pallas_call x2, Pallas kernels, block_attend(): pl.pallas_call(functools.partial(attn_kernel, scale=scale), out_shape=jax...  15.4 us
    all_gather x1, blocking collectives, on_device(): near = lax.all_gather(stale_kv[None], PIPE[1], axis=0, tiled=True)  14.8 us
    all_to_all x1, starting transfers between devices, exchange_rows(): lax.all_to_all(spread, SEQ, 1, 1, tiled=False)  12.6 us
    all_gather x1, blocking collectives, gather_pipe(): piece = lax.all_gather(piece, name, axis=0, tiled=True)  10 us
    all_to_all x1, starting transfers between devices, attend(): lax.all_to_all(part.reshape(n_seq, tokens // n_seq, -1), SEQ, 0, 0, tiled...  7.31 us
  transfers between devices with their start and end apart: 4, of which 2 were waited for; matrix products, arithmetic and copies ran while one was open for 9% of the time, Pallas kernels for 4%

profile of v12, /device:TPU:65, one launch (start us, length us, event | category | flops | bytes accessed | tf_op | source)
XLA Modules:
  0.0 178.4 jit_solution(18296845749092563250)
XLA Ops:
  7.2 0.0 copy-start
  7.2 0.0 all-gather.5.cloned.1.call-start
  7.2 14.8 %all-gather = bf16[8,128,128]{2,1,0:T(8,128)(2,1)} all-gather(bf16[2,128,128]{2,1,0:T(8,128)(2,1)} %param.12), channel_id=2, replica_groups=mesh['y'=8,'zl'=4,'zh'=2,'x'=4,'c'=2] {'zl'}, dimensions={0}, use_global_device_ids=true | all-gather | bytes 327680 | tf_op jit(solution)/shard_map/all_gather | solution.py:118
  22.0 0.8 pad_maximum_fusion
  22.8 0.0 all-gather.5.cloned.1.call-update
  22.9 1.2 broadcast_in_dim.7
  24.1 12.6 %all-to-all-start = ((bf16[2,16,8,2560]{3,2,0,1:T(8,128)(2,1)}), bf16[2,16,8,2560]{3,2,0,1:T(8,128)(2,1)}, u32[]{:S(2)}, u32[]{:S(2)}) async-start(bf16[2,16,8,2560]{3,2,0,1:T(8,128)(2,1)} %broadcast_in_dim.7), calls=%async_computation | async-start | bytes 2621440 | tf_op jit(solution)/shard_map/all_to_all | solution.py:124
  36.7 0.0 all-gather.7.cloned.1.call-start
  36.7 0.0 copy-start.1
  36.7 0.0 copy-start.4
  36.8 2.7 %copy.46 = bf16[3,2560,128]{1,2,0:T(8,128)(2,1)S(1)} copy(bf16[3,2560,128]{2,1,0:T(8,128)(2,1)} %param.13) | data formatting | bytes 3932160 | tf_op args[3]
  39.4 0.0 copy-start.2
  39.5 0.0 copy-done.1
  39.5 0.1 copy.45
  39.5 0.0 copy-done.4
  39.5 0.1 iota_compare_fusion.1
  39.6 0.2 convert_reduce_fusion
  39.9 33.3 %all-to-all-done = bf16[2,16,8,2560]{3,2,0,1:T(8,128)(2,1)} async-done(((bf16[2,16,8,2560]{3,2,0,1:T(8,128)(2,1)}), bf16[2,16,8,2560]{3,2,0,1:T(8,128)(2,1)}, u32[]{:S(2)}, u32[]{:S(2)}) %all-to-all-start) | async-done | bytes 1310752 | tf_op jit(solution)/shard_map/all_to_all | solution.py:124
  73.1 0.0 copy-start.5
  73.1 1.8 fusion.3
  74.9 0.1 copy.47
  75.0 0.1 copy.50
  75.2 0.1 copy.52
  75.3 0.0 copy-done.2
  75.3 10.0 %all-gather.1 = bf16[8,128,128]{2,1,0:T(8,128)(2,1)} all-gather(bf16[2,128,128]{2,1,0:T(8,128)(2,1)S(1)} %pad_maximum_fusion.1), channel_id=3, replica_groups=mesh['y'=8,'zl'=4,'zh'=2,'x'=4,'c'=2] {'zl'}, dimensions={0}, use_global_device_ids=true | all-gather | bytes 327680 | tf_op jit(solution)/shard_map/all_gather | solution.py:98
  85.4 0.0 all-gather.7.cloned.1.call-update
  85.4 0.0 copy-done.5
  85.4 0.2 fusion.15
  85.6 0.2 fusion.14
  85.8 1.6 sort.19
  87.5 0.6 convert_reduce_fusion.1
  88.1 0.1 copy.48
  88.3 0.1 copy.49
  88.4 0.1 copy.51
  88.5 0.0 copy-start.3
  88.5 1.8 fusion.2
  90.2 0.1 copy.54
  90.4 0.1 copy.55
  90.5 0.1 copy.56
  90.6 0.1 copy.57
  90.8 0.1 copy.58
  90.9 0.6 slice_bitcast_fusion.4.v_ref
  91.5 0.0 copy-done.3
  91.5 0.7 fusion.10
  92.2 0.0 all-gather.5.cloned.1.call-done.kv_ref
  92.2 7.7 %shard_map.113 = bf16[128,128]{1,0:T(8,128)(2,1)} custom-call(s32[1]{0:T(128)} %bitcast.count_ref, s32[32]{0:T(128)} %get-tuple-element.7.listed_ref, bf16[128,128]{1,0:T(8,128)(2,1)} %get-tuple-element.21.q_ref, bf16[128,128]{1,0:T(8,128)(2,1)} %get-tuple-element.20.k_ref, bf16[128,128]{1,0:T(8,128)(2,1)} %slice_bitcast_fusion.4.v_ref, ...), custom_call_target="tpu_custom_call" | custom-call | tf_op jit(solution)/shard_map/pallas_call | solution.py:88
  99.9 0.0 copy-done
  99.9 1.9 %fusion = bf16[16,8,2560]{2,1,0:T(8,128)(2,1)} fusion(bf16[128,128]{1,0:T(8,128)(2,1)} %shard_map.113, bf16[128,2560]{1,0:T(8,128)(2,1)S(1)} %copy-done), kind=kOutput, calls=%fused_computation.2 | convolution fusion | flops 84213760 | bytes 1343488 | tf_op jit(solution)/shard_map/dot_general | solution.py:141
  101.8 7.3 %all-to-all-start.1 = ((bf16[16,8,2560]{2,1,0:T(8,128)(2,1)}), bf16[16,8,2560]{2,1,0:T(8,128)(2,1)S(1)}, u32[]{:S(2)}, u32[]{:S(2)}) async-start(bf16[16,8,2560]{2,1,0:T(8,128)(2,1)} %fusion), calls=%async_computation.1 | async-start | bytes 1310720 | tf_op jit(solution)/shard_map/all_to_all | solution.py:142
  109.1 0.6 fusion.13.v_ref
  109.7 21.5 %all-to-all-done.1 = bf16[16,8,2560]{2,1,0:T(8,128)(2,1)S(1)} async-done(((bf16[16,8,2560]{2,1,0:T(8,128)(2,1)}), bf16[16,8,2560]{2,1,0:T(8,128)(2,1)S(1)}, u32[]{:S(2)}, u32[]{:S(2)}) %all-to-all-start.1) | async-done | bytes 655392 | tf_op jit(solution)/shard_map/all_to_all | solution.py:142
  131.2 0.7 reduce_sum.86
  131.9 0.0 all-gather.7.cloned.1.call-done.kv_ref
  131.9 7.7 %shard_map.114 = bf16[128,128]{1,0:T(8,128)(2,1)} custom-call(s32[1]{0:T(128)} %bitcast.count_ref, s32[32]{0:T(128)} %get-tuple-element.7.listed_ref, bf16[128,128]{1,0:T(8,128)(2,1)} %get-tuple-element.22.q_ref, bf16[128,128]{1,0:T(8,128)(2,1)} %get-tuple-element.23.k_ref, bf16[128,128]{1,0:T(8,128)(2,1)} %fusion.13.v_ref, ...), custom_call_target="tpu_custom_call" | custom-call | tf_op jit(solution)/shard_map/pallas_call | solution.py:88
  139.6 1.1 fusion.1
  140.7 30.2 %all_to_all.15 = bf16[16,8,2560]{2,1,0:T(8,128)(2,1)S(1)} all-to-all(bf16[16,8,2560]{2,1,0:T(8,128)(2,1)S(1)} %fusion.1), channel_id=1, replica_groups=mesh['y'=8,'zl'=4,'zh'=2,'x'=4,'c'=2] {'zh','x','c'}, dimensions={0} | all-to-all | bytes 1310720 | tf_op jit(solution)/shard_map/all_to_all | solution.py:142
  170.9 0.7 reduce_sum.89
  (19 shorter events, 0.2 us)
Async XLA Ops:
  7.2 92.7 %copy-start = (bf16[128,2560]{1,0:T(8,128)(2,1)S(1)}, bf16[128,2560]{1,0:T(8,128)(2,1)}, u32[]{:S(2)}) copy-start(bf16[128,2560]{1,0:T(8,128)(2,1)} %param.14) | copy-start | bytes 1966084
  7.2 85.0 %all-gather.5.cloned.1.call-start = ((), (), s32[]{:S(2)}) async-start(), calls=%async_computation.3 | async-start | bytes 2359296 | tf_op jit(solution)/shard_map/all_gather | solution.py:120
  24.1 49.1 %all-to-all-start = ((bf16[2,16,8,2560]{3,2,0,1:T(8,128)(2,1)}), bf16[2,16,8,2560]{3,2,0,1:T(8,128)(2,1)}, u32[]{:S(2)}, u32[]{:S(2)}) async-start(bf16[2,16,8,2560]{3,2,0,1:T(8,128)(2,1)} %broadcast_in_dim.7), calls=%async_computation | async-start | bytes 2621440 | tf_op jit(solution)/shard_map/all_to_all | solution.py:124
  36.7 95.2 %all-gather.7.cloned.1.call-start = ((), (), s32[]{:S(2)}) async-start(), calls=%async_computation.4 | async-start | bytes 2359296 | tf_op jit(solution)/shard_map/all_gather | solution.py:98
  36.7 2.7 %copy-start.1 = (s32[32,16]{0,1:T(8,128)S(1)}, s32[32,16]{0,1:T(8,128)}, u32[]{:S(2)}) copy-start(s32[32,16]{0,1:T(8,128)} %param.17) | copy-start | bytes 6148
  36.7 2.8 %copy-start.4 = (s32[32]{0:T(128)S(1)}, s32[32]{0:T(128)}, u32[]{:S(2)}) copy-start(s32[32]{0:T(128)} %param.18) | copy-start | bytes 388
  39.4 35.9 %copy-start.2 = (f32[128]{0:T(128)S(1)}, f32[128]{0:T(128)}, u32[]{:S(2)}) copy-start(f32[128]{0:T(128)} %param.16) | copy-start | bytes 1540
  73.1 12.3 %copy-start.5 = (s32[32]{0:T(128)S(1)}, s32[32]{0:T(128)}, u32[]{:S(2)}) copy-start(s32[32]{0:T(128)} %param.19) | copy-start | bytes 388
  88.5 3.0 %copy-start.3 = (f32[128]{0:T(128)S(1)}, f32[128]{0:T(128)}, u32[]{:S(2)}) copy-start(f32[128]{0:T(128)} %param.15) | copy-start | bytes 1540
  101.8 29.4 %all-to-all-start.1 = ((bf16[16,8,2560]{2,1,0:T(8,128)(2,1)}), bf16[16,8,2560]{2,1,0:T(8,128)(2,1)S(1)}, u32[]{:S(2)}, u32[]{:S(2)}) async-start(bf16[16,8,2560]{2,1,0:T(8,128)(2,1)} %fusion), calls=%async_computation.1 | async-start | bytes 1310720 | tf_op jit(solution)/shard_map/all_to_all | solution.py:142
Sparse Core Ops, SparseCore 0:
  23.0 44.0 all-gather.4
  85.5 40.4 all-gather.6

commit v13 on v8

--- a/solution.py
+++ b/solution.py
@@ -149,7 +149,10 @@
         allowed = remote[0].astype(jnp.int32)
         attn = block_attend(allowed, query, keys, values, kv, scale)
         part = jnp.dot(attn, w_out, preferred_element_type=jnp.float32).astype(jnp.bfloat16)
-        sent = lax.all_to_all(part.reshape(n_seq, tokens // n_seq, -1), SEQ, 0, 0, tiled=False)
+        chip = SEQ_PARTS[-1][1]
+        split = part.reshape(n_seq // chip, chip, tokens // n_seq, -1)
+        pair_sum = jnp.sum(lax.all_to_all(split, SEQ[-1], 1, 1, tiled=False).astype(jnp.float32), axis=1)
+        sent = lax.all_to_all(pair_sum.astype(jnp.bfloat16), SEQ[:-1], 0, 0, tiled=False)
         return jnp.sum(sent.astype(jnp.float32), axis=0).astype(jnp.bfloat16)
 
     out_first = attend(q1, k1, v1, stale, remote)

time: 178 us -> 176 us (0.989)
  waiting for transfers between devices: 46.9 us -> 38.9 us
  blocking collectives: 66.2 us -> 70.4 us
  Pallas kernels: 12.6 us -> 16.6 us
  starting transfers between devices: 19.6 us -> 16.1 us
    all_to_all x1, waiting for transfers between devices: 19.2 us -> 9.75 us  [attend(): lax.all_to_all(pair_sum.astype(jnp.bfloat16), SEQ[:-1], 0, 0, tiled=False)]
    all_to_all x1 -> x3, blocking collectives: 32.4 us -> 36.6 us  [the longest x1 20.6 us: attend(): lax.all_to_all(pair_sum.astype(jnp.bfloat16), SEQ[:-1], 0, 0, tiled=False)]
    pallas_call x2, Pallas kernels: 12.6 us -> 16.6 us  [block_attend(): pl.pallas_call(functools.partial(attn_kernel, scale=scale, n_blocks=n_blo...]
    all_to_all x1, starting transfers between devices: 7 us -> 3.43 us  [attend(): lax.all_to_all(pair_sum.astype(jnp.bfloat16), SEQ[:-1], 0, 0, tiled=False)]
  transfers between devices with their start and end apart: 4 -> 4, of which waited for: 2 -> 3; matrix products, arithmetic and copies ran while one was open for 8% -> 8% of each run, Pallas kernels for 4% -> 5%
where the time goes in v13:
time: 176 us; the launch traced here: 174 us
  blocking collectives  70.4 us (40%)
  waiting for transfers between devices  38.9 us (22%)
  Pallas kernels  16.6 us (9%)
  starting transfers between devices  16.1 us (9%)
  between operations  14.4 us (8%)
  local copies, waits for them, and re-layouts  6.39 us (4%)
  matrix products  6.06 us (3%)
  other arithmetic  4.95 us (3%)
    all_to_all x1, waiting for transfers between devices, exchange_rows(): lax.all_to_all(spread, SEQ, 1, 1, tiled=False)  27.8 us
    all_to_all x1, blocking collectives, attend(): lax.all_to_all(pair_sum.astype(jnp.bfloat16), SEQ[:-1], 0, 0, tiled=False)  20.6 us
    all_gather x1, blocking collectives, on_device(): near = lax.all_gather(stale_kv[None], PIPE[1], axis=0, tiled=True)  17.5 us
    pallas_call x2, Pallas kernels, block_attend(): pl.pallas_call(functools.partial(attn_kernel, scale=scale, n_blocks=n_blo...  16.6 us
    all_gather x1, blocking collectives, gather_pipe(): piece = lax.all_gather(piece, name, axis=0, tiled=True)  16.2 us
    all_to_all x2, blocking collectives, attend(): lax.all_to_all(split, SEQ[-1], 1, 1, tiled=False).astype(jnp.float32)  16 us
    all_to_all x1, starting transfers between devices, exchange_rows(): lax.all_to_all(spread, SEQ, 1, 1, tiled=False)  12.6 us
    all_to_all x1, waiting for transfers between devices, attend(): lax.all_to_all(pair_sum.astype(jnp.bfloat16), SEQ[:-1], 0, 0, tiled=False)  9.75 us
  transfers between devices with their start and end apart: 4, of which 3 were waited for; matrix products, arithmetic and copies ran while one was open for 8% of the time, Pallas kernels for 5%

profile of v13, /device:TPU:1, one launch (start us, length us, event | category | flops | bytes accessed | tf_op | source)
XLA Modules:
  0.0 173.8 jit_solution(1953402972109885867)
XLA Ops:
  7.2 0.0 copy-start
  7.2 0.0 all-gather.5.cloned.1.call-start
  7.2 17.5 %all-gather = bf16[8,128,128]{2,1,0:T(8,128)(2,1)} all-gather(bf16[2,128,128]{2,1,0:T(8,128)(2,1)} %param.12), channel_id=2, replica_groups=mesh['y'=8,'zl'=4,'zh'=2,'x'=4,'c'=2] {'zl'}, dimensions={0}, use_global_device_ids=true | all-gather | bytes 327680 | tf_op jit(solution)/shard_map/all_gather | solution.py:127
  24.8 0.8 pad_maximum_fusion
  25.6 0.0 all-gather.5.cloned.1.call-update
  25.6 1.2 broadcast_in_dim.7
  26.8 12.6 %all-to-all-start = ((bf16[2,16,8,2560]{3,2,0,1:T(8,128)(2,1)}), bf16[2,16,8,2560]{3,2,0,1:T(8,128)(2,1)}, u32[]{:S(2)}, u32[]{:S(2)}) async-start(bf16[2,16,8,2560]{3,2,0,1:T(8,128)(2,1)} %broadcast_in_dim.7), calls=%async_computation | async-start | bytes 2621440 | tf_op jit(solution)/shard_map/all_to_all | solution.py:133
  39.4 0.0 all-gather.7.cloned.1.call-start
  39.4 2.7 %copy.48 = bf16[3,2560,128]{1,2,0:T(8,128)(2,1)S(1)} copy(bf16[3,2560,128]{2,1,0:T(8,128)(2,1)} %param.13) | data formatting | bytes 3932160 | tf_op args[3]
  42.1 0.0 copy-start.2
  42.1 27.8 %all-to-all-done = bf16[2,16,8,2560]{3,2,0,1:T(8,128)(2,1)} async-done(((bf16[2,16,8,2560]{3,2,0,1:T(8,128)(2,1)}), bf16[2,16,8,2560]{3,2,0,1:T(8,128)(2,1)}, u32[]{:S(2)}, u32[]{:S(2)}) %all-to-all-start) | async-done | bytes 1310752 | tf_op jit(solution)/shard_map/all_to_all | solution.py:133
  69.9 0.0 copy-start.1
  69.9 0.0 copy-start.4
  69.9 0.0 copy-start.5
  69.9 1.8 %fusion.1 = f32[128,384]{0,1:S(1)} fusion(bf16[2560,384]{0,1:T(8,128)(2,1)S(1)} %bitcast.68, bf16[2,16,8,2560]{3,2,0,1:T(8,128)(2,1)} %all-to-all-done), kind=kOutput, calls=%fused_computation.5 | convolution fusion | flops 251658240 | bytes 2818048
  71.7 0.1 copy.49
  71.9 0.1 copy.52
  72.0 0.1 copy.55
  72.1 0.0 copy-done.2
  72.2 16.2 %all-gather.1 = bf16[8,128,128]{2,1,0:T(8,128)(2,1)} all-gather(bf16[2,128,128]{2,1,0:T(8,128)(2,1)S(1)} %pad_maximum_fusion.1), channel_id=3, replica_groups=mesh['y'=8,'zl'=4,'zh'=2,'x'=4,'c'=2] {'zl'}, dimensions={0}, use_global_device_ids=true | all-gather | bytes 327680 | tf_op jit(solution)/shard_map/all_gather | solution.py:107
  88.4 0.0 all-gather.7.cloned.1.call-update
  88.4 0.0 copy-done.1
  88.4 0.1 copy.47
  88.5 0.0 copy-done.4
  88.5 0.1 iota_compare_fusion.1
  88.6 0.2 convert_reduce_fusion
  88.8 0.0 copy-done.5
  88.8 0.2 fusion.13
  89.0 0.2 fusion.12
  89.2 0.6 fusion.16.allowed_ref
  89.7 0.1 copy.50
  89.9 0.1 copy.51
  90.0 0.1 copy.53
  90.1 0.0 copy-start.3
  90.1 1.8 %fusion = f32[128,384]{0,1:S(1)} fusion(bf16[2560,384]{0,1:T(8,128)(2,1)S(1)} %bitcast.69, bf16[2,16,8,2560]{3,2,0,1:T(8,128)(2,1)} %all-to-all-done), kind=kOutput, calls=%fused_computation.3 | convolution fusion | flops 251658240 | bytes 2818048
  91.9 0.1 copy.57
  92.0 0.1 copy.58
  92.2 0.1 copy.59
  92.3 0.1 copy.60
  92.4 0.1 copy.61
  92.5 0.6 slice_bitcast_fusion.4.v_ref
  93.1 0.0 copy-done.3
  93.1 0.7 fusion.8
  93.8 0.0 all-gather.5.cloned.1.call-done.kv_ref
  93.8 8.3 %shard_map.113 = bf16[128,128]{1,0:T(8,128)(2,1)} custom-call(s32[32]{0:T(128)} %fusion.16.allowed_ref, bf16[128,128]{1,0:T(8,128)(2,1)} %get-tuple-element.17.q_ref, bf16[128,128]{1,0:T(8,128)(2,1)} %get-tuple-element.16.k_ref, bf16[128,128]{1,0:T(8,128)(2,1)} %slice_bitcast_fusion.4.v_ref, bf16[32,2,128,128]{3,2,1,0:T(8,128)(2,1)} %all-gather.5.cloned.1.call-done.kv_ref), custom_call_target="tpu_custom_call" | custom-call | tf_op jit(solution)/shard_map/pallas_call | solution.py:97
  102.1 0.0 copy-done
  102.1 1.1 convolution_convert_fusion.1
  103.2 7.5 %all_to_all.25 = bf16[8,2,8,2560]{3,2,0,1:T(8,128)(2,1)S(1)} all-to-all(bf16[8,2,8,2560]{3,2,0,1:T(8,128)(2,1)S(1)} %copy.54), channel_id=1, replica_groups=mesh['y'=8,'zl'=4,'zh'=2,'x'=4,'c'=2] {'c'}, dimensions={1} | all-to-all | bytes 1310720 | tf_op jit(solution)/shard_map/all_to_all | solution.py:154
  110.7 0.9 reduce_sum.96
  111.7 3.4 %all-to-all-start.2 = ((bf16[8,8,2560]{2,1,0:T(8,128)(2,1)}), bf16[8,8,2560]{2,1,0:T(8,128)(2,1)S(1)}, u32[]{:S(2)}, u32[]{:S(2)}) async-start(bf16[8,8,2560]{2,1,0:T(8,128)(2,1)} %reduce_sum.96), calls=%async_computation.2 | async-start | bytes 655360 | tf_op jit(solution)/shard_map/all_to_all | solution.py:155
  115.1 0.6 fusion.11.v_ref
  115.7 9.8 %all-to-all-done.2 = bf16[8,8,2560]{2,1,0:T(8,128)(2,1)S(1)} async-done(((bf16[8,8,2560]{2,1,0:T(8,128)(2,1)}), bf16[8,8,2560]{2,1,0:T(8,128)(2,1)S(1)}, u32[]{:S(2)}, u32[]{:S(2)}) %all-to-all-start.2) | async-done | bytes 327712 | tf_op jit(solution)/shard_map/all_to_all | solution.py:155
  125.5 0.7 reduce_sum.97
  126.2 1.3 all-gather.7.cloned.1.call-done.kv_ref
  127.5 8.3 %shard_map.114 = bf16[128,128]{1,0:T(8,128)(2,1)} custom-call(s32[32]{0:T(128)} %fusion.16.allowed_ref, bf16[128,128]{1,0:T(8,128)(2,1)} %get-tuple-element.18.q_ref, bf16[128,128]{1,0:T(8,128)(2,1)} %get-tuple-element.19.k_ref, bf16[128,128]{1,0:T(8,128)(2,1)} %fusion.11.v_ref, bf16[32,2,128,128]{3,2,1,0:T(8,128)(2,1)} %all-gather.7.cloned.1.call-done.kv_ref), custom_call_target="tpu_custom_call" | custom-call | tf_op jit(solution)/shard_map/pallas_call | solution.py:97
  135.8 1.1 convolution_convert_fusion
  136.9 8.5 %all_to_all.26 = bf16[8,2,8,2560]{3,2,0,1:T(8,128)(2,1)S(1)} all-to-all(bf16[8,2,8,2560]{3,2,0,1:T(8,128)(2,1)S(1)} %copy.62), channel_id=1, replica_groups=mesh['y'=8,'zl'=4,'zh'=2,'x'=4,'c'=2] {'c'}, dimensions={1} | all-to-all | bytes 1310720 | tf_op jit(solution)/shard_map/all_to_all | solution.py:154
  145.4 0.2 reduce_sum.100
  145.6 20.6 %all_to_all.27 = bf16[8,8,2560]{2,1,0:T(8,128)(2,1)S(1)} all-to-all(bf16[8,8,2560]{2,1,0:T(8,128)(2,1)S(1)} %reduce_sum.100), channel_id=1, replica_groups=mesh['y'=8,'zl'=4,'zh'=2,'x'=4,'c'=2] {'zh','x'}, dimensions={0} | all-to-all | bytes 655360 | tf_op jit(solution)/shard_map/all_to_all | solution.py:155
  166.3 0.7 reduce_sum.101
  (19 shorter events, 0.3 us)
Async XLA Ops:
  7.2 94.9 %copy-start = (bf16[128,2560]{1,0:T(8,128)(2,1)S(1)}, bf16[128,2560]{1,0:T(8,128)(2,1)}, u32[]{:S(2)}) copy-start(bf16[128,2560]{1,0:T(8,128)(2,1)} %param.14) | copy-start | bytes 1966084
  7.2 86.6 %all-gather.5.cloned.1.call-start = ((), (), s32[]{:S(2)}) async-start(), calls=%async_computation.5 | async-start | bytes 2359296 | tf_op jit(solution)/shard_map/all_gather | solution.py:129
  26.8 43.1 %all-to-all-start = ((bf16[2,16,8,2560]{3,2,0,1:T(8,128)(2,1)}), bf16[2,16,8,2560]{3,2,0,1:T(8,128)(2,1)}, u32[]{:S(2)}, u32[]{:S(2)}) async-start(bf16[2,16,8,2560]{3,2,0,1:T(8,128)(2,1)} %broadcast_in_dim.7), calls=%async_computation | async-start | bytes 2621440 | tf_op jit(solution)/shard_map/all_to_all | solution.py:133
  39.4 88.1 %all-gather.7.cloned.1.call-start = ((), (), s32[]{:S(2)}) async-start(), calls=%async_computation.6 | async-start | bytes 2359296 | tf_op jit(solution)/shard_map/all_gather | solution.py:107
  42.1 30.0 %copy-start.2 = (f32[128]{0:T(128)S(1)}, f32[128]{0:T(128)}, u32[]{:S(2)}) copy-start(f32[128]{0:T(128)} %param.16) | copy-start | bytes 1540
  69.9 18.5 %copy-start.1 = (s32[32,16]{0,1:T(8,128)S(1)}, s32[32,16]{0,1:T(8,128)}, u32[]{:S(2)}) copy-start(s32[32,16]{0,1:T(8,128)} %param.17) | copy-start | bytes 6148
  69.9 18.6 %copy-start.4 = (s32[32]{0:T(128)S(1)}, s32[32]{0:T(128)}, u32[]{:S(2)}) copy-start(s32[32]{0:T(128)} %param.18) | copy-start | bytes 388
  69.9 18.9 %copy-start.5 = (s32[32]{0:T(128)S(1)}, s32[32]{0:T(128)}, u32[]{:S(2)}) copy-start(s32[32]{0:T(128)} %param.19) | copy-start | bytes 388
  90.1 3.0 %copy-start.3 = (f32[128]{0:T(128)S(1)}, f32[128]{0:T(128)}, u32[]{:S(2)}) copy-start(f32[128]{0:T(128)} %param.15) | copy-start | bytes 1540
  111.7 13.8 %all-to-all-start.2 = ((bf16[8,8,2560]{2,1,0:T(8,128)(2,1)}), bf16[8,8,2560]{2,1,0:T(8,128)(2,1)S(1)}, u32[]{:S(2)}, u32[]{:S(2)}) async-start(bf16[8,8,2560]{2,1,0:T(8,128)(2,1)} %reduce_sum.96), calls=%async_computation.2 | async-start | bytes 655360 | tf_op jit(solution)/shard_map/all_to_all | solution.py:155
Sparse Core Ops, SparseCore 0:
  25.7 42.9 all-gather.4
  88.5 38.9 all-gather.6

commit v14 on v8

--- a/solution.py
+++ b/solution.py
@@ -128,9 +128,14 @@
     pair, near = lax.optimization_barrier((jnp.stack([x_first, x_second]), near))
     stale = lax.all_gather(near, PIPE[0], axis=0, tiled=True)
 
+    chip = SEQ_PARTS[-1][1]
+
     def exchange_rows(x):
-        spread = jnp.broadcast_to(x[:, None], (x.shape[0], n_seq) + x.shape[1:])
-        return lax.all_to_all(spread, SEQ, 1, 1, tiled=False).reshape(x.shape[0], tokens, -1)
+        steps = x.shape[0]
+        spread = jnp.broadcast_to(x[:, None], (steps, n_seq // chip) + x.shape[1:])
+        among = lax.all_to_all(spread, SEQ[:-1], 1, 1, tiled=False)
+        spread = jnp.broadcast_to(among[:, None], (steps, chip) + among.shape[1:])
+        return lax.all_to_all(spread, SEQ[-1], 1, 1, tiled=False).reshape(steps, tokens, -1)
 
     def project(x):
         raw = jnp.einsum("rd,cdh->crh", x, w_qkv, preferred_element_type=jnp.float32)
@@ -149,7 +154,9 @@
         allowed = remote[0].astype(jnp.int32)
         attn = block_attend(allowed, query, keys, values, kv, scale)
         part = jnp.dot(attn, w_out, preferred_element_type=jnp.float32).astype(jnp.bfloat16)
-        sent = lax.all_to_all(part.reshape(n_seq, tokens // n_seq, -1), SEQ, 0, 0, tiled=False)
+        split = part.reshape(chip, n_seq // chip, tokens // n_seq, -1)
+        pair_sum = jnp.sum(lax.all_to_all(split, SEQ[-1], 0, 0, tiled=False).astype(jnp.float32), axis=0)
+        sent = lax.all_to_all(pair_sum.astype(jnp.bfloat16), SEQ[:-1], 0, 0, tiled=False)
         return jnp.sum(sent.astype(jnp.float32), axis=0).astype(jnp.bfloat16)
 
     out_first = attend(q1, k1, v1, stale, remote)

time: 178 us -> 167 us (0.938); the launches traced: 177 us -> 163 us
  waiting for transfers between devices: 46.9 us -> 19.6 us
  local copies, waits for them, and re-layouts: 6.31 us -> 15 us
  starting transfers between devices: 19.6 us -> 12.7 us
  other arithmetic: 3.92 us -> 10.1 us
  blocking collectives: 66.2 us -> 71.9 us
    all_to_all x2, waiting for transfers between devices: 46.8 us -> 19.6 us  [the longest x1 10 us: attend(): lax.all_to_all(pair_sum.astype(jnp.bfloat16), SEQ[:-1], 0, 0, tiled=False)]
    all_to_all x1 -> x4, blocking collectives: 32.4 us -> 41.2 us  [the longest x1 15.7 us: attend(): lax.all_to_all(pair_sum.astype(jnp.bfloat16), SEQ[:-1], 0, 0, tiled=False)]
    all_to_all x2, starting transfers between devices: 19.6 us -> 12.6 us  [the longest x1 9.19 us: exchange_rows(): among = lax.all_to_all(spread, SEQ[:-1], 1, 1, tiled=False)]
    mul x9, local copies, waits for them, and re-layouts: 0.47 us -> 3.81 us  [normalize(): return (grid * factor).reshape(count, -1) * gain[None, :]]
    all_gather x1, blocking collectives: 16.2 us -> 13.1 us  [gather_pipe(): piece = lax.all_gather(piece, name, axis=0, tiled=True)]
    mul x4, local copies, waits for them, and re-layouts: 0.36 us -> 2.66 us  [normalize(): factor = lax.rsqrt(jnp.mean(grid * grid, axis=2, keepdims=True) + 1e-06)]
    convert_element_type x2, other arithmetic: 0.68 us -> 2.97 us  [project(): keys = normalize(raw[1], k_gain, HS).astype(jnp.bfloat16)]
    dot_general x2, local copies, waits for them, and re-layouts: 0.26 us -> 2.11 us  [project(): jnp.einsum('rd,cdh->crh', x, w_qkv, preferred_element_type=jnp.float32)]
  transfers between devices with their start and end apart: 4 -> 4, of which waited for: 2 -> 2; matrix products, arithmetic and copies ran while one was open for 8% -> 18% of each run, Pallas kernels for 4% -> 4%
where the time goes in v14:
time: 167 us; the launch traced here: 163 us
  blocking collectives  71.9 us (43%)
  waiting for transfers between devices  19.6 us (12%)
  local copies, waits for them, and re-layouts  15 us (9%)
  between operations  14.2 us (9%)
  Pallas kernels  13.3 us (8%)
  starting transfers between devices  12.7 us (8%)
  other arithmetic  10.1 us (6%)
  matrix products  6.53 us (4%)
    all_gather x1, blocking collectives, on_device(): near = lax.all_gather(stale_kv[None], PIPE[1], axis=0, tiled=True)  17.6 us
    all_to_all x1, blocking collectives, attend(): lax.all_to_all(pair_sum.astype(jnp.bfloat16), SEQ[:-1], 0, 0, tiled=False)  15.7 us
    all_to_all x2, blocking collectives, attend(): lax.all_to_all(split, SEQ[-1], 0, 0, tiled=False).astype(jnp.float32)  14 us
    pallas_call x2, Pallas kernels, block_attend(): pl.pallas_call(functools.partial(attn_kernel, scale=scale, n_blocks=n_blo...  13.3 us
    all_gather x1, blocking collectives, gather_pipe(): piece = lax.all_gather(piece, name, axis=0, tiled=True)  13.1 us
    all_to_all x1, blocking collectives, exchange_rows(): lax.all_to_all(spread, SEQ[-1], 1, 1, tiled=False)  11.6 us
    all_to_all x1, waiting for transfers between devices, attend(): lax.all_to_all(pair_sum.astype(jnp.bfloat16), SEQ[:-1], 0, 0, tiled=False)  10 us
    all_to_all x1, waiting for transfers between devices, exchange_rows(): among = lax.all_to_all(spread, SEQ[:-1], 1, 1, tiled=False)  9.57 us
  transfers between devices with their start and end apart: 4, of which 2 were waited for; matrix products, arithmetic and copies ran while one was open for 18% of the time, Pallas kernels for 4%

profile of v14, /device:TPU:1, one launch (start us, length us, event | category | flops | bytes accessed | tf_op | source)
XLA Modules:
  0.0 163.4 jit_solution(18340094395630488027)
XLA Ops:
  7.2 0.0 copy-start
  7.2 0.0 all-gather.5.cloned.1.call-start
  7.2 17.6 %all-gather = bf16[8,128,128]{2,1,0:T(8,128)(2,1)} all-gather(bf16[2,128,128]{2,1,0:T(8,128)(2,1)} %param.12), channel_id=2, replica_groups=mesh['y'=8,'zl'=4,'zh'=2,'x'=4,'c'=2] {'zl'}, dimensions={0}, use_global_device_ids=true | all-gather | bytes 327680 | tf_op jit(solution)/shard_map/all_gather | solution.py:127
  24.8 0.8 pad_maximum_fusion
  25.6 0.0 all-gather.5.cloned.1.call-update
  25.6 0.9 broadcast_in_dim.9
  26.5 9.2 %all-to-all-start = ((bf16[2,8,8,2560]{3,2,0,1:T(8,128)(2,1)}), bf16[2,8,8,2560]{3,2,0,1:T(8,128)(2,1)S(1)}, u32[]{:S(2)}, u32[]{:S(2)}) async-start(bf16[2,8,8,2560]{3,2,0,1:T(8,128)(2,1)} %broadcast_in_dim.9), calls=%async_computation | async-start | bytes 1310720 | tf_op jit(solution)/shard_map/all_to_all | solution.py:136
  35.7 0.0 all-gather.7.cloned.1.call-start
  35.7 2.7 %copy.48 = bf16[3,2560,128]{1,2,0:T(8,128)(2,1)S(1)} copy(bf16[3,2560,128]{2,1,0:T(8,128)(2,1)} %param.13) | data formatting | bytes 3932160 | tf_op args[3]
  38.4 9.6 %all-to-all-done = bf16[2,8,8,2560]{3,2,0,1:T(8,128)(2,1)S(1)} async-done(((bf16[2,8,8,2560]{3,2,0,1:T(8,128)(2,1)}), bf16[2,8,8,2560]{3,2,0,1:T(8,128)(2,1)S(1)}, u32[]{:S(2)}, u32[]{:S(2)}) %all-to-all-start) | async-done | bytes 655392 | tf_op jit(solution)/shard_map/all_to_all | solution.py:136
  48.0 0.1 broadcast_in_dim.10
  48.1 11.6 %all_to_all.30 = bf16[2,2,8,8,2560]{4,3,2,0,1:T(8,128)(2,1)S(1)} all-to-all(bf16[2,2,8,8,2560]{4,3,2,0,1:T(8,128)(2,1)S(1)} %broadcast_in_dim.10), channel_id=1, replica_groups=mesh['y'=8,'zl'=4,'zh'=2,'x'=4,'c'=2] {'c'}, dimensions={1} | all-to-all | bytes 2621440 | tf_op jit(solution)/shard_map/all_to_all | solution.py:138
  59.7 0.1 fusion.15
  59.8 0.0 copy-start.2
  59.8 1.4 fusion.16
  61.2 1.1 copy.49
  62.2 0.6 slice.56
  62.9 0.6 slice_multiply_fusion.3
  63.5 0.9 copy.52
  64.5 0.7 copy.54
  65.2 0.0 copy-done.2
  65.2 1.5 multiply_convert_fusion
  66.7 0.8 pad_maximum_fusion.1
  67.4 13.1 %all-gather.1 = bf16[8,128,128]{2,1,0:T(8,128)(2,1)} all-gather(bf16[2,128,128]{2,1,0:T(8,128)(2,1)S(1)} %pad_maximum_fusion.1), channel_id=3, replica_groups=mesh['y'=8,'zl'=4,'zh'=2,'x'=4,'c'=2] {'zl'}, dimensions={0}, use_global_device_ids=true | all-gather | bytes 327680 | tf_op jit(solution)/shard_map/all_gather | solution.py:107
  80.5 0.0 all-gather.7.cloned.1.call-update
  80.6 0.8 copy.46
  81.3 0.7 iota_compare_fusion.1
  82.1 0.2 convert_reduce_fusion
  82.3 0.8 fusion.11
  83.1 0.9 fusion.10
  84.0 0.6 fusion.14.allowed_ref
  84.6 1.6 copy.50
  86.2 0.9 reduce_sum.94
  87.0 0.6 mul.128
  87.7 1.6 copy.51
  89.2 0.7 copy.53
  89.9 0.0 copy-start.1
  89.9 0.0 copy-start.3
  89.9 1.3 fusion.17
  91.3 1.1 copy.56
  92.4 0.1 copy.57
  92.5 0.1 copy.58
  92.6 0.1 copy.59
  92.8 0.1 copy.60
  92.9 0.6 slice_bitcast_fusion.v_ref
  93.5 0.0 copy-done.1
  93.5 0.0 copy-done.3
  93.5 0.0 copy-done.4
  93.5 1.5 fusion.6
  95.0 6.6 %shard_map.113 = bf16[128,128]{1,0:T(8,128)(2,1)} custom-call(s32[32]{0:T(128)} %fusion.14.allowed_ref, bf16[128,128]{1,0:T(8,128)(2,1)} %get-tuple-element.19.q_ref, bf16[128,128]{1,0:T(8,128)(2,1)} %get-tuple-element.18.k_ref, bf16[128,128]{1,0:T(8,128)(2,1)} %slice_bitcast_fusion.v_ref, bf16[32,2,128,128]{3,2,1,0:T(8,128)(2,1)} %all-gather.5.cloned.1.call-done.kv_ref), custom_call_target="tpu_custom_call" | custom-call | tf_op jit(solution)/shard_map/pallas_call | solution.py:97
  101.6 0.0 copy-done
  101.6 1.1 convolution_convert_fusion.1
  102.7 7.0 %all_to_all.31 = bf16[2,8,8,2560]{3,2,1,0:T(8,128)(2,1)S(1)} all-to-all(bf16[2,8,8,2560]{3,2,1,0:T(8,128)(2,1)S(1)} %bitcast.70), channel_id=1, replica_groups=mesh['y'=8,'zl'=4,'zh'=2,'x'=4,'c'=2] {'c'}, dimensions={0} | all-to-all | bytes 1310720 | tf_op jit(solution)/shard_map/all_to_all | solution.py:158
  109.6 0.9 reduce_sum.96
  110.5 3.4 %all-to-all-start.3 = ((bf16[8,8,2560]{2,1,0:T(8,128)(2,1)}), bf16[8,8,2560]{2,1,0:T(8,128)(2,1)S(1)}, u32[]{:S(2)}, u32[]{:S(2)}) async-start(bf16[8,8,2560]{2,1,0:T(8,128)(2,1)} %reduce_sum.96), calls=%async_computation.3 | async-start | bytes 655360 | tf_op jit(solution)/shard_map/all_to_all | solution.py:159
  114.0 0.6 fusion.9.v_ref
  114.6 10.0 %all-to-all-done.3 = bf16[8,8,2560]{2,1,0:T(8,128)(2,1)S(1)} async-done(((bf16[8,8,2560]{2,1,0:T(8,128)(2,1)}), bf16[8,8,2560]{2,1,0:T(8,128)(2,1)S(1)}, u32[]{:S(2)}, u32[]{:S(2)}) %all-to-all-start.3) | async-done | bytes 327712 | tf_op jit(solution)/shard_map/all_to_all | solution.py:159
  124.6 0.7 reduce_sum.97
  125.3 6.6 %shard_map.114 = bf16[128,128]{1,0:T(8,128)(2,1)} custom-call(s32[32]{0:T(128)} %fusion.14.allowed_ref, bf16[128,128]{1,0:T(8,128)(2,1)} %get-tuple-element.20.q_ref, bf16[128,128]{1,0:T(8,128)(2,1)} %get-tuple-element.21.k_ref, bf16[128,128]{1,0:T(8,128)(2,1)} %fusion.9.v_ref, bf16[32,2,128,128]{3,2,1,0:T(8,128)(2,1)} %all-gather.7.cloned.1.call-done.kv_ref), custom_call_target="tpu_custom_call" | custom-call | tf_op jit(solution)/shard_map/pallas_call | solution.py:97
  131.9 1.1 convolution_convert_fusion
  133.0 7.0 %all_to_all.32 = bf16[2,8,8,2560]{3,2,1,0:T(8,128)(2,1)S(1)} all-to-all(bf16[2,8,8,2560]{3,2,1,0:T(8,128)(2,1)S(1)} %bitcast.71), channel_id=1, replica_groups=mesh['y'=8,'zl'=4,'zh'=2,'x'=4,'c'=2] {'c'}, dimensions={0} | all-to-all | bytes 1310720 | tf_op jit(solution)/shard_map/all_to_all | solution.py:158
  140.0 0.2 reduce_sum.100
  140.2 15.7 %all_to_all.33 = bf16[8,8,2560]{2,1,0:T(8,128)(2,1)S(1)} all-to-all(bf16[8,8,2560]{2,1,0:T(8,128)(2,1)S(1)} %reduce_sum.100), channel_id=1, replica_groups=mesh['y'=8,'zl'=4,'zh'=2,'x'=4,'c'=2] {'zh','x'}, dimensions={0} | all-to-all | bytes 655360 | tf_op jit(solution)/shard_map/all_to_all | solution.py:159
  155.9 0.7 reduce_sum.101
  (15 shorter events, 0.2 us)
Async XLA Ops:
  7.2 94.4 %copy-start = (bf16[128,2560]{1,0:T(8,128)(2,1)S(1)}, bf16[128,2560]{1,0:T(8,128)(2,1)}, u32[]{:S(2)}) copy-start(bf16[128,2560]{1,0:T(8,128)(2,1)} %param.14) | copy-start | bytes 1966084
  7.2 87.8 %all-gather.5.cloned.1.call-start = ((), (), s32[]{:S(2)}) async-start(), calls=%async_computation.6 | async-start | bytes 2359296 | tf_op jit(solution)/shard_map/all_gather | solution.py:129
  26.5 21.5 %all-to-all-start = ((bf16[2,8,8,2560]{3,2,0,1:T(8,128)(2,1)}), bf16[2,8,8,2560]{3,2,0,1:T(8,128)(2,1)S(1)}, u32[]{:S(2)}, u32[]{:S(2)}) async-start(bf16[2,8,8,2560]{3,2,0,1:T(8,128)(2,1)} %broadcast_in_dim.9), calls=%async_computation | async-start | bytes 1310720 | tf_op jit(solution)/shard_map/all_to_all | solution.py:136
  35.7 89.6 %all-gather.7.cloned.1.call-start = ((), (), s32[]{:S(2)}) async-start(), calls=%async_computation.7 | async-start | bytes 2359296 | tf_op jit(solution)/shard_map/all_gather | solution.py:107
  59.8 5.4 %copy-start.2 = (f32[128]{0:T(128)S(1)}, f32[128]{0:T(128)}, u32[]{:S(2)}) copy-start(f32[128]{0:T(128)} %param.16) | copy-start | bytes 1540
  89.9 3.5 %copy-start.1 = (f32[128,128]{1,0:T(8,128)S(1)}, f32[128,128]{1,0:T(8,128)}, u32[]{:S(2)}) copy-start(f32[128,128]{1,0:T(8,128)} %copy.51) | copy-start | bytes 196612
  89.9 3.5 %copy-start.3 = (f32[128]{0:T(128)S(1)}, f32[128]{0:T(128)}, u32[]{:S(2)}) copy-start(f32[128]{0:T(128)} %param.16) | copy-start | bytes 1540
  89.9 3.5 %copy-start.4 = (f32[128]{0:T(128)S(1)}, f32[128]{0:T(128)}, u32[]{:S(2)}) copy-start(f32[128]{0:T(128)} %param.15) | copy-start | bytes 1540
  110.5 14.1 %all-to-all-start.3 = ((bf16[8,8,2560]{2,1,0:T(8,128)(2,1)}), bf16[8,8,2560]{2,1,0:T(8,128)(2,1)S(1)}, u32[]{:S(2)}, u32[]{:S(2)}) async-start(bf16[8,8,2560]{2,1,0:T(8,128)(2,1)} %reduce_sum.96), calls=%async_computation.3 | async-start | bytes 655360 | tf_op jit(solution)/shard_map/all_to_all | solution.py:159
Sparse Core Ops, SparseCore 0:
  25.7 42.9 all-gather.4
  80.7 38.2 all-gather.6

commit v15 on v14

--- a/solution.py
+++ b/solution.py
@@ -137,16 +137,20 @@
         spread = jnp.broadcast_to(among[:, None], (steps, chip) + among.shape[1:])
         return lax.all_to_all(spread, SEQ[-1], 1, 1, tiled=False).reshape(steps, tokens, -1)
 
-    def project(x):
-        raw = jnp.einsum("rd,cdh->crh", x, w_qkv, preferred_element_type=jnp.float32)
-        query = normalize(raw[0], q_gain, HS).astype(jnp.bfloat16)
-        keys = normalize(raw[1], k_gain, HS).astype(jnp.bfloat16)
-        values = raw[2].astype(jnp.bfloat16)
+    n_proj = w_qkv.shape[0]
+    w_all = w_qkv.transpose(1, 0, 2).reshape(w_qkv.shape[1], n_proj * width)
+    xs = exchange_rows(pair)
+    raw = jnp.dot(xs.reshape(-1, xs.shape[-1]), w_all, preferred_element_type=jnp.float32)
+    raw = raw.reshape(xs.shape[0], tokens, n_proj, width)
+
+    def project(raw):
+        query = normalize(raw[:, 0], q_gain, HS).astype(jnp.bfloat16)
+        keys = normalize(raw[:, 1], k_gain, HS).astype(jnp.bfloat16)
+        values = raw[:, 2].astype(jnp.bfloat16)
         return (query, keys, values)
 
-    xs = exchange_rows(pair)
-    q1, k1, v1 = project(xs[0])
-    q2, k2, v2 = project(xs[1])
+    q1, k1, v1 = project(raw[0])
+    q2, k2, v2 = project(raw[1])
 
     fresh_kv = gather_pipe(jnp.stack([k1, v1])[None], tuple(reversed(PIPE)))
 

time: 167 us -> 160 us (0.958); the launches traced: 163 us -> 158 us
  local copies, waits for them, and re-layouts: 15 us -> 6.22 us
  blocking collectives: 71.9 us -> 78.5 us
  other arithmetic: 10.1 us -> 5.6 us
  waiting for transfers between devices: 19.6 us -> 23.3 us
  matrix products: 6.53 us -> 3.38 us
    all_to_all x1, blocking collectives: 15.7 us -> 20.7 us  [attend(): lax.all_to_all(pair_sum.astype(jnp.bfloat16), SEQ[:-1], 0, 0, tiled=False)]
    all_gather x1, waiting for transfers between devices: 0.01 us -> 3.69 us  [gather_pipe(): piece = lax.all_gather(piece, name, axis=0, tiled=True)]
    mul x9, local copies, waits for them, and re-layouts: 3.81 us -> 0.46 us  [normalize(): return (grid * factor).reshape(count, -1) * gain[None, :]]
    unnamed x2 -> x0, matrix products: 2.69 us -> none
    mul x4, local copies, waits for them, and re-layouts: 2.66 us -> 0.35 us  [normalize(): factor = lax.rsqrt(jnp.mean(grid * grid, axis=2, keepdims=True) + 1e-06)]
    dot_general x2 -> x0, local copies, waits for them, and re-layouts: 2.11 us -> none  [project(): jnp.einsum('rd,cdh->crh', x, w_qkv, preferred_element_type=jnp.float32)]
    convert_element_type x2 -> x3, other arithmetic: 2.97 us -> 1.3 us  [the longest x2 0.65 us: project(): keys = normalize(raw[:, 1], k_gain, HS).astype(jnp.bfloat16)]
    unnamed x12 -> x22, local copies, waits for them, and re-layouts: 3.48 us -> 3.99 us
  transfers between devices with their start and end apart: 4 -> 4, of which waited for: 2 -> 3; matrix products, arithmetic and copies ran while one was open for 18% -> 8% of each run, Pallas kernels for 4% -> 4%
where the time goes in v15:
time: 160 us; the launch traced here: 158 us
  blocking collectives  78.5 us (49%)
  waiting for transfers between devices  23.3 us (15%)
  between operations  14.5 us (9%)
  Pallas kernels  13.9 us (9%)
  starting transfers between devices  12.7 us (8%)
  local copies, waits for them, and re-layouts  6.22 us (4%)
  other arithmetic  5.6 us (4%)
  matrix products  3.38 us (2%)
    all_to_all x1, blocking collectives, attend(): lax.all_to_all(pair_sum.astype(jnp.bfloat16), SEQ[:-1], 0, 0, tiled=False)  20.7 us
    all_gather x1, blocking collectives, on_device(): near = lax.all_gather(stale_kv[None], PIPE[1], axis=0, tiled=True)  17.5 us
    all_to_all x2, blocking collectives, attend(): lax.all_to_all(split, SEQ[-1], 0, 0, tiled=False).astype(jnp.float32)  15.6 us
    pallas_call x2, Pallas kernels, block_attend(): pl.pallas_call(functools.partial(attn_kernel, scale=scale, n_blocks=n_blo...  13.9 us
    all_gather x1, blocking collectives, gather_pipe(): piece = lax.all_gather(piece, name, axis=0, tiled=True)  13.1 us
    all_to_all x1, blocking collectives, exchange_rows(): lax.all_to_all(spread, SEQ[-1], 1, 1, tiled=False)  11.6 us
    all_to_all x1, waiting for transfers between devices, attend(): lax.all_to_all(pair_sum.astype(jnp.bfloat16), SEQ[:-1], 0, 0, tiled=False)  9.98 us
    all_to_all x1, waiting for transfers between devices, exchange_rows(): among = lax.all_to_all(spread, SEQ[:-1], 1, 1, tiled=False)  9.57 us
  transfers between devices with their start and end apart: 4, of which 3 were waited for; matrix products, arithmetic and copies ran while one was open for 8% of the time, Pallas kernels for 4%

profile of v15, /device:TPU:1, one launch (start us, length us, event | category | flops | bytes accessed | tf_op | source)
XLA Modules:
  0.0 158.1 jit_solution(8437141518854837893)
XLA Ops:
  7.2 0.0 copy-start
  7.2 0.0 all-gather.5.cloned.1.call-start
  7.2 17.5 %all-gather = bf16[8,128,128]{2,1,0:T(8,128)(2,1)} all-gather(bf16[2,128,128]{2,1,0:T(8,128)(2,1)} %param.12), channel_id=2, replica_groups=mesh['y'=8,'zl'=4,'zh'=2,'x'=4,'c'=2] {'zl'}, dimensions={0}, use_global_device_ids=true | all-gather | bytes 327680 | tf_op jit(solution)/shard_map/all_gather | solution.py:127
  24.7 0.8 pad_maximum_fusion
  25.5 0.0 all-gather.5.cloned.1.call-update
  25.6 0.9 broadcast_in_dim.9
  26.4 9.2 %all-to-all-start = ((bf16[2,8,8,2560]{3,2,0,1:T(8,128)(2,1)}), bf16[2,8,8,2560]{3,2,0,1:T(8,128)(2,1)S(1)}, u32[]{:S(2)}, u32[]{:S(2)}) async-start(bf16[2,8,8,2560]{3,2,0,1:T(8,128)(2,1)} %broadcast_in_dim.9), calls=%async_computation | async-start | bytes 1310720 | tf_op jit(solution)/shard_map/all_to_all | solution.py:136
  35.7 0.0 all-gather.7.cloned.1.call-start
  35.7 2.7 %copy.76 = bf16[3,2560,128]{1,2,0:T(8,128)(2,1)S(1)} copy(bf16[3,2560,128]{2,1,0:T(8,128)(2,1)} %param.13) | data formatting | bytes 3932160 | tf_op args[3]
  38.4 9.6 %all-to-all-done = bf16[2,8,8,2560]{3,2,0,1:T(8,128)(2,1)S(1)} async-done(((bf16[2,8,8,2560]{3,2,0,1:T(8,128)(2,1)}), bf16[2,8,8,2560]{3,2,0,1:T(8,128)(2,1)S(1)}, u32[]{:S(2)}, u32[]{:S(2)}) %all-to-all-start) | async-done | bytes 655392 | tf_op jit(solution)/shard_map/all_to_all | solution.py:136
  48.0 0.1 broadcast_in_dim.10
  48.1 11.6 %all_to_all.30 = bf16[2,2,8,8,2560]{4,3,2,0,1:T(8,128)(2,1)S(1)} all-to-all(bf16[2,2,8,8,2560]{4,3,2,0,1:T(8,128)(2,1)S(1)} %broadcast_in_dim.10), channel_id=1, replica_groups=mesh['y'=8,'zl'=4,'zh'=2,'x'=4,'c'=2] {'c'}, dimensions={1} | all-to-all | bytes 2621440 | tf_op jit(solution)/shard_map/all_to_all | solution.py:138
  59.7 0.1 copy.75
  59.8 0.9 fusion.19
  60.7 0.0 copy-start.3
  60.7 0.0 copy-start.2
  60.7 0.0 copy-start.5
  60.7 0.0 copy-start.6
  60.8 0.1 copy.77
  60.9 0.1 copy.95
  61.0 0.1 copy.82
  61.1 0.1 copy.96
  61.3 0.0 copy-start.1
  61.3 0.1 copy.85
  61.4 0.0 copy-done.3
  61.5 13.1 %all-gather.1 = bf16[8,128,128]{2,1,0:T(8,128)(2,1)} all-gather(bf16[2,128,128]{2,1,0:T(8,128)(2,1)S(1)} %pad_maximum_fusion.1), channel_id=3, replica_groups=mesh['y'=8,'zl'=4,'zh'=2,'x'=4,'c'=2] {'zl'}, dimensions={0}, use_global_device_ids=true | all-gather | bytes 327680 | tf_op jit(solution)/shard_map/all_gather | solution.py:107
  74.6 0.0 all-gather.7.cloned.1.call-update
  74.6 0.0 copy-done.2
  74.6 0.1 copy.73
  74.7 0.0 copy-done.5
  74.7 0.1 iota_compare_fusion.1
  74.7 0.2 convert_reduce_fusion
  75.0 0.2 fusion.12
  75.2 0.2 fusion.11
  75.4 0.6 fusion.15.allowed_ref
  75.9 0.1 copy.83
  76.0 0.1 copy.86
  76.2 0.0 copy-start.4
  76.2 0.1 copy.98
  76.3 0.1 copy.91
  76.5 0.1 copy.92
  76.6 0.1 copy.94
  76.7 0.1 copy.79
  76.8 0.1 copy.80
  76.9 0.1 copy.97
  77.1 0.1 copy.88
  77.2 0.1 copy.89
  77.3 0.6 fusion.2
  78.0 0.6 fusion.4
  78.6 7.0 %shard_map.113 = bf16[128,128]{1,0:T(8,128)(2,1)} custom-call(s32[32]{0:T(128)} %fusion.15.allowed_ref, bf16[128,128]{1,0:T(8,128)(2,1)} %get-tuple-element.19.q_ref, bf16[128,128]{1,0:T(8,128)(2,1)} %get-tuple-element.17.k_ref, bf16[128,128]{1,0:T(8,128)(2,1)} %bitcast.83, bf16[32,2,128,128]{3,2,1,0:T(8,128)(2,1)} %all-gather.5.cloned.1.call-done.kv_ref), custom_call_target="tpu_custom_call" | custom-call | tf_op jit(solution)/shard_map/pallas_call | solution.py:97
  85.6 1.1 convolution_convert_fusion.1
  86.6 6.9 %all_to_all.31 = bf16[2,8,8,2560]{3,2,1,0:T(8,128)(2,1)S(1)} all-to-all(bf16[2,8,8,2560]{3,2,1,0:T(8,128)(2,1)S(1)} %bitcast.72), channel_id=1, replica_groups=mesh['y'=8,'zl'=4,'zh'=2,'x'=4,'c'=2] {'c'}, dimensions={0} | all-to-all | bytes 1310720 | tf_op jit(solution)/shard_map/all_to_all | solution.py:162
  93.6 0.9 reduce_sum.96
  94.5 3.4 %all-to-all-start.3 = ((bf16[8,8,2560]{2,1,0:T(8,128)(2,1)}), bf16[8,8,2560]{2,1,0:T(8,128)(2,1)S(1)}, u32[]{:S(2)}, u32[]{:S(2)}) async-start(bf16[8,8,2560]{2,1,0:T(8,128)(2,1)} %reduce_sum.96), calls=%async_computation.3 | async-start | bytes 655360 | tf_op jit(solution)/shard_map/all_to_all | solution.py:163
  98.0 0.7 copy.99
  98.7 10.0 %all-to-all-done.3 = bf16[8,8,2560]{2,1,0:T(8,128)(2,1)S(1)} async-done(((bf16[8,8,2560]{2,1,0:T(8,128)(2,1)}), bf16[8,8,2560]{2,1,0:T(8,128)(2,1)S(1)}, u32[]{:S(2)}, u32[]{:S(2)}) %all-to-all-start.3) | async-done | bytes 327712 | tf_op jit(solution)/shard_map/all_to_all | solution.py:163
  108.6 0.7 reduce_sum.97
  109.3 3.7 %all-gather.7.cloned.1.call-done.kv_ref = bf16[32,2,128,128]{3,2,1,0:T(8,128)(2,1)} async-done(((bf16[4,2,128,128]{3,2,1,0:T(8,128)(2,1)}), bf16[32,2,128,128]{3,2,1,0:T(8,128)(2,1)}) %all-gather.7.cloned.1.call-update) | async-done | bytes 2097168 | tf_op jit(solution)/shard_map/all_gather | solution.py:107
  113.0 7.0 %shard_map.114 = bf16[128,128]{1,0:T(8,128)(2,1)} custom-call(s32[32]{0:T(128)} %fusion.15.allowed_ref, bf16[128,128]{1,0:T(8,128)(2,1)} %get-tuple-element.18.q_ref, bf16[128,128]{1,0:T(8,128)(2,1)} %get-tuple-element.16.k_ref, bf16[128,128]{1,0:T(8,128)(2,1)} %bitcast.91, bf16[32,2,128,128]{3,2,1,0:T(8,128)(2,1)} %all-gather.7.cloned.1.call-done.kv_ref), custom_call_target="tpu_custom_call" | custom-call | tf_op jit(solution)/shard_map/pallas_call | solution.py:97
  120.0 1.1 convolution_convert_fusion
  121.0 8.7 %all_to_all.32 = bf16[2,8,8,2560]{3,2,1,0:T(8,128)(2,1)S(1)} all-to-all(bf16[2,8,8,2560]{3,2,1,0:T(8,128)(2,1)S(1)} %bitcast.73), channel_id=1, replica_groups=mesh['y'=8,'zl'=4,'zh'=2,'x'=4,'c'=2] {'c'}, dimensions={0} | all-to-all | bytes 1310720 | tf_op jit(solution)/shard_map/all_to_all | solution.py:162
  129.7 0.2 reduce_sum.100
  129.9 20.7 %all_to_all.33 = bf16[8,8,2560]{2,1,0:T(8,128)(2,1)S(1)} all-to-all(bf16[8,8,2560]{2,1,0:T(8,128)(2,1)S(1)} %reduce_sum.100), channel_id=1, replica_groups=mesh['y'=8,'zl'=4,'zh'=2,'x'=4,'c'=2] {'zh','x'}, dimensions={0} | all-to-all | bytes 655360 | tf_op jit(solution)/shard_map/all_to_all | solution.py:163
  150.6 0.7 reduce_sum.101
  (29 shorter events, 0.3 us)
Async XLA Ops:
  7.2 78.4 %copy-start = (bf16[128,2560]{1,0:T(8,128)(2,1)S(1)}, bf16[128,2560]{1,0:T(8,128)(2,1)}, u32[]{:S(2)}) copy-start(bf16[128,2560]{1,0:T(8,128)(2,1)} %param.14) | copy-start | bytes 1966084
  7.2 71.4 %all-gather.5.cloned.1.call-start = ((), (), s32[]{:S(2)}) async-start(), calls=%async_computation.6 | async-start | bytes 2359296 | tf_op jit(solution)/shard_map/all_gather | solution.py:129
  26.4 21.5 %all-to-all-start = ((bf16[2,8,8,2560]{3,2,0,1:T(8,128)(2,1)}), bf16[2,8,8,2560]{3,2,0,1:T(8,128)(2,1)S(1)}, u32[]{:S(2)}, u32[]{:S(2)}) async-start(bf16[2,8,8,2560]{3,2,0,1:T(8,128)(2,1)} %broadcast_in_dim.9), calls=%async_computation | async-start | bytes 1310720 | tf_op jit(solution)/shard_map/all_to_all | solution.py:136
  35.7 77.3 %all-gather.7.cloned.1.call-start = ((), (), s32[]{:S(2)}) async-start(), calls=%async_computation.7 | async-start | bytes 2359296 | tf_op jit(solution)/shard_map/all_gather | solution.py:107
  60.7 0.7 copy-start.3
  60.7 13.9 %copy-start.2 = (s32[32,16]{0,1:T(8,128)S(1)}, s32[32,16]{0,1:T(8,128)}, u32[]{:S(2)}) copy-start(s32[32,16]{0,1:T(8,128)} %param.17) | copy-start | bytes 6148
  60.7 13.9 %copy-start.5 = (s32[32]{0:T(128)S(1)}, s32[32]{0:T(128)}, u32[]{:S(2)}) copy-start(s32[32]{0:T(128)} %param.18) | copy-start | bytes 388
  60.7 14.2 %copy-start.6 = (s32[32]{0:T(128)S(1)}, s32[32]{0:T(128)}, u32[]{:S(2)}) copy-start(s32[32]{0:T(128)} %param.19) | copy-start | bytes 388
  61.3 15.2 %copy-start.1 = (bf16[128,1,128]{2,0,1:T(8,128)(2,1)}, bf16[128,1,128]{2,0,1:T(8,128)(2,1)S(1)}, u32[]{:S(2)}) copy-start(bf16[128,1,128]{2,0,1:T(8,128)(2,1)S(1)} %copy.96) | copy-start | bytes 98308
  76.2 1.8 %copy-start.4 = (f32[128]{0:T(128)S(1)}, f32[128]{0:T(128)}, u32[]{:S(2)}) copy-start(f32[128]{0:T(128)} %param.15) | copy-start | bytes 1540
  94.5 14.1 %all-to-all-start.3 = ((bf16[8,8,2560]{2,1,0:T(8,128)(2,1)}), bf16[8,8,2560]{2,1,0:T(8,128)(2,1)S(1)}, u32[]{:S(2)}, u32[]{:S(2)}) async-start(bf16[8,8,2560]{2,1,0:T(8,128)(2,1)} %reduce_sum.96), calls=%async_computation.3 | async-start | bytes 655360 | tf_op jit(solution)/shard_map/all_to_all | solution.py:163
Sparse Core Ops, SparseCore 0:
  25.7 42.9 all-gather.4
  74.7 38.2 all-gather.6

commit v16 on v15

--- a/solution.py
+++ b/solution.py
@@ -124,9 +124,15 @@
     mine = lax.dynamic_slice_in_dim(linked, me * BPM, BPM, 0)
     remote = mine & (batch_of != me)[None, :]
 
-    near = lax.all_gather(stale_kv[None], PIPE[1], axis=0, tiled=True)
-    pair, near = lax.optimization_barrier((jnp.stack([x_first, x_second]), near))
+    nz = PIPE_PARTS[1][1]
+    shifted = [lax.ppermute(stale_kv, PIPE[1], [(i, (i + m) % nz) for i in range(nz)]) for m in range(1, nz)]
+    near = jnp.stack([stale_kv] + shifted)
+    pair = jnp.stack([x_first, x_second])
     stale = lax.all_gather(near, PIPE[0], axis=0, tiled=True)
+    ny = PIPE_PARTS[0][1]
+    from_z = (lax.axis_index(PIPE[1]) - jnp.arange(nz, dtype=jnp.int32)) % nz
+    order = (jnp.arange(ny, dtype=jnp.int32)[:, None] * nz + from_z[None, :]).reshape(-1)
+    remote_stale = remote[:, order]
 
     chip = SEQ_PARTS[-1][1]
 
@@ -163,7 +169,7 @@
         sent = lax.all_to_all(pair_sum.astype(jnp.bfloat16), SEQ[:-1], 0, 0, tiled=False)
         return jnp.sum(sent.astype(jnp.float32), axis=0).astype(jnp.bfloat16)
 
-    out_first = attend(q1, k1, v1, stale, remote)
+    out_first = attend(q1, k1, v1, stale, remote_stale)
     out_first, fresh_kv = lax.optimization_barrier((out_first, fresh_kv))
     out_second = attend(q2, k2, v2, fresh_kv, remote)
     return (out_first, out_second)

time: 160 us -> 161 us (level)
  blocking collectives: 78.5 us -> 61.1 us
  starting transfers between devices: 12.7 us -> 26.2 us
  other arithmetic: 5.6 us -> 7.86 us
    all_gather x1 -> x0, blocking collectives: 17.5 us -> none  [on_device(): near = lax.all_gather(stale_kv[None], PIPE[1], axis=0, tiled=True)]
    ppermute x0 -> x3, starting transfers between devices: none -> 12.9 us  [on_device(): lax.ppermute(stale_kv, PIPE[1], [(i, (i + m) % nz) for i in range(nz)])]
    ppermute x0 -> x3, waiting for transfers between devices: none -> 3.59 us  [on_device(): lax.ppermute(stale_kv, PIPE[1], [(i, (i + m) % nz) for i in range(nz)])]
    all_gather x1, waiting for transfers between devices: 3.69 us -> 2.07 us  [gather_pipe(): piece = lax.all_gather(piece, name, axis=0, tiled=True)]
  transfers between devices with their start and end apart: 4 -> 7, of which waited for: 3 -> 5; matrix products, arithmetic and copies ran while one was open for 8% -> 9% of each run, Pallas kernels for 4% -> 5%
where the time goes in v16:
time: 161 us; the launch traced here: 160 us
  blocking collectives  61.1 us (38%)
  starting transfers between devices  26.2 us (16%)
  waiting for transfers between devices  24.7 us (15%)
  Pallas kernels  15.3 us (10%)
  between operations  14.5 us (9%)
  other arithmetic  7.86 us (5%)
  local copies, waits for them, and re-layouts  7 us (4%)
  matrix products  3.38 us (2%)
    all_to_all x1, blocking collectives, attend(): lax.all_to_all(pair_sum.astype(jnp.bfloat16), SEQ[:-1], 0, 0, tiled=False)  20.5 us
    all_to_all x2, blocking collectives, attend(): lax.all_to_all(split, SEQ[-1], 0, 0, tiled=False).astype(jnp.float32)  15.6 us
    pallas_call x2, Pallas kernels, block_attend(): pl.pallas_call(functools.partial(attn_kernel, scale=scale, n_blocks=n_blo...  15.3 us
    all_gather x1, blocking collectives, gather_pipe(): piece = lax.all_gather(piece, name, axis=0, tiled=True)  13.1 us
    ppermute x3, starting transfers between devices, on_device(): lax.ppermute(stale_kv, PIPE[1], [(i, (i + m) % nz) for i in range(nz)])  12.9 us
    all_to_all x1, blocking collectives, exchange_rows(): lax.all_to_all(spread, SEQ[-1], 1, 1, tiled=False)  11.8 us
    all_to_all x1, waiting for transfers between devices, exchange_rows(): among = lax.all_to_all(spread, SEQ[:-1], 1, 1, tiled=False)  9.53 us
    all_to_all x1, waiting for transfers between devices, attend(): lax.all_to_all(pair_sum.astype(jnp.bfloat16), SEQ[:-1], 0, 0, tiled=False)  9.53 us
  transfers between devices with their start and end apart: 7, of which 5 were waited for; matrix products, arithmetic and copies ran while one was open for 9% of the time, Pallas kernels for 5%

profile of v16, /device:TPU:1, one launch (start us, length us, event | category | flops | bytes accessed | tf_op | source)
XLA Modules:
  0.0 160.1 jit_solution(12746019273594357361)
XLA Ops:
  7.2 0.0 copy-start
  7.2 0.0 all-gather.4.cloned.1.call-start
  7.2 4.9 %collective-permute-start = (bf16[2,128,128]{2,1,0:T(8,128)(2,1)}, bf16[2,128,128]{2,1,0:T(8,128)(2,1)S(1)}, u32[]{:S(2)}, u32[]{:S(2)}) collective-permute-start(bf16[2,128,128]{2,1,0:T(8,128)(2,1)} %param.12), channel_id=1, source_target_pairs={{0,16},{16,32},{32,48},{48,0},{1,17},{17,33},{33,49},{49,1},{2,18}... | collective-permute-start | bytes 196616 | tf_op jit(solution)/shard_map/ppermute | solution.py:128
  12.2 5.8 %collective-permute-start.1 = (bf16[2,128,128]{2,1,0:T(8,128)(2,1)}, bf16[2,128,128]{2,1,0:T(8,128)(2,1)S(1)}, u32[]{:S(2)}, u32[]{:S(2)}) collective-permute-start(bf16[2,128,128]{2,1,0:T(8,128)(2,1)} %param.12), channel_id=1, source_target_pairs={{0,32},{16,48},{32,0},{48,16},{1,33},{17,49},{33,1},{49,17},{2,34}... | collective-permute-start | bytes 196616 | tf_op jit(solution)/shard_map/ppermute | solution.py:128
  18.0 2.2 %collective-permute-start.2 = (bf16[2,128,128]{2,1,0:T(8,128)(2,1)}, bf16[2,128,128]{2,1,0:T(8,128)(2,1)S(1)}, u32[]{:S(2)}, u32[]{:S(2)}) collective-permute-start(bf16[2,128,128]{2,1,0:T(8,128)(2,1)} %param.12), channel_id=1, source_target_pairs={{0,48},{16,0},{32,16},{48,32},{1,49},{17,1},{33,17},{49,33},{2,50}... | collective-permute-start | bytes 196616 | tf_op jit(solution)/shard_map/ppermute | solution.py:128
  20.2 0.4 collective-permute-done.1
  20.6 3.2 %collective-permute-done.2 = bf16[2,128,128]{2,1,0:T(8,128)(2,1)S(1)} collective-permute-done((bf16[2,128,128]{2,1,0:T(8,128)(2,1)}, bf16[2,128,128]{2,1,0:T(8,128)(2,1)S(1)}, u32[]{:S(2)}, u32[]{:S(2)}) %collective-permute-start.2) | collective-permute-done | bytes 65568 | tf_op jit(solution)/shard_map/ppermute | solution.py:128
  23.8 1.6 pad_maximum_fusion
  25.4 0.0 all-gather.4.cloned.1.call-update
  25.4 0.8 pad_maximum_fusion.1
  26.2 0.9 broadcast_in_dim.6
  27.1 9.2 %all-to-all-start = ((bf16[2,8,8,2560]{3,2,0,1:T(8,128)(2,1)}), bf16[2,8,8,2560]{3,2,0,1:T(8,128)(2,1)S(1)}, u32[]{:S(2)}, u32[]{:S(2)}) async-start(bf16[2,8,8,2560]{3,2,0,1:T(8,128)(2,1)} %broadcast_in_dim.6), calls=%async_computation | async-start | bytes 1310720 | tf_op jit(solution)/shard_map/all_to_all | solution.py:142
  36.3 0.0 all-gather.6.cloned.1.call-start
  36.3 0.1 copy.73
  36.4 2.7 %copy.76 = bf16[3,2560,128]{1,2,0:T(8,128)(2,1)S(1)} copy(bf16[3,2560,128]{2,1,0:T(8,128)(2,1)} %param.13) | data formatting | bytes 3932160 | tf_op args[3]
  39.1 9.5 %all-to-all-done = bf16[2,8,8,2560]{3,2,0,1:T(8,128)(2,1)S(1)} async-done(((bf16[2,8,8,2560]{3,2,0,1:T(8,128)(2,1)}), bf16[2,8,8,2560]{3,2,0,1:T(8,128)(2,1)S(1)}, u32[]{:S(2)}, u32[]{:S(2)}) %all-to-all-start) | async-done | bytes 655392 | tf_op jit(solution)/shard_map/all_to_all | solution.py:142
  48.7 0.1 broadcast_in_dim.7
  48.8 11.8 %all_to_all.30 = bf16[2,2,8,8,2560]{4,3,2,0,1:T(8,128)(2,1)S(1)} all-to-all(bf16[2,2,8,8,2560]{4,3,2,0,1:T(8,128)(2,1)S(1)} %broadcast_in_dim.7), channel_id=1, replica_groups=mesh['y'=8,'zl'=4,'zh'=2,'x'=4,'c'=2] {'c'}, dimensions={1} | all-to-all | bytes 2621440 | tf_op jit(solution)/shard_map/all_to_all | solution.py:144
  60.6 0.1 copy.75
  60.7 0.9 fusion.20
  61.6 0.1 copy.77
  61.8 0.1 copy.95
  61.9 0.1 copy.82
  62.0 0.1 copy.96
  62.2 0.1 copy.85
  62.3 13.1 %all-gather = bf16[8,128,128]{2,1,0:T(8,128)(2,1)} all-gather(bf16[2,128,128]{2,1,0:T(8,128)(2,1)S(1)} %pad_maximum_fusion.2), channel_id=2, replica_groups=mesh['y'=8,'zl'=4,'zh'=2,'x'=4,'c'=2] {'zl'}, dimensions={0}, use_global_device_ids=true | all-gather | bytes 327680 | tf_op jit(solution)/shard_map/all_gather | solution.py:107
  75.4 0.0 all-gather.6.cloned.1.call-update
  75.5 0.1 broadcast_add_fusion
  75.5 0.1 add.93
  75.6 0.1 iota_compare_fusion.1
  75.7 0.2 convert_reduce_fusion
  75.9 0.2 fusion.12
  76.1 0.2 fusion.11
  76.3 0.6 convert_bitcast_fusion.3
  76.9 0.7 gather_fusion
  77.6 0.6 convert_element_type.70.allowed_ref
  78.2 0.1 copy.83
  78.3 0.1 copy.86
  78.5 0.1 copy.98
  78.6 0.1 copy.91
  78.7 0.1 copy.92
  78.8 0.1 copy.94
  78.9 0.1 copy.79
  79.1 0.1 copy.80
  79.2 0.1 copy.97
  79.3 0.1 copy.88
  79.5 0.1 copy.89
  79.6 0.6 fusion.2
  80.2 0.6 fusion.4
  80.8 7.6 %shard_map.113 = bf16[128,128]{1,0:T(8,128)(2,1)} custom-call(s32[32]{0:T(128)} %convert_element_type.70.allowed_ref, bf16[128,128]{1,0:T(8,128)(2,1)} %get-tuple-element.17.q_ref, bf16[128,128]{1,0:T(8,128)(2,1)} %get-tuple-element.15.k_ref, bf16[128,128]{1,0:T(8,128)(2,1)} %bitcast.89, bf16[32,2,128,128]{3,2,1,0:T(8,128)(2,1)} %all-gather.4.cloned.1.call-done.kv_ref), custom_call_target="tpu_custom_call" | custom-call | tf_op jit(solution)/shard_map/pallas_call | solution.py:97
  88.5 1.1 convolution_convert_fusion.1
  89.6 6.9 %all_to_all.31 = bf16[2,8,8,2560]{3,2,1,0:T(8,128)(2,1)S(1)} all-to-all(bf16[2,8,8,2560]{3,2,1,0:T(8,128)(2,1)S(1)} %bitcast.79), channel_id=1, replica_groups=mesh['y'=8,'zl'=4,'zh'=2,'x'=4,'c'=2] {'c'}, dimensions={0} | all-to-all | bytes 1310720 | tf_op jit(solution)/shard_map/all_to_all | solution.py:168
  96.5 0.9 reduce_sum.96
  97.4 4.0 %all-to-all-start.3 = ((bf16[8,8,2560]{2,1,0:T(8,128)(2,1)}), bf16[8,8,2560]{2,1,0:T(8,128)(2,1)S(1)}, u32[]{:S(2)}, u32[]{:S(2)}) async-start(bf16[8,8,2560]{2,1,0:T(8,128)(2,1)} %reduce_sum.96), calls=%async_computation.3 | async-start | bytes 655360 | tf_op jit(solution)/shard_map/all_to_all | solution.py:169
  101.4 0.7 copy.99
  102.1 9.5 %all-to-all-done.3 = bf16[8,8,2560]{2,1,0:T(8,128)(2,1)S(1)} async-done(((bf16[8,8,2560]{2,1,0:T(8,128)(2,1)}), bf16[8,8,2560]{2,1,0:T(8,128)(2,1)S(1)}, u32[]{:S(2)}, u32[]{:S(2)}) %all-to-all-start.3) | async-done | bytes 327712 | tf_op jit(solution)/shard_map/all_to_all | solution.py:169
  111.7 0.7 reduce_sum.97
  112.3 2.1 %all-gather.6.cloned.1.call-done.kv_ref = bf16[32,2,128,128]{3,2,1,0:T(8,128)(2,1)} async-done(((bf16[4,2,128,128]{3,2,1,0:T(8,128)(2,1)}), bf16[32,2,128,128]{3,2,1,0:T(8,128)(2,1)}) %all-gather.6.cloned.1.call-update) | async-done | bytes 2097168 | tf_op jit(solution)/shard_map/all_gather | solution.py:107
  114.4 7.6 %shard_map.114 = bf16[128,128]{1,0:T(8,128)(2,1)} custom-call(s32[32]{0:T(128)} %get-tuple-element.6.allowed_ref, bf16[128,128]{1,0:T(8,128)(2,1)} %get-tuple-element.16.q_ref, bf16[128,128]{1,0:T(8,128)(2,1)} %get-tuple-element.14.k_ref, bf16[128,128]{1,0:T(8,128)(2,1)} %bitcast.97, bf16[32,2,128,128]{3,2,1,0:T(8,128)(2,1)} %all-gather.6.cloned.1.call-done.kv_ref), custom_call_target="tpu_custom_call" | custom-call | tf_op jit(solution)/shard_map/pallas_call | solution.py:97
  122.1 1.1 convolution_convert_fusion
  123.1 8.7 %all_to_all.32 = bf16[2,8,8,2560]{3,2,1,0:T(8,128)(2,1)S(1)} all-to-all(bf16[2,8,8,2560]{3,2,1,0:T(8,128)(2,1)S(1)} %bitcast.80), channel_id=1, replica_groups=mesh['y'=8,'zl'=4,'zh'=2,'x'=4,'c'=2] {'c'}, dimensions={0} | all-to-all | bytes 1310720 | tf_op jit(solution)/shard_map/all_to_all | solution.py:168
  131.9 0.2 reduce_sum.100
  132.1 20.5 %all_to_all.33 = bf16[8,8,2560]{2,1,0:T(8,128)(2,1)S(1)} all-to-all(bf16[8,8,2560]{2,1,0:T(8,128)(2,1)S(1)} %reduce_sum.100), channel_id=1, replica_groups=mesh['y'=8,'zl'=4,'zh'=2,'x'=4,'c'=2] {'zh','x'}, dimensions={0} | all-to-all | bytes 655360 | tf_op jit(solution)/shard_map/all_to_all | solution.py:169
  152.6 0.7 reduce_sum.101
  (43 shorter events, 0.4 us)
Async XLA Ops:
  7.2 81.3 %copy-start = (bf16[128,2560]{1,0:T(8,128)(2,1)S(1)}, bf16[128,2560]{1,0:T(8,128)(2,1)}, u32[]{:S(2)}) copy-start(bf16[128,2560]{1,0:T(8,128)(2,1)} %param.14) | copy-start | bytes 1966084
  7.2 73.7 %all-gather.4.cloned.1.call-start = ((), (), s32[]{:S(2)}) async-start(), calls=%async_computation.6 | async-start | bytes 2359296 | tf_op jit(solution)/shard_map/all_gather | solution.py:131
  7.2 13.0 %collective-permute-start = (bf16[2,128,128]{2,1,0:T(8,128)(2,1)}, bf16[2,128,128]{2,1,0:T(8,128)(2,1)S(1)}, u32[]{:S(2)}, u32[]{:S(2)}) collective-permute-start(bf16[2,128,128]{2,1,0:T(8,128)(2,1)} %param.12), channel_id=1, source_target_pairs={{0,16},{16,32},{32,48},{48,0},{1,17},{17,33},{33,49},{49,1},{2,18}... | collective-permute-start | bytes 196616 | tf_op jit(solution)/shard_map/ppermute | solution.py:128
  12.2 8.4 %collective-permute-start.1 = (bf16[2,128,128]{2,1,0:T(8,128)(2,1)}, bf16[2,128,128]{2,1,0:T(8,128)(2,1)S(1)}, u32[]{:S(2)}, u32[]{:S(2)}) collective-permute-start(bf16[2,128,128]{2,1,0:T(8,128)(2,1)} %param.12), channel_id=1, source_target_pairs={{0,32},{16,48},{32,0},{48,16},{1,33},{17,49},{33,1},{49,17},{2,34}... | collective-permute-start | bytes 196616 | tf_op jit(solution)/shard_map/ppermute | solution.py:128
  18.0 5.8 %collective-permute-start.2 = (bf16[2,128,128]{2,1,0:T(8,128)(2,1)}, bf16[2,128,128]{2,1,0:T(8,128)(2,1)S(1)}, u32[]{:S(2)}, u32[]{:S(2)}) collective-permute-start(bf16[2,128,128]{2,1,0:T(8,128)(2,1)} %param.12), channel_id=1, source_target_pairs={{0,48},{16,0},{32,16},{48,32},{1,49},{17,1},{33,17},{49,33},{2,50}... | collective-permute-start | bytes 196616 | tf_op jit(solution)/shard_map/ppermute | solution.py:128
  25.4 11.0 %copy-start.2 = (s32[32,16]{0,1:T(8,128)S(1)}, s32[32,16]{0,1:T(8,128)}, u32[]{:S(2)}) copy-start(s32[32,16]{0,1:T(8,128)} %param.17) | copy-start | bytes 6148
  27.1 21.6 %all-to-all-start = ((bf16[2,8,8,2560]{3,2,0,1:T(8,128)(2,1)}), bf16[2,8,8,2560]{3,2,0,1:T(8,128)(2,1)S(1)}, u32[]{:S(2)}, u32[]{:S(2)}) async-start(bf16[2,8,8,2560]{3,2,0,1:T(8,128)(2,1)} %broadcast_in_dim.6), calls=%async_computation | async-start | bytes 1310720 | tf_op jit(solution)/shard_map/all_to_all | solution.py:142
  36.3 78.1 %all-gather.6.cloned.1.call-start = ((), (), s32[]{:S(2)}) async-start(), calls=%async_computation.7 | async-start | bytes 2359296 | tf_op jit(solution)/shard_map/all_gather | solution.py:107
  61.5 0.7 copy-start.3
  61.6 14.0 %copy-start.5 = (s32[32]{0:T(128)S(1)}, s32[32]{0:T(128)}, u32[]{:S(2)}) copy-start(s32[32]{0:T(128)} %param.18) | copy-start | bytes 388
  61.6 14.3 %copy-start.6 = (s32[32]{0:T(128)S(1)}, s32[32]{0:T(128)}, u32[]{:S(2)}) copy-start(s32[32]{0:T(128)} %param.19) | copy-start | bytes 388
  62.1 16.3 %copy-start.1 = (bf16[128,1,128]{2,0,1:T(8,128)(2,1)}, bf16[128,1,128]{2,0,1:T(8,128)(2,1)S(1)}, u32[]{:S(2)}) copy-start(bf16[128,1,128]{2,0,1:T(8,128)(2,1)S(1)} %copy.96) | copy-start | bytes 98308
  78.4 1.8 %copy-start.4 = (f32[128]{0:T(128)S(1)}, f32[128]{0:T(128)}, u32[]{:S(2)}) copy-start(f32[128]{0:T(128)} %param.15) | copy-start | bytes 1540
  97.4 14.3 %all-to-all-start.3 = ((bf16[8,8,2560]{2,1,0:T(8,128)(2,1)}), bf16[8,8,2560]{2,1,0:T(8,128)(2,1)S(1)}, u32[]{:S(2)}, u32[]{:S(2)}) async-start(bf16[8,8,2560]{2,1,0:T(8,128)(2,1)} %reduce_sum.96), calls=%async_computation.3 | async-start | bytes 655360 | tf_op jit(solution)/shard_map/all_to_all | solution.py:169
Sparse Core Ops, SparseCore 0:
  25.5 42.2 all-gather.3
  75.6 38.7 all-gather.5

commit v17 on v15

--- a/solution.py
+++ b/solution.py
@@ -102,12 +102,6 @@
     )(allowed, query, keys, values, kv)
 
 
-def gather_pipe(piece, order):
-    for name in order:
-        piece = lax.all_gather(piece, name, axis=0, tiled=True)
-    return piece
-
-
 def on_device(
     x_first, x_second, stale_kv, w_qkv, w_out, q_gain, k_gain, layout, counts, slot_block
 ):
@@ -125,7 +119,7 @@
     remote = mine & (batch_of != me)[None, :]
 
     near = lax.all_gather(stale_kv[None], PIPE[1], axis=0, tiled=True)
-    pair, near = lax.optimization_barrier((jnp.stack([x_first, x_second]), near))
+    first_rows, near = lax.optimization_barrier((x_first, near))
     stale = lax.all_gather(near, PIPE[0], axis=0, tiled=True)
 
     chip = SEQ_PARTS[-1][1]
@@ -139,20 +133,20 @@
 
     n_proj = w_qkv.shape[0]
     w_all = w_qkv.transpose(1, 0, 2).reshape(w_qkv.shape[1], n_proj * width)
-    xs = exchange_rows(pair)
-    raw = jnp.dot(xs.reshape(-1, xs.shape[-1]), w_all, preferred_element_type=jnp.float32)
-    raw = raw.reshape(xs.shape[0], tokens, n_proj, width)
-
-    def project(raw):
+    def project(x):
+        xs = exchange_rows(x[None])[0]
+        raw = jnp.dot(xs, w_all, preferred_element_type=jnp.float32).reshape(tokens, n_proj, width)
         query = normalize(raw[:, 0], q_gain, HS).astype(jnp.bfloat16)
         keys = normalize(raw[:, 1], k_gain, HS).astype(jnp.bfloat16)
         values = raw[:, 2].astype(jnp.bfloat16)
         return (query, keys, values)
 
-    q1, k1, v1 = project(raw[0])
-    q2, k2, v2 = project(raw[1])
+    q1, k1, v1 = project(first_rows)
 
-    fresh_kv = gather_pipe(jnp.stack([k1, v1])[None], tuple(reversed(PIPE)))
+    near_fresh = lax.all_gather(jnp.stack([k1, v1])[None], PIPE[1], axis=0, tiled=True)
+    second_rows, near_fresh = lax.optimization_barrier((x_second, near_fresh))
+    fresh_kv = lax.all_gather(near_fresh, PIPE[0], axis=0, tiled=True)
+    q2, k2, v2 = project(second_rows)
 
     def attend(query, keys, values, kv, remote):
         allowed = remote[0].astype(jnp.int32)

time: 160 us -> 165 us (1.031)
  the two profiles are of different devices: /device:TPU:1 before, /device:TPU:72 now
where the time goes in v17:
time: 165 us; the launch traced here: 164 us
  blocking collectives  66.9 us (41%)
  waiting for transfers between devices  33.5 us (20%)
  starting transfers between devices  17 us (10%)
  Pallas kernels  16.7 us (10%)
  between operations  14.3 us (9%)
  local copies, waits for them, and re-layouts  7.19 us (4%)
  other arithmetic  4.19 us (3%)
  matrix products  4 us (2%)
    all_to_all x2, waiting for transfers between devices, exchange_rows(): among = lax.all_to_all(spread, SEQ[:-1], 1, 1, tiled=False)  18.8 us
    all_to_all x1, blocking collectives, attend(): lax.all_to_all(pair_sum.astype(jnp.bfloat16), SEQ[:-1], 0, 0, tiled=False)  18.5 us
    all_gather x1, blocking collectives, on_device(): near = lax.all_gather(stale_kv[None], PIPE[1], axis=0, tiled=True)  16.7 us
    pallas_call x2, Pallas kernels, block_attend(): pl.pallas_call(functools.partial(attn_kernel, scale=scale, n_blocks=n_blo...  16.7 us
    all_to_all x1, waiting for transfers between devices, attend(): lax.all_to_all(pair_sum.astype(jnp.bfloat16), SEQ[:-1], 0, 0, tiled=False)  14.7 us
    all_gather x1, blocking collectives, on_device(): lax.all_gather(jnp.stack([k1, v1])[None], PIPE[1], axis=0, tiled=True)  14.7 us
    all_to_all x2, starting transfers between devices, exchange_rows(): among = lax.all_to_all(spread, SEQ[:-1], 1, 1, tiled=False)  13.5 us
    all_to_all x2, blocking collectives, exchange_rows(): lax.all_to_all(spread, SEQ[-1], 1, 1, tiled=False)  8.52 us
  transfers between devices with their start and end apart: 5, of which 3 were waited for; matrix products, arithmetic and copies ran while one was open for 8% of the time, Pallas kernels for 5%

profile of v17, /device:TPU:72, one launch (start us, length us, event | category | flops | bytes accessed | tf_op | source)
XLA Modules:
  0.0 163.7 jit_solution(5016880222048836303)
XLA Ops:
  7.2 0.0 copy-start
  7.2 0.0 all-gather.5.cloned.1.call-start
  7.2 16.7 %all-gather = bf16[8,128,128]{2,1,0:T(8,128)(2,1)} all-gather(bf16[2,128,128]{2,1,0:T(8,128)(2,1)} %param.12), channel_id=2, replica_groups=mesh['y'=8,'zl'=4,'zh'=2,'x'=4,'c'=2] {'zl'}, dimensions={0}, use_global_device_ids=true | all-gather | bytes 327680 | tf_op jit(solution)/shard_map/all_gather | solution.py:121
  23.9 0.0 all-gather.5.cloned.1.call-update
  23.9 1.5 broadcast_in_dim.17
  25.5 10.0 %all-to-all-start = ((bf16[1,8,8,2560]{3,2,0,1:T(8,128)(2,1)}), bf16[1,8,8,2560]{3,2,0,1:T(8,128)(2,1)S(1)}, u32[]{:S(2)}, u32[]{:S(2)}) async-start(bf16[1,8,8,2560]{3,2,0,1:T(8,128)(2,1)} %broadcast_in_dim.17), calls=%async_computation | async-start | bytes 655360 | tf_op jit(solution)/shard_map/all_to_all | solution.py:130
  35.5 0.0 all-gather.7.cloned.1.call-start
  35.5 2.7 %copy.54 = bf16[3,2560,128]{1,2,0:T(8,128)(2,1)S(1)} copy(bf16[3,2560,128]{2,1,0:T(8,128)(2,1)} %param.13) | data formatting | bytes 3932160 | tf_op args[3]
  38.2 8.7 %all-to-all-done = bf16[1,8,8,2560]{3,2,0,1:T(8,128)(2,1)S(1)} async-done(((bf16[1,8,8,2560]{3,2,0,1:T(8,128)(2,1)}), bf16[1,8,8,2560]{3,2,0,1:T(8,128)(2,1)S(1)}, u32[]{:S(2)}, u32[]{:S(2)}) %all-to-all-start) | async-done | bytes 327712 | tf_op jit(solution)/shard_map/all_to_all | solution.py:130
  46.9 4.3 %all_to_all.40 = bf16[1,2,8,8,2560]{4,3,2,0,1:T(8,128)(2,1)S(1)} all-to-all(bf16[1,2,8,8,2560]{4,3,2,0,1:T(8,128)(2,1)S(1)} %broadcast_in_dim.19), channel_id=1, replica_groups=mesh['y'=8,'zl'=4,'zh'=2,'x'=4,'c'=2] {'c'}, dimensions={1} | all-to-all | bytes 1310720 | tf_op jit(solution)/shard_map/all_to_all | solution.py:132
  51.2 0.0 copy-start.3
  51.2 0.0 copy-start.2
  51.2 0.0 copy-start.5
  51.2 0.0 copy-start.1
  51.2 0.7 fusion.2
  52.0 0.0 copy-start.6
  52.0 0.1 copy.59
  52.1 0.1 copy.62
  52.2 0.6 fusion.18
  52.9 0.0 copy-done.3
  52.9 14.7 %all-gather.1 = bf16[8,128,128]{2,1,0:T(8,128)(2,1)} all-gather(bf16[2,128,128]{2,1,0:T(8,128)(2,1)S(1)} %pad_maximum_fusion), channel_id=3, replica_groups=mesh['y'=8,'zl'=4,'zh'=2,'x'=4,'c'=2] {'zl'}, dimensions={0}, use_global_device_ids=true | all-gather | bytes 327680 | tf_op jit(solution)/shard_map/all_gather | solution.py:146
  67.5 0.0 all-gather.7.cloned.1.call-update
  67.6 0.0 copy-done.2
  67.6 0.1 copy.53
  67.7 0.0 copy-done.5
  67.7 0.1 iota_compare_fusion.1
  67.7 0.2 convert_reduce_fusion
  68.0 0.0 copy-done.1
  68.0 0.7 broadcast_in_dim.21
  68.7 3.4 %all-to-all-start.4 = ((bf16[1,8,8,2560]{3,2,0,1:T(8,128)(2,1)}), bf16[1,8,8,2560]{3,2,0,1:T(8,128)(2,1)S(1)}, u32[]{:S(2)}, u32[]{:S(2)}) async-start(bf16[1,8,8,2560]{3,2,0,1:T(8,128)(2,1)} %broadcast_in_dim.21), calls=%async_computation.4 | async-start | bytes 655360 | tf_op jit(solution)/shard_map/all_to_all | solution.py:130
  72.1 0.0 copy-done.6
  72.2 0.2 fusion.17
  72.3 0.2 fusion.16
  72.5 0.6 fusion.22.allowed_ref
  73.1 0.1 copy.60
  73.2 0.1 copy.56
  73.4 0.1 copy.57
  73.5 10.1 %all-to-all-done.4 = bf16[1,8,8,2560]{3,2,0,1:T(8,128)(2,1)S(1)} async-done(((bf16[1,8,8,2560]{3,2,0,1:T(8,128)(2,1)}), bf16[1,8,8,2560]{3,2,0,1:T(8,128)(2,1)S(1)}, u32[]{:S(2)}, u32[]{:S(2)}) %all-to-all-start.4) | async-done | bytes 327712 | tf_op jit(solution)/shard_map/all_to_all | solution.py:130
  83.6 4.3 %all_to_all.41 = bf16[1,2,8,8,2560]{4,3,2,0,1:T(8,128)(2,1)S(1)} all-to-all(bf16[1,2,8,8,2560]{4,3,2,0,1:T(8,128)(2,1)S(1)} %broadcast_in_dim.23), channel_id=1, replica_groups=mesh['y'=8,'zl'=4,'zh'=2,'x'=4,'c'=2] {'c'}, dimensions={1} | all-to-all | bytes 1310720 | tf_op jit(solution)/shard_map/all_to_all | solution.py:132
  87.9 0.0 copy-start.4
  87.9 0.7 fusion
  88.7 0.1 copy.64
  88.8 0.1 copy.65
  88.9 0.1 copy.67
  89.1 0.1 copy.68
  89.2 0.0 copy-done.4
  89.2 0.7 fusion.12
  89.9 0.0 all-gather.5.cloned.1.call-done.kv_ref
  89.9 8.3 %shard_map.113 = bf16[128,128]{1,0:T(8,128)(2,1)} custom-call(s32[32]{0:T(128)} %fusion.22.allowed_ref, bf16[128,128]{1,0:T(8,128)(2,1)} %get-tuple-element.21.q_ref, bf16[128,128]{1,0:T(8,128)(2,1)} %get-tuple-element.20.k_ref, bf16[128,128]{1,0:T(8,128)(2,1)} %get-tuple-element.19.v_ref, bf16[32,2,128,128]{3,2,1,0:T(8,128)(2,1)} %all-gather.5.cloned.1.call-done.kv_ref), custom_call_target="tpu_custom_call" | custom-call | tf_op jit(solution)/shard_map/pallas_call | solution.py:97
  98.2 0.0 copy-done
  98.2 1.1 convolution_convert_fusion.1
  99.3 4.3 %all_to_all.42 = bf16[2,8,8,2560]{3,2,1,0:T(8,128)(2,1)S(1)} all-to-all(bf16[2,8,8,2560]{3,2,1,0:T(8,128)(2,1)S(1)} %bitcast.78), channel_id=1, replica_groups=mesh['y'=8,'zl'=4,'zh'=2,'x'=4,'c'=2] {'c'}, dimensions={0} | all-to-all | bytes 1310720 | tf_op jit(solution)/shard_map/all_to_all | solution.py:156
  103.5 0.9 reduce_sum.96
  104.5 3.4 %all-to-all-start.3 = ((bf16[8,8,2560]{2,1,0:T(8,128)(2,1)}), bf16[8,8,2560]{2,1,0:T(8,128)(2,1)S(1)}, u32[]{:S(2)}, u32[]{:S(2)}) async-start(bf16[8,8,2560]{2,1,0:T(8,128)(2,1)} %reduce_sum.96), calls=%async_computation.3 | async-start | bytes 655360 | tf_op jit(solution)/shard_map/all_to_all | solution.py:157
  107.9 0.6 fusion.15.v_ref
  108.5 14.7 %all-to-all-done.3 = bf16[8,8,2560]{2,1,0:T(8,128)(2,1)S(1)} async-done(((bf16[8,8,2560]{2,1,0:T(8,128)(2,1)}), bf16[8,8,2560]{2,1,0:T(8,128)(2,1)S(1)}, u32[]{:S(2)}, u32[]{:S(2)}) %all-to-all-start.3) | async-done | bytes 327712 | tf_op jit(solution)/shard_map/all_to_all | solution.py:157
  123.2 0.7 reduce_sum.97
  123.9 0.0 all-gather.7.cloned.1.call-done.kv_ref
  123.9 8.3 %shard_map.114 = bf16[128,128]{1,0:T(8,128)(2,1)} custom-call(s32[32]{0:T(128)} %fusion.22.allowed_ref, bf16[128,128]{1,0:T(8,128)(2,1)} %get-tuple-element.24.q_ref, bf16[128,128]{1,0:T(8,128)(2,1)} %get-tuple-element.25.k_ref, bf16[128,128]{1,0:T(8,128)(2,1)} %fusion.15.v_ref, bf16[32,2,128,128]{3,2,1,0:T(8,128)(2,1)} %all-gather.7.cloned.1.call-done.kv_ref), custom_call_target="tpu_custom_call" | custom-call | tf_op jit(solution)/shard_map/pallas_call | solution.py:97
  132.2 1.1 convolution_convert_fusion
  133.3 4.3 %all_to_all.43 = bf16[2,8,8,2560]{3,2,1,0:T(8,128)(2,1)S(1)} all-to-all(bf16[2,8,8,2560]{3,2,1,0:T(8,128)(2,1)S(1)} %bitcast.79), channel_id=1, replica_groups=mesh['y'=8,'zl'=4,'zh'=2,'x'=4,'c'=2] {'c'}, dimensions={0} | all-to-all | bytes 1310720 | tf_op jit(solution)/shard_map/all_to_all | solution.py:156
  137.6 0.2 reduce_sum.100
  137.7 18.5 %all_to_all.44 = bf16[8,8,2560]{2,1,0:T(8,128)(2,1)S(1)} all-to-all(bf16[8,8,2560]{2,1,0:T(8,128)(2,1)S(1)} %reduce_sum.100), channel_id=1, replica_groups=mesh['y'=8,'zl'=4,'zh'=2,'x'=4,'c'=2] {'zh','x'}, dimensions={0} | all-to-all | bytes 655360 | tf_op jit(solution)/shard_map/all_to_all | solution.py:157
  156.2 0.7 reduce_sum.101
  (18 shorter events, 0.3 us)
Async XLA Ops:
  7.2 91.0 %copy-start = (bf16[128,2560]{1,0:T(8,128)(2,1)S(1)}, bf16[128,2560]{1,0:T(8,128)(2,1)}, u32[]{:S(2)}) copy-start(bf16[128,2560]{1,0:T(8,128)(2,1)} %param.14) | copy-start | bytes 1966084
  7.2 82.7 %all-gather.5.cloned.1.call-start = ((), (), s32[]{:S(2)}) async-start(), calls=%async_computation.8 | async-start | bytes 2359296 | tf_op jit(solution)/shard_map/all_gather | solution.py:123
  25.5 21.4 %all-to-all-start = ((bf16[1,8,8,2560]{3,2,0,1:T(8,128)(2,1)}), bf16[1,8,8,2560]{3,2,0,1:T(8,128)(2,1)S(1)}, u32[]{:S(2)}, u32[]{:S(2)}) async-start(bf16[1,8,8,2560]{3,2,0,1:T(8,128)(2,1)} %broadcast_in_dim.17), calls=%async_computation | async-start | bytes 655360 | tf_op jit(solution)/shard_map/all_to_all | solution.py:130
  35.5 88.4 %all-gather.7.cloned.1.call-start = ((), (), s32[]{:S(2)}) async-start(), calls=%async_computation.9 | async-start | bytes 2359296 | tf_op jit(solution)/shard_map/all_gather | solution.py:148
  51.2 1.7 %copy-start.3 = (f32[128]{0:T(128)S(1)}, f32[128]{0:T(128)}, u32[]{:S(2)}) copy-start(f32[128]{0:T(128)} %param.16) | copy-start | bytes 1540
  51.2 16.4 %copy-start.2 = (s32[32,16]{0,1:T(8,128)S(1)}, s32[32,16]{0,1:T(8,128)}, u32[]{:S(2)}) copy-start(s32[32,16]{0,1:T(8,128)} %param.17) | copy-start | bytes 6148
  51.2 16.4 %copy-start.5 = (s32[32]{0:T(128)S(1)}, s32[32]{0:T(128)}, u32[]{:S(2)}) copy-start(s32[32]{0:T(128)} %param.18) | copy-start | bytes 388
  51.2 16.7 %copy-start.1 = (bf16[8,2560]{1,0:T(8,128)(2,1)S(1)}, bf16[8,2560]{1,0:T(8,128)(2,1)}, u32[]{:S(2)}) copy-start(bf16[8,2560]{1,0:T(8,128)(2,1)} %param.11) | copy-start | bytes 122884
  52.0 20.2 %copy-start.6 = (s32[32]{0:T(128)S(1)}, s32[32]{0:T(128)}, u32[]{:S(2)}) copy-start(s32[32]{0:T(128)} %param.19) | copy-start | bytes 388
  68.7 14.9 %all-to-all-start.4 = ((bf16[1,8,8,2560]{3,2,0,1:T(8,128)(2,1)}), bf16[1,8,8,2560]{3,2,0,1:T(8,128)(2,1)S(1)}, u32[]{:S(2)}, u32[]{:S(2)}) async-start(bf16[1,8,8,2560]{3,2,0,1:T(8,128)(2,1)} %broadcast_in_dim.21), calls=%async_computation.4 | async-start | bytes 655360 | tf_op jit(solution)/shard_map/all_to_all | solution.py:130
  87.9 1.3 copy-start.4
  104.5 18.8 %all-to-all-start.3 = ((bf16[8,8,2560]{2,1,0:T(8,128)(2,1)}), bf16[8,8,2560]{2,1,0:T(8,128)(2,1)S(1)}, u32[]{:S(2)}, u32[]{:S(2)}) async-start(bf16[8,8,2560]{2,1,0:T(8,128)(2,1)} %reduce_sum.96), calls=%async_computation.3 | async-start | bytes 655360 | tf_op jit(solution)/shard_map/all_to_all | solution.py:157
Sparse Core Ops, SparseCore 0:
  24.1 46.1 all-gather.4
  72.3 42.0 all-gather.6

commit v18 on v15

--- a/solution.py
+++ b/solution.py
@@ -45,7 +45,7 @@
     return (grid * factor).reshape(count, -1) * gain[None, :]
 
 
-def attn_kernel(allowed_ref, q_ref, k_ref, v_ref, kv_ref, o_ref, *, scale, n_blocks):
+def attn_kernel(allowed_ref, q_ref, k_ref, v_ref, kv_ref, w_ref, o_ref, *, scale, n_blocks):
     q = q_ref[...] * jnp.asarray(scale, q_ref.dtype)
     rows, width = q.shape
     lane = lax.broadcasted_iota(jnp.int32, (rows, width), 1)
@@ -88,18 +88,19 @@
         return lax.cond(allowed_ref[b] > 0, functools.partial(visit, b), lambda c: c, carry)
 
     m0, m1, l0, l1, acc = lax.fori_loop(0, n_blocks, body, carry)
-    o_ref[...] = (acc / jnp.where(first, l0, l1)).T.astype(o_ref.dtype)
+    attn = (acc / jnp.where(first, l0, l1)).T.astype(q_ref.dtype)
+    o_ref[...] = jnp.dot(attn, w_ref[...], preferred_element_type=jnp.float32).astype(o_ref.dtype)
 
 
-def block_attend(allowed, query, keys, values, kv, scale):
+def block_attend(allowed, query, keys, values, kv, w_out, scale):
     n_blocks = kv.shape[0]
     vmem = pltpu.MemorySpace.VMEM
     return pl.pallas_call(
         functools.partial(attn_kernel, scale=scale, n_blocks=n_blocks),
-        out_shape=jax.ShapeDtypeStruct(query.shape, jnp.bfloat16),
-        in_specs=[pl.BlockSpec(memory_space=pltpu.MemorySpace.SMEM)] + [pl.BlockSpec(memory_space=vmem)] * 4,
+        out_shape=jax.ShapeDtypeStruct((query.shape[0], w_out.shape[1]), jnp.bfloat16),
+        in_specs=[pl.BlockSpec(memory_space=pltpu.MemorySpace.SMEM)] + [pl.BlockSpec(memory_space=vmem)] * 5,
         out_specs=pl.BlockSpec(memory_space=vmem),
-    )(allowed, query, keys, values, kv)
+    )(allowed, query, keys, values, kv, w_out)
 
 
 def gather_pipe(piece, order):
@@ -156,8 +157,7 @@
 
     def attend(query, keys, values, kv, remote):
         allowed = remote[0].astype(jnp.int32)
-        attn = block_attend(allowed, query, keys, values, kv, scale)
-        part = jnp.dot(attn, w_out, preferred_element_type=jnp.float32).astype(jnp.bfloat16)
+        part = block_attend(allowed, query, keys, values, kv, w_out, scale)
         split = part.reshape(chip, n_seq // chip, tokens // n_seq, -1)
         pair_sum = jnp.sum(lax.all_to_all(split, SEQ[-1], 0, 0, tiled=False).astype(jnp.float32), axis=0)
         sent = lax.all_to_all(pair_sum.astype(jnp.bfloat16), SEQ[:-1], 0, 0, tiled=False)

time: 160 us -> 161 us (level)
  matrix products: 3.38 us -> 1.24 us
  blocking collectives: 78.5 us -> 80.4 us
    all_to_all x2, blocking collectives: 15.6 us -> 17.7 us  [attend(): lax.all_to_all(split, SEQ[-1], 0, 0, tiled=False).astype(jnp.float32)]
    dot_general x2 -> x0, matrix products: 2.14 us -> none  [attend(): jnp.dot(attn, w_out, preferred_element_type=jnp.float32)]
    unnamed x22 -> x20, local copies, waits for them, and re-layouts: 3.99 us -> 3.97 us
  transfers between devices with their start and end apart: 4 -> 4, of which waited for: 3 -> 3; matrix products, arithmetic and copies ran while one was open for 8% -> 7% of each run, Pallas kernels for 4% -> 4%
where the time goes in v18:
time: 161 us; the launch traced here: 158 us
  blocking collectives  80.4 us (50%)
  waiting for transfers between devices  23.5 us (15%)
  between operations  14.5 us (9%)
  Pallas kernels  13.3 us (8%)
  starting transfers between devices  12.7 us (8%)
  local copies, waits for them, and re-layouts  6.21 us (4%)
  other arithmetic  5.63 us (3%)
    all_to_all x1, blocking collectives, attend(): lax.all_to_all(pair_sum.astype(jnp.bfloat16), SEQ[:-1], 0, 0, tiled=False)  20.6 us
    all_to_all x2, blocking collectives, attend(): lax.all_to_all(split, SEQ[-1], 0, 0, tiled=False).astype(jnp.float32)  17.7 us
    all_gather x1, blocking collectives, on_device(): near = lax.all_gather(stale_kv[None], PIPE[1], axis=0, tiled=True)  17.4 us
    pallas_call x2, Pallas kernels, block_attend(): pl.pallas_call(functools.partial(attn_kernel, scale=scale, n_blocks=n_blo...  13.3 us
    all_gather x1, blocking collectives, gather_pipe(): piece = lax.all_gather(piece, name, axis=0, tiled=True)  13.1 us
    all_to_all x1, blocking collectives, exchange_rows(): lax.all_to_all(spread, SEQ[-1], 1, 1, tiled=False)  11.6 us
    all_to_all x1, waiting for transfers between devices, attend(): lax.all_to_all(pair_sum.astype(jnp.bfloat16), SEQ[:-1], 0, 0, tiled=False)  9.65 us
    all_to_all x1, waiting for transfers between devices, exchange_rows(): among = lax.all_to_all(spread, SEQ[:-1], 1, 1, tiled=False)  9.58 us
  transfers between devices with their start and end apart: 4, of which 3 were waited for; matrix products, arithmetic and copies ran while one was open for 7% of the time, Pallas kernels for 4%

profile of v18, /device:TPU:1, one launch (start us, length us, event | category | flops | bytes accessed | tf_op | source)
XLA Modules:
  0.0 157.5 jit_solution(6676415109688085584)
XLA Ops:
  7.2 0.0 all-gather.5.cloned.1.call-start
  7.2 17.4 %all-gather = bf16[8,128,128]{2,1,0:T(8,128)(2,1)} all-gather(bf16[2,128,128]{2,1,0:T(8,128)(2,1)} %param.12), channel_id=2, replica_groups=mesh['y'=8,'zl'=4,'zh'=2,'x'=4,'c'=2] {'zl'}, dimensions={0}, use_global_device_ids=true | all-gather | bytes 327680 | tf_op jit(solution)/shard_map/all_gather | solution.py:128
  24.6 0.8 pad_maximum_fusion
  25.4 0.0 all-gather.5.cloned.1.call-update
  25.5 0.9 broadcast_in_dim.9
  26.3 9.2 %all-to-all-start = ((bf16[2,8,8,2560]{3,2,0,1:T(8,128)(2,1)}), bf16[2,8,8,2560]{3,2,0,1:T(8,128)(2,1)S(1)}, u32[]{:S(2)}, u32[]{:S(2)}) async-start(bf16[2,8,8,2560]{3,2,0,1:T(8,128)(2,1)} %broadcast_in_dim.9), calls=%async_computation | async-start | bytes 1310720 | tf_op jit(solution)/shard_map/all_to_all | solution.py:137
  35.5 0.0 all-gather.7.cloned.1.call-start
  35.6 2.7 %copy.76 = bf16[3,2560,128]{1,2,0:T(8,128)(2,1)S(1)} copy(bf16[3,2560,128]{2,1,0:T(8,128)(2,1)} %param.13) | data formatting | bytes 3932160 | tf_op args[3]
  38.3 9.6 %all-to-all-done = bf16[2,8,8,2560]{3,2,0,1:T(8,128)(2,1)S(1)} async-done(((bf16[2,8,8,2560]{3,2,0,1:T(8,128)(2,1)}), bf16[2,8,8,2560]{3,2,0,1:T(8,128)(2,1)S(1)}, u32[]{:S(2)}, u32[]{:S(2)}) %all-to-all-start) | async-done | bytes 655392 | tf_op jit(solution)/shard_map/all_to_all | solution.py:137
  47.9 0.1 broadcast_in_dim.10
  48.0 11.6 %all_to_all.30 = bf16[2,2,8,8,2560]{4,3,2,0,1:T(8,128)(2,1)S(1)} all-to-all(bf16[2,2,8,8,2560]{4,3,2,0,1:T(8,128)(2,1)S(1)} %broadcast_in_dim.10), channel_id=1, replica_groups=mesh['y'=8,'zl'=4,'zh'=2,'x'=4,'c'=2] {'c'}, dimensions={1} | all-to-all | bytes 2621440 | tf_op jit(solution)/shard_map/all_to_all | solution.py:139
  59.6 0.1 copy.75
  59.7 0.9 fusion.19
  60.5 0.0 copy-start.2
  60.5 0.0 copy-start.1
  60.5 0.0 copy-start.4
  60.6 0.0 copy-start.5
  60.6 0.1 copy.77
  60.8 0.1 copy.95
  60.9 0.1 copy.82
  61.0 0.1 copy.96
  61.1 0.0 copy-start
  61.2 0.1 copy.85
  61.3 0.0 copy-done.2
  61.3 13.1 %all-gather.1 = bf16[8,128,128]{2,1,0:T(8,128)(2,1)} all-gather(bf16[2,128,128]{2,1,0:T(8,128)(2,1)S(1)} %pad_maximum_fusion.1), channel_id=3, replica_groups=mesh['y'=8,'zl'=4,'zh'=2,'x'=4,'c'=2] {'zl'}, dimensions={0}, use_global_device_ids=true | all-gather | bytes 327680 | tf_op jit(solution)/shard_map/all_gather | solution.py:108
  74.4 0.0 copy-start.3
  74.4 0.0 all-gather.7.cloned.1.call-update
  74.4 0.0 copy-done.1
  74.5 0.1 copy.73
  74.5 0.0 copy-done.4
  74.5 0.1 iota_compare_fusion.1
  74.6 0.2 convert_reduce_fusion
  74.8 0.0 copy-done.5
  74.8 0.2 fusion.12
  75.0 0.2 fusion.11
  75.2 0.6 fusion.15.allowed_ref
  75.8 0.1 copy.83
  75.9 0.1 copy.86
  76.1 0.1 copy.98
  76.2 0.1 copy.91
  76.3 0.1 copy.92
  76.4 0.1 copy.94
  76.6 0.1 copy.79
  76.7 0.1 copy.80
  76.8 0.1 copy.97
  76.9 0.0 copy-done
  76.9 0.1 copy.88
  77.1 0.1 copy.89
  77.2 0.6 fusion.2
  77.8 0.0 copy-done.3
  77.8 0.6 fusion.4
  78.5 6.7 %shard_map.113 = bf16[128,2560]{1,0:T(8,128)(2,1)} custom-call(s32[32]{0:T(128)} %fusion.15.allowed_ref, bf16[128,128]{1,0:T(8,128)(2,1)} %get-tuple-element.19.q_ref, bf16[128,128]{1,0:T(8,128)(2,1)} %get-tuple-element.17.k_ref, bf16[128,128]{1,0:T(8,128)(2,1)} %bitcast.79, bf16[32,2,128,128]{3,2,1,0:T(8,128)(2,1)} %all-gather.5.cloned.1.call-done.kv_ref, ...), custom_call_target="tpu_custom_call" | custom-call | tf_op jit(solution)/shard_map/pallas_call | solution.py:98
  85.2 8.0 %all_to_all.31 = bf16[2,8,8,2560]{3,2,1,0:T(8,128)(2,1)S(1)} all-to-all(bf16[2,8,8,2560]{3,2,1,0:T(8,128)(2,1)} %bitcast.69), channel_id=1, replica_groups=mesh['y'=8,'zl'=4,'zh'=2,'x'=4,'c'=2] {'c'}, dimensions={0} | all-to-all | bytes 1310720 | tf_op jit(solution)/shard_map/all_to_all | solution.py:162
  93.2 0.9 reduce_sum.96
  94.1 3.4 %all-to-all-start.3 = ((bf16[8,8,2560]{2,1,0:T(8,128)(2,1)}), bf16[8,8,2560]{2,1,0:T(8,128)(2,1)S(1)}, u32[]{:S(2)}, u32[]{:S(2)}) async-start(bf16[8,8,2560]{2,1,0:T(8,128)(2,1)} %reduce_sum.96), calls=%async_computation.3 | async-start | bytes 655360 | tf_op jit(solution)/shard_map/all_to_all | solution.py:163
  97.6 0.7 copy.99
  98.3 9.6 %all-to-all-done.3 = bf16[8,8,2560]{2,1,0:T(8,128)(2,1)S(1)} async-done(((bf16[8,8,2560]{2,1,0:T(8,128)(2,1)}), bf16[8,8,2560]{2,1,0:T(8,128)(2,1)S(1)}, u32[]{:S(2)}, u32[]{:S(2)}) %all-to-all-start.3) | async-done | bytes 327712 | tf_op jit(solution)/shard_map/all_to_all | solution.py:163
  107.9 0.7 reduce_sum.97
  108.6 4.3 %all-gather.7.cloned.1.call-done.kv_ref = bf16[32,2,128,128]{3,2,1,0:T(8,128)(2,1)} async-done(((bf16[4,2,128,128]{3,2,1,0:T(8,128)(2,1)}), bf16[32,2,128,128]{3,2,1,0:T(8,128)(2,1)}) %all-gather.7.cloned.1.call-update) | async-done | bytes 2097168 | tf_op jit(solution)/shard_map/all_gather | solution.py:108
  112.8 6.7 %shard_map.114 = bf16[128,2560]{1,0:T(8,128)(2,1)} custom-call(s32[32]{0:T(128)} %fusion.15.allowed_ref, bf16[128,128]{1,0:T(8,128)(2,1)} %get-tuple-element.18.q_ref, bf16[128,128]{1,0:T(8,128)(2,1)} %get-tuple-element.16.k_ref, bf16[128,128]{1,0:T(8,128)(2,1)} %bitcast.87, bf16[32,2,128,128]{3,2,1,0:T(8,128)(2,1)} %all-gather.7.cloned.1.call-done.kv_ref, ...), custom_call_target="tpu_custom_call" | custom-call | tf_op jit(solution)/shard_map/pallas_call | solution.py:98
  119.5 9.7 %all_to_all.32 = bf16[2,8,8,2560]{3,2,1,0:T(8,128)(2,1)S(1)} all-to-all(bf16[2,8,8,2560]{3,2,1,0:T(8,128)(2,1)} %bitcast.68), channel_id=1, replica_groups=mesh['y'=8,'zl'=4,'zh'=2,'x'=4,'c'=2] {'c'}, dimensions={0} | all-to-all | bytes 1310720 | tf_op jit(solution)/shard_map/all_to_all | solution.py:162
  129.2 0.2 reduce_sum.100
  129.4 20.6 %all_to_all.33 = bf16[8,8,2560]{2,1,0:T(8,128)(2,1)S(1)} all-to-all(bf16[8,8,2560]{2,1,0:T(8,128)(2,1)S(1)} %reduce_sum.100), channel_id=1, replica_groups=mesh['y'=8,'zl'=4,'zh'=2,'x'=4,'c'=2] {'zh','x'}, dimensions={0} | all-to-all | bytes 655360 | tf_op jit(solution)/shard_map/all_to_all | solution.py:163
  150.0 0.7 reduce_sum.101
  (25 shorter events, 0.3 us)
Async XLA Ops:
  7.2 71.3 %all-gather.5.cloned.1.call-start = ((), (), s32[]{:S(2)}) async-start(), calls=%async_computation.6 | async-start | bytes 2359296 | tf_op jit(solution)/shard_map/all_gather | solution.py:130
  26.3 21.5 %all-to-all-start = ((bf16[2,8,8,2560]{3,2,0,1:T(8,128)(2,1)}), bf16[2,8,8,2560]{3,2,0,1:T(8,128)(2,1)S(1)}, u32[]{:S(2)}, u32[]{:S(2)}) async-start(bf16[2,8,8,2560]{3,2,0,1:T(8,128)(2,1)} %broadcast_in_dim.9), calls=%async_computation | async-start | bytes 1310720 | tf_op jit(solution)/shard_map/all_to_all | solution.py:137
  35.5 77.3 %all-gather.7.cloned.1.call-start = ((), (), s32[]{:S(2)}) async-start(), calls=%async_computation.7 | async-start | bytes 2359296 | tf_op jit(solution)/shard_map/all_gather | solution.py:108
  60.5 0.7 copy-start.2
  60.5 13.9 %copy-start.1 = (s32[32,16]{0,1:T(8,128)S(1)}, s32[32,16]{0,1:T(8,128)}, u32[]{:S(2)}) copy-start(s32[32,16]{0,1:T(8,128)} %param.17) | copy-start | bytes 6148
  60.5 14.0 %copy-start.4 = (s32[32]{0:T(128)S(1)}, s32[32]{0:T(128)}, u32[]{:S(2)}) copy-start(s32[32]{0:T(128)} %param.18) | copy-start | bytes 388
  60.6 14.3 %copy-start.5 = (s32[32]{0:T(128)S(1)}, s32[32]{0:T(128)}, u32[]{:S(2)}) copy-start(s32[32]{0:T(128)} %param.19) | copy-start | bytes 388
  61.1 15.8 %copy-start = (bf16[128,1,128]{2,0,1:T(8,128)(2,1)}, bf16[128,1,128]{2,0,1:T(8,128)(2,1)S(1)}, u32[]{:S(2)}) copy-start(bf16[128,1,128]{2,0,1:T(8,128)(2,1)S(1)} %copy.96) | copy-start | bytes 98308
  74.4 3.4 %copy-start.3 = (f32[128]{0:T(128)S(1)}, f32[128]{0:T(128)}, u32[]{:S(2)}) copy-start(f32[128]{0:T(128)} %param.15) | copy-start | bytes 1540
  94.1 13.8 %all-to-all-start.3 = ((bf16[8,8,2560]{2,1,0:T(8,128)(2,1)}), bf16[8,8,2560]{2,1,0:T(8,128)(2,1)S(1)}, u32[]{:S(2)}, u32[]{:S(2)}) async-start(bf16[8,8,2560]{2,1,0:T(8,128)(2,1)} %reduce_sum.96), calls=%async_computation.3 | async-start | bytes 655360 | tf_op jit(solution)/shard_map/all_to_all | solution.py:163
Sparse Core Ops, SparseCore 0:
  25.6 42.8 all-gather.4
  74.6 38.2 all-gather.6

commit v19 on v18

--- a/solution.py
+++ b/solution.py
@@ -103,10 +103,14 @@
     )(allowed, query, keys, values, kv, w_out)
 
 
+def gather_near(piece, name, size):
+    spread = jnp.broadcast_to(piece, (size,) + piece.shape[1:])
+    return lax.all_to_all(spread, name, 0, 0, tiled=True)
+
+
 def gather_pipe(piece, order):
-    for name in order:
-        piece = lax.all_gather(piece, name, axis=0, tiled=True)
-    return piece
+    piece = gather_near(piece, order[0], PIPE_PARTS[1][1])
+    return lax.all_gather(piece, order[1], axis=0, tiled=True)
 
 
 def on_device(
@@ -125,7 +129,7 @@
     mine = lax.dynamic_slice_in_dim(linked, me * BPM, BPM, 0)
     remote = mine & (batch_of != me)[None, :]
 
-    near = lax.all_gather(stale_kv[None], PIPE[1], axis=0, tiled=True)
+    near = gather_near(stale_kv[None], PIPE[1], PIPE_PARTS[1][1])
     pair, near = lax.optimization_barrier((jnp.stack([x_first, x_second]), near))
     stale = lax.all_gather(near, PIPE[0], axis=0, tiled=True)
 

time: 161 us -> 160 us (level)
  the two profiles are of different devices: /device:TPU:1 before, /device:TPU:120 now
where the time goes in v19:
time: 160 us; the launch traced here: 159 us
  blocking collectives  51.1 us (32%)
  waiting for transfers between devices  39.1 us (24%)
  starting transfers between devices  22.2 us (14%)
  Pallas kernels  16.8 us (10%)
  between operations  14.5 us (9%)
  local copies, waits for them, and re-layouts  8.5 us (5%)
  other arithmetic  5.63 us (4%)
    all_to_all x1, blocking collectives, attend(): lax.all_to_all(pair_sum.astype(jnp.bfloat16), SEQ[:-1], 0, 0, tiled=False)  24.5 us
    pallas_call x2, Pallas kernels, block_attend(): pl.pallas_call(functools.partial(attn_kernel, scale=scale, n_blocks=n_blo...  16.8 us
    all_to_all x1, waiting for transfers between devices, exchange_rows(): among = lax.all_to_all(spread, SEQ[:-1], 1, 1, tiled=False)  16.4 us
    all_to_all x1, waiting for transfers between devices, attend(): lax.all_to_all(pair_sum.astype(jnp.bfloat16), SEQ[:-1], 0, 0, tiled=False)  14.7 us
    all_to_all x1, blocking collectives, gather_near(): return lax.all_to_all(spread, name, 0, 0, tiled=True)  11.1 us
    all_to_all x2, blocking collectives, attend(): lax.all_to_all(split, SEQ[-1], 0, 0, tiled=False).astype(jnp.float32)  10.7 us
    all_to_all x1, starting transfers between devices, exchange_rows(): among = lax.all_to_all(spread, SEQ[:-1], 1, 1, tiled=False)  10 us
    all_to_all x1, starting transfers between devices, gather_near(): return lax.all_to_all(spread, name, 0, 0, tiled=True)  6.91 us
  transfers between devices with their start and end apart: 5, of which 4 were waited for; matrix products, arithmetic and copies ran while one was open for 8% of the time, Pallas kernels for 5%

profile of v19, /device:TPU:120, one launch (start us, length us, event | category | flops | bytes accessed | tf_op | source)
XLA Modules:
  0.0 159.1 jit_solution(5479442144871516755)
XLA Ops:
  7.2 1.6 broadcast_in_dim.8
  8.7 6.9 %all-to-all-start = ((bf16[4,2,128,128]{3,2,1,0:T(8,128)(2,1)}), bf16[4,2,128,128]{3,2,1,0:T(8,128)(2,1)S(1)}, u32[]{:S(2)}, u32[]{:S(2)}) async-start(bf16[4,2,128,128]{3,2,1,0:T(8,128)(2,1)} %broadcast_in_dim.8), calls=%async_computation | async-start | bytes 524288 | tf_op jit(solution)/shard_map/all_to_all | solution.py:108
  15.6 0.0 all-gather.3.cloned.1.call-start
  15.6 0.8 pad_maximum_fusion
  16.5 6.2 %all-to-all-done = bf16[4,2,128,128]{3,2,1,0:T(8,128)(2,1)S(1)} async-done(((bf16[4,2,128,128]{3,2,1,0:T(8,128)(2,1)}), bf16[4,2,128,128]{3,2,1,0:T(8,128)(2,1)S(1)}, u32[]{:S(2)}, u32[]{:S(2)}) %all-to-all-start) | async-done | bytes 262176 | tf_op jit(solution)/shard_map/all_to_all | solution.py:108
  22.7 0.7 copy-done
  23.4 0.0 all-gather.3.cloned.1.call-update
  23.4 0.9 broadcast_in_dim.9
  24.3 10.0 %all-to-all-start.1 = ((bf16[2,8,8,2560]{3,2,0,1:T(8,128)(2,1)}), bf16[2,8,8,2560]{3,2,0,1:T(8,128)(2,1)S(1)}, u32[]{:S(2)}, u32[]{:S(2)}) async-start(bf16[2,8,8,2560]{3,2,0,1:T(8,128)(2,1)} %broadcast_in_dim.9), calls=%async_computation.1 | async-start | bytes 1310720 | tf_op jit(solution)/shard_map/all_to_all | solution.py:141
  34.3 0.0 all-gather.5.cloned.1.call-start
  34.4 2.7 %copy.76 = bf16[3,2560,128]{1,2,0:T(8,128)(2,1)S(1)} copy(bf16[3,2560,128]{2,1,0:T(8,128)(2,1)} %param.13) | data formatting | bytes 3932160 | tf_op args[3]
  37.1 16.4 %all-to-all-done.1 = bf16[2,8,8,2560]{3,2,0,1:T(8,128)(2,1)S(1)} async-done(((bf16[2,8,8,2560]{3,2,0,1:T(8,128)(2,1)}), bf16[2,8,8,2560]{3,2,0,1:T(8,128)(2,1)S(1)}, u32[]{:S(2)}, u32[]{:S(2)}) %all-to-all-start.1) | async-done | bytes 655392 | tf_op jit(solution)/shard_map/all_to_all | solution.py:141
  53.6 0.1 broadcast_in_dim.10
  53.7 4.8 %all_to_all.40 = bf16[2,2,8,8,2560]{4,3,2,0,1:T(8,128)(2,1)S(1)} all-to-all(bf16[2,2,8,8,2560]{4,3,2,0,1:T(8,128)(2,1)S(1)} %broadcast_in_dim.10), channel_id=1, replica_groups=mesh['y'=8,'zl'=4,'zh'=2,'x'=4,'c'=2] {'c'}, dimensions={1} | all-to-all | bytes 2621440 | tf_op jit(solution)/shard_map/all_to_all | solution.py:143
  58.4 0.1 copy.75
  58.6 0.8 fusion.19
  59.4 0.0 copy-start.3
  59.4 0.0 copy-start.2
  59.4 0.0 copy-start.5
  59.4 0.0 copy-start.6
  59.5 0.1 copy.77
  59.7 0.1 copy.95
  59.8 0.1 copy.82
  59.9 0.1 copy.96
  60.0 0.0 copy-start.1
  60.1 0.1 copy.85
  60.1 0.0 copy-done.3
  60.2 11.1 %all_to_all.41 = bf16[4,2,128,128]{3,2,1,0:T(8,128)(2,1)} all-to-all(bf16[4,2,128,128]{3,2,1,0:T(8,128)(2,1)S(1)} %broadcast_in_dim.11), channel_id=1, replica_groups=mesh['y'=8,'zl'=4,'zh'=2,'x'=4,'c'=2] {'zl'}, dimensions={0} | all-to-all | bytes 524288 | tf_op jit(solution)/shard_map/all_to_all | solution.py:108
  71.4 0.0 all-gather.5.cloned.1.call-update
  71.4 0.0 copy-done.2
  71.4 0.1 copy.73
  71.5 0.0 copy-done.5
  71.5 0.1 iota_compare_fusion.1
  71.6 0.2 convert_reduce_fusion
  71.8 0.0 copy-done.6
  71.8 0.2 fusion.12
  72.0 0.2 fusion.11
  72.2 0.6 fusion.15.allowed_ref
  72.8 0.1 copy.83
  72.9 0.1 copy.86
  73.0 0.1 copy.98
  73.2 0.1 copy.91
  73.3 0.1 copy.92
  73.4 0.1 copy.94
  73.5 0.1 copy.79
  73.7 0.1 copy.80
  73.8 0.1 copy.97
  73.9 0.1 copy.88
  74.1 0.1 copy.89
  74.2 0.6 fusion.2
  74.8 0.6 fusion.4
  75.4 8.4 %shard_map.113 = bf16[128,2560]{1,0:T(8,128)(2,1)} custom-call(s32[32]{0:T(128)} %fusion.15.allowed_ref, bf16[128,128]{1,0:T(8,128)(2,1)} %get-tuple-element.19.q_ref, bf16[128,128]{1,0:T(8,128)(2,1)} %get-tuple-element.17.k_ref, bf16[128,128]{1,0:T(8,128)(2,1)} %bitcast.75, bf16[32,2,128,128]{3,2,1,0:T(8,128)(2,1)} %all-gather.3.cloned.1.call-done.kv_ref, ...), custom_call_target="tpu_custom_call" | custom-call | tf_op jit(solution)/shard_map/pallas_call | solution.py:98
  83.8 5.3 %all_to_all.42 = bf16[2,8,8,2560]{3,2,1,0:T(8,128)(2,1)S(1)} all-to-all(bf16[2,8,8,2560]{3,2,1,0:T(8,128)(2,1)} %bitcast.67), channel_id=1, replica_groups=mesh['y'=8,'zl'=4,'zh'=2,'x'=4,'c'=2] {'c'}, dimensions={0} | all-to-all | bytes 1310720 | tf_op jit(solution)/shard_map/all_to_all | solution.py:166
  89.2 0.9 reduce_sum.96
  90.1 5.3 %all-to-all-start.4 = ((bf16[8,8,2560]{2,1,0:T(8,128)(2,1)}), bf16[8,8,2560]{2,1,0:T(8,128)(2,1)S(1)}, u32[]{:S(2)}, u32[]{:S(2)}) async-start(bf16[8,8,2560]{2,1,0:T(8,128)(2,1)} %reduce_sum.96), calls=%async_computation.4 | async-start | bytes 655360 | tf_op jit(solution)/shard_map/all_to_all | solution.py:167
  95.4 0.7 copy.99
  96.1 14.7 %all-to-all-done.4 = bf16[8,8,2560]{2,1,0:T(8,128)(2,1)S(1)} async-done(((bf16[8,8,2560]{2,1,0:T(8,128)(2,1)}), bf16[8,8,2560]{2,1,0:T(8,128)(2,1)S(1)}, u32[]{:S(2)}, u32[]{:S(2)}) %all-to-all-start.4) | async-done | bytes 327712 | tf_op jit(solution)/shard_map/all_to_all | solution.py:167
  110.8 0.7 reduce_sum.97
  111.5 1.7 %all-gather.5.cloned.1.call-done.kv_ref = bf16[32,2,128,128]{3,2,1,0:T(8,128)(2,1)} async-done(((bf16[4,2,128,128]{3,2,1,0:T(8,128)(2,1)}), bf16[32,2,128,128]{3,2,1,0:T(8,128)(2,1)}) %all-gather.5.cloned.1.call-update) | async-done | bytes 2097168 | tf_op jit(solution)/shard_map/all_gather | solution.py:113
  113.2 8.4 %shard_map.114 = bf16[128,2560]{1,0:T(8,128)(2,1)} custom-call(s32[32]{0:T(128)} %fusion.15.allowed_ref, bf16[128,128]{1,0:T(8,128)(2,1)} %get-tuple-element.18.q_ref, bf16[128,128]{1,0:T(8,128)(2,1)} %get-tuple-element.16.k_ref, bf16[128,128]{1,0:T(8,128)(2,1)} %bitcast.83, bf16[32,2,128,128]{3,2,1,0:T(8,128)(2,1)} %all-gather.5.cloned.1.call-done.kv_ref, ...), custom_call_target="tpu_custom_call" | custom-call | tf_op jit(solution)/shard_map/pallas_call | solution.py:98
  121.6 5.3 %all_to_all.43 = bf16[2,8,8,2560]{3,2,1,0:T(8,128)(2,1)S(1)} all-to-all(bf16[2,8,8,2560]{3,2,1,0:T(8,128)(2,1)} %bitcast.66), channel_id=1, replica_groups=mesh['y'=8,'zl'=4,'zh'=2,'x'=4,'c'=2] {'c'}, dimensions={0} | all-to-all | bytes 1310720 | tf_op jit(solution)/shard_map/all_to_all | solution.py:166
  126.9 0.2 reduce_sum.100
  127.1 24.5 %all_to_all.44 = bf16[8,8,2560]{2,1,0:T(8,128)(2,1)S(1)} all-to-all(bf16[8,8,2560]{2,1,0:T(8,128)(2,1)S(1)} %reduce_sum.100), channel_id=1, replica_groups=mesh['y'=8,'zl'=4,'zh'=2,'x'=4,'c'=2] {'zh','x'}, dimensions={0} | all-to-all | bytes 655360 | tf_op jit(solution)/shard_map/all_to_all | solution.py:167
  151.6 0.7 reduce_sum.101
  (30 shorter events, 0.4 us)
Async XLA Ops:
  8.7 14.0 %all-to-all-start = ((bf16[4,2,128,128]{3,2,1,0:T(8,128)(2,1)}), bf16[4,2,128,128]{3,2,1,0:T(8,128)(2,1)S(1)}, u32[]{:S(2)}, u32[]{:S(2)}) async-start(bf16[4,2,128,128]{3,2,1,0:T(8,128)(2,1)} %broadcast_in_dim.8), calls=%async_computation | async-start | bytes 524288 | tf_op jit(solution)/shard_map/all_to_all | solution.py:108
  15.6 59.8 %all-gather.3.cloned.1.call-start = ((), (), s32[]{:S(2)}) async-start(), calls=%async_computation.8 | async-start | bytes 2359296 | tf_op jit(solution)/shard_map/all_gather | solution.py:134
  22.7 0.7 copy-start
  24.3 29.2 %all-to-all-start.1 = ((bf16[2,8,8,2560]{3,2,0,1:T(8,128)(2,1)}), bf16[2,8,8,2560]{3,2,0,1:T(8,128)(2,1)S(1)}, u32[]{:S(2)}, u32[]{:S(2)}) async-start(bf16[2,8,8,2560]{3,2,0,1:T(8,128)(2,1)} %broadcast_in_dim.9), calls=%async_computation.1 | async-start | bytes 1310720 | tf_op jit(solution)/shard_map/all_to_all | solution.py:141
  34.3 78.8 %all-gather.5.cloned.1.call-start = ((), (), s32[]{:S(2)}) async-start(), calls=%async_computation.9 | async-start | bytes 2359296 | tf_op jit(solution)/shard_map/all_gather | solution.py:113
  59.4 0.7 copy-start.3
  59.4 12.0 %copy-start.2 = (s32[32,16]{0,1:T(8,128)S(1)}, s32[32,16]{0,1:T(8,128)}, u32[]{:S(2)}) copy-start(s32[32,16]{0,1:T(8,128)} %param.17) | copy-start | bytes 6148
  59.4 12.1 %copy-start.5 = (s32[32]{0:T(128)S(1)}, s32[32]{0:T(128)}, u32[]{:S(2)}) copy-start(s32[32]{0:T(128)} %param.18) | copy-start | bytes 388
  59.4 12.4 %copy-start.6 = (s32[32]{0:T(128)S(1)}, s32[32]{0:T(128)}, u32[]{:S(2)}) copy-start(s32[32]{0:T(128)} %param.19) | copy-start | bytes 388
  60.0 13.7 %copy-start.1 = (bf16[128,1,128]{2,0,1:T(8,128)(2,1)}, bf16[128,1,128]{2,0,1:T(8,128)(2,1)S(1)}, u32[]{:S(2)}) copy-start(bf16[128,1,128]{2,0,1:T(8,128)(2,1)S(1)} %copy.96) | copy-start | bytes 98308
  71.4 3.4 %copy-start.4 = (f32[128]{0:T(128)S(1)}, f32[128]{0:T(128)}, u32[]{:S(2)}) copy-start(f32[128]{0:T(128)} %param.15) | copy-start | bytes 1540
  90.1 20.7 %all-to-all-start.4 = ((bf16[8,8,2560]{2,1,0:T(8,128)(2,1)}), bf16[8,8,2560]{2,1,0:T(8,128)(2,1)S(1)}, u32[]{:S(2)}, u32[]{:S(2)}) async-start(bf16[8,8,2560]{2,1,0:T(8,128)(2,1)} %reduce_sum.96), calls=%async_computation.4 | async-start | bytes 655360 | tf_op jit(solution)/shard_map/all_to_all | solution.py:167
Sparse Core Ops, SparseCore 0:
  23.5 45.3 all-gather.2
  71.5 41.5 all-gather.4
